TPU v7x, 128 devices: a whole 4x4x4 slice. The times are simulated.
128 devices in a mesh: wall: 4 (over z), span: 32 (over y, x, core).
Axes of the slice: x: 4, y: 4, z: 4, core: 2. Of those that a mesh axis runs over, the one named last changes fastest.
Arguments:
- solution: float32 [5, 125, 32768], P(None, None, ('wall', 'span')), may hold values from -6 to 6
- level_map: int32 [32768], P(('wall', 'span')), may hold values from 0 to 3, as said below
- send_list: int32 [128, 1024], P(('wall', 'span')), may hold values from 0 to 1535, as said below
- face_partner: int32 [6, 32768], P(None, ('wall', 'span')), may hold values from 0 to 2559, as said below
- volume_block: float32 [125, 125], replicated
- lift_block: float32 [125, 150], replicated, may hold values from -0.5 to 0.5
- flux_mixing: float32 [5, 5], replicated
- metric_scale: float32 [32768], P(('wall', 'span')), may hold values from 0.5 to 2
Outputs:
- advanced_solution: float32 [5, 125, 32768], P(None, None, ('wall', 'span'))
Inputs may be any that keep to these rules, and one draw needn't show every extreme that they name: `level_map`: each partition holds elements of every level. `send_list`: slot k (of 8) from any sender to any receiver names a face of a sender's element of level max(3 - j, 0), where j is the largest whole number with 2**j * (8 - k) <= 8. `face_partner`: in each partition's 256 elements, every column of the received traces is named by exactly one face; the other faces name columns of the partition's own trace table.
All inputs are finite; a program needn't handle non-finite values.
Results may differ from a plain program's by a relative error of at most 0.0001.
Values sent between devices are 32-bit elements; how exact they have to be, the bound alone decides.
No kernel may reach another device: no remote copies, remote signals or barrier semaphores. Data moves between devices by JAX's collectives and lax.ppermute only.
A program may use at most 64 MiB of HBM per device.

v0:
```python
import jax
import jax.numpy as jnp
from jax import lax
from jax.sharding import PartitionSpec as P

VARIABLES = 5
DEGREE = 4
FACE_NODES = 25
TRACE_ROWS = 125
LEVELS = 4
COARSE_STEPS = 3


COURANT = 0.6


def face_traces(fields):
    local_count = fields.shape[2]
    node_cube = fields.reshape(VARIABLES, DEGREE + 1, DEGREE + 1, DEGREE + 1, local_count)
    face_list = [
        node_cube[:, 0],
        node_cube[:, -1],
        node_cube[:, :, 0],
        node_cube[:, :, -1],
        node_cube[:, :, :, 0],
        node_cube[:, :, :, -1],
    ]
    return jnp.stack(
        [face.reshape(VARIABLES, FACE_NODES, local_count) for face in face_list], axis=1
    )


def tendency(fields, nearby, volume_block, lift_block, flux_mixing, metric_scale):
    own_trace = face_traces(fields).reshape(VARIABLES, 6 * FACE_NODES, fields.shape[2])
    face_jumps = nearby - own_trace
    combined = jnp.einsum("pj,vje->vpe", lift_block, face_jumps, precision=lax.Precision.HIGHEST)
    combined = combined - jnp.einsum(
        "pq,vqe->vpe", volume_block, fields, precision=lax.Precision.HIGHEST
    )
    return metric_scale * jnp.einsum(
        "vw,wpe->vpe", flux_mixing, combined, precision=lax.Precision.HIGHEST
    )


def arrange(columns, local_count):
    shaped = columns.reshape(VARIABLES, FACE_NODES, 6, local_count).transpose(0, 2, 1, 3)
    return shaped.reshape(VARIABLES, 6 * FACE_NODES, local_count)


def make_table(fields):
    return face_traces(fields).transpose(0, 2, 1, 3).reshape(TRACE_ROWS, 6 * fields.shape[2])


def send_slots(outgoing):
    return lax.all_to_all(outgoing, ("wall", "span"), split_axis=1, concat_axis=1, tiled=True)


def lowest_level(substep):
    for candidate in range(LEVELS):
        if substep % 2 ** (LEVELS - 1 - candidate) == 0:
            return candidate
    return LEVELS - 1


def body(
    solution,
    level_map,
    send_list,
    face_partner,
    volume_block,
    lift_block,
    flux_mixing,
    metric_scale,
):
    local_count = solution.shape[2]
    peers = lax.axis_size(("wall", "span"))
    slot_count = send_list.shape[1] // peers
    send_row = send_list[0]
    pointers = face_partner.reshape(-1)
    divisors = jnp.power(2, level_map).astype(jnp.float32)
    substeps = 2 ** (LEVELS - 1)
    start_cache = jnp.zeros((TRACE_ROWS, peers, slot_count), jnp.float32)

    def coarse_step(coarse_index, carry):
        fields, cache = carry
        element_rates = metric_scale * (1.0 + jnp.sqrt(jnp.mean(fields * fields, axis=(0, 1))))
        fastest = lax.pmax(jnp.max(element_rates), ("wall", "span"))
        step_sizes = COURANT / fastest / divisors
        for substep in range(substeps):
            lowest = lowest_level(substep)
            trace_table = make_table(fields)
            outgoing = jnp.take(trace_table, send_row, axis=1).reshape(
                TRACE_ROWS, peers, slot_count
            )
            received = send_slots(outgoing).reshape(TRACE_ROWS, peers * slot_count)
            lookup = jnp.concatenate([trace_table, received], axis=1)
            nearby = arrange(jnp.take(lookup, pointers, axis=1), local_count)
            change = tendency(fields, nearby, volume_block, lift_block, flux_mixing, metric_scale)
            fields = fields + jnp.where(level_map >= lowest, step_sizes * change, 0.0)
        return (fields, cache)

    final_fields, final_cache = lax.fori_loop(0, COARSE_STEPS, coarse_step, (solution, start_cache))
    return final_fields


def solution(mesh):
    return jax.shard_map(
        body,
        mesh=mesh,
        in_specs=(
            P(None, None, ("wall", "span")),
            P(("wall", "span")),
            P(("wall", "span"), None),
            P(None, ("wall", "span")),
            P(),
            P(),
            P(),
            P(("wall", "span")),
        ),
        out_specs=P(None, None, ("wall", "span")),
        check_vma=False,
    )
```

profile of v0, /device:TPU:1, one launch (start us, length us, event | category | flops | bytes accessed | tf_op | source)
XLA Modules:
  0.0 1181.2 jit_solution(2986283469730470943)
XLA Ops:
  4.4 1174.3 %while.10 = (s32[]{:T(128)}, f32[5,125,256]{2,0,1:T(8,128)}, s32[256]{0:T(256)}, f32[256]{0:T(256)S(1)}, f32[256]{0:T(256)}, /*index=5*/s32[1024]{0:T(1024)}, s3...) while((s32[]{:T(128)}, f32[5,125,256]{2,0,1:T(8,128)}, ...), condition=%wide.region_4.0_spmd, body=%wide.region_0.6_spmd.sunk | while | flops 4314204160 | bytes 334789824 | solution.py:102
  28.7 67.2 %pmax.8 = f32[]{:T(128)} all-reduce(f32[]{:T(128)} %multiply_reduce_fusion.5), channel_id=1, replica_groups=mesh['wall'=4,'span'=32] {'wall','span'}, use_global_device_ids=true, to_apply=%region_3.3 | all-reduce | flops 1 | bytes 8 | tf_op jit(solution)/shard_map/while/body/eval_jaxpr/pmax | solution.py:87
  128.9 11.9 %all-to-all-done.1 = f32[125,128,8]{0,2,1:T(8,128)S(1)} async-done(((f32[125,128,8]{0,2,1:T(8,128)}), f32[125,128,8]{0,2,1:T(8,128)S(1)}, u32[]{:S(2)}, u32[]{:S(2)}) %all-to-all-start.1) | async-done | bytes 512032 | tf_op jit(solution)/shard_map/while/body/eval_jaxpr/all_to_all | solution.py:55
  174.5 11.6 all-to-all-done.2
  211.2 11.9 %all-to-all-done.3 = f32[125,128,8]{0,2,1:T(8,128)S(1)} async-done(((f32[125,128,8]{0,2,1:T(8,128)}), f32[125,128,8]{0,2,1:T(8,128)S(1)}, u32[]{:S(2)}, u32[]{:S(2)}) %all-to-all-start.3) | async-done | bytes 512032 | tf_op jit(solution)/shard_map/while/body/eval_jaxpr/all_to_all | solution.py:55
  249.9 11.9 %all-to-all-done.4 = f32[125,128,8]{0,2,1:T(8,128)S(1)} async-done(((f32[125,128,8]{0,2,1:T(8,128)}), f32[125,128,8]{0,2,1:T(8,128)S(1)}, u32[]{:S(2)}, u32[]{:S(2)}) %all-to-all-start.4) | async-done | bytes 512032 | tf_op jit(solution)/shard_map/while/body/eval_jaxpr/all_to_all | solution.py:55
  295.2 11.6 all-to-all-done.5
  332.2 11.9 %all-to-all-done.6 = f32[125,128,8]{0,2,1:T(8,128)S(1)} async-done(((f32[125,128,8]{0,2,1:T(8,128)}), f32[125,128,8]{0,2,1:T(8,128)S(1)}, u32[]{:S(2)}, u32[]{:S(2)}) %all-to-all-start.6) | async-done | bytes 512032 | tf_op jit(solution)/shard_map/while/body/eval_jaxpr/all_to_all | solution.py:55
  377.3 11.6 all-to-all-done.7
  417.6 67.2 %pmax.8 = f32[]{:T(128)} all-reduce(f32[]{:T(128)} %multiply_reduce_fusion.5), channel_id=1, replica_groups=mesh['wall'=4,'span'=32] {'wall','span'}, use_global_device_ids=true, to_apply=%region_3.3 | all-reduce | flops 1 | bytes 8 | tf_op jit(solution)/shard_map/while/body/eval_jaxpr/pmax | solution.py:87
  517.6 11.9 %all-to-all-done.1 = f32[125,128,8]{0,2,1:T(8,128)S(1)} async-done(((f32[125,128,8]{0,2,1:T(8,128)}), f32[125,128,8]{0,2,1:T(8,128)S(1)}, u32[]{:S(2)}, u32[]{:S(2)}) %all-to-all-start.1) | async-done | bytes 512032 | tf_op jit(solution)/shard_map/while/body/eval_jaxpr/all_to_all | solution.py:55
  563.1 11.6 all-to-all-done.2
  599.8 11.9 %all-to-all-done.3 = f32[125,128,8]{0,2,1:T(8,128)S(1)} async-done(((f32[125,128,8]{0,2,1:T(8,128)}), f32[125,128,8]{0,2,1:T(8,128)S(1)}, u32[]{:S(2)}, u32[]{:S(2)}) %all-to-all-start.3) | async-done | bytes 512032 | tf_op jit(solution)/shard_map/while/body/eval_jaxpr/all_to_all | solution.py:55
  638.5 11.9 %all-to-all-done.4 = f32[125,128,8]{0,2,1:T(8,128)S(1)} async-done(((f32[125,128,8]{0,2,1:T(8,128)}), f32[125,128,8]{0,2,1:T(8,128)S(1)}, u32[]{:S(2)}, u32[]{:S(2)}) %all-to-all-start.4) | async-done | bytes 512032 | tf_op jit(solution)/shard_map/while/body/eval_jaxpr/all_to_all | solution.py:55
  720.7 11.9 %all-to-all-done.6 = f32[125,128,8]{0,2,1:T(8,128)S(1)} async-done(((f32[125,128,8]{0,2,1:T(8,128)}), f32[125,128,8]{0,2,1:T(8,128)S(1)}, u32[]{:S(2)}, u32[]{:S(2)}) %all-to-all-start.6) | async-done | bytes 512032 | tf_op jit(solution)/shard_map/while/body/eval_jaxpr/all_to_all | solution.py:55
  765.9 11.6 all-to-all-done.7
  806.1 67.2 %pmax.8 = f32[]{:T(128)} all-reduce(f32[]{:T(128)} %multiply_reduce_fusion.5), channel_id=1, replica_groups=mesh['wall'=4,'span'=32] {'wall','span'}, use_global_device_ids=true, to_apply=%region_3.3 | all-reduce | flops 1 | bytes 8 | tf_op jit(solution)/shard_map/while/body/eval_jaxpr/pmax | solution.py:87
  906.2 11.9 %all-to-all-done.1 = f32[125,128,8]{0,2,1:T(8,128)S(1)} async-done(((f32[125,128,8]{0,2,1:T(8,128)}), f32[125,128,8]{0,2,1:T(8,128)S(1)}, u32[]{:S(2)}, u32[]{:S(2)}) %all-to-all-start.1) | async-done | bytes 512032 | tf_op jit(solution)/shard_map/while/body/eval_jaxpr/all_to_all | solution.py:55
  951.7 11.6 all-to-all-done.2
  988.4 11.9 %all-to-all-done.3 = f32[125,128,8]{0,2,1:T(8,128)S(1)} async-done(((f32[125,128,8]{0,2,1:T(8,128)}), f32[125,128,8]{0,2,1:T(8,128)S(1)}, u32[]{:S(2)}, u32[]{:S(2)}) %all-to-all-start.3) | async-done | bytes 512032 | tf_op jit(solution)/shard_map/while/body/eval_jaxpr/all_to_all | solution.py:55
  1027.1 11.9 %all-to-all-done.4 = f32[125,128,8]{0,2,1:T(8,128)S(1)} async-done(((f32[125,128,8]{0,2,1:T(8,128)}), f32[125,128,8]{0,2,1:T(8,128)S(1)}, u32[]{:S(2)}, u32[]{:S(2)}) %all-to-all-start.4) | async-done | bytes 512032 | tf_op jit(solution)/shard_map/while/body/eval_jaxpr/all_to_all | solution.py:55
  1072.3 11.6 all-to-all-done.5
  1109.3 11.9 %all-to-all-done.6 = f32[125,128,8]{0,2,1:T(8,128)S(1)} async-done(((f32[125,128,8]{0,2,1:T(8,128)}), f32[125,128,8]{0,2,1:T(8,128)S(1)}, u32[]{:S(2)}, u32[]{:S(2)}) %all-to-all-start.6) | async-done | bytes 512032 | tf_op jit(solution)/shard_map/while/body/eval_jaxpr/all_to_all | solution.py:55
  1154.5 11.6 all-to-all-done.7
  (942 shorter events, 734.6 us)
Async XLA Ops:
  15.9 85.6 %all-to-all-start = ((f32[125,128,8]{0,2,1:T(8,128)}), f32[125,128,8]{0,2,1:T(8,128)S(1)}, u32[]{:S(2)}, u32[]{:S(2)}) async-start(f32[125,128,8]{0,2,1:T(8,128)} %select_bitcast_fusion.32), calls=%async_computation | async-start | bytes 1048576 | tf_op jit(solution)/shard_map/while/body/eval_jaxpr/all_to_all | solution.py:55
  121.9 18.8 %all-to-all-start.1 = ((f32[125,128,8]{0,2,1:T(8,128)}), f32[125,128,8]{0,2,1:T(8,128)S(1)}, u32[]{:S(2)}, u32[]{:S(2)}) async-start(f32[125,128,8]{0,2,1:T(8,128)} %select_bitcast_fusion.34), calls=%async_computation.1 | async-start | bytes 1048576 | tf_op jit(solution)/shard_map/while/body/eval_jaxpr/all_to_all | solution.py:55
  166.6 19.5 %all-to-all-start.2 = ((f32[125,128,8]{0,2,1:T(8,128)}), f32[125,128,8]{0,2,1:T(8,128)}, u32[]{:S(2)}, u32[]{:S(2)}) async-start(f32[125,128,8]{0,2,1:T(8,128)} %select_bitcast_fusion.36), calls=%async_computation.2 | async-start | bytes 1048576 | tf_op jit(solution)/shard_map/while/body/eval_jaxpr/all_to_all | solution.py:55
  204.7 18.4 %all-to-all-start.3 = ((f32[125,128,8]{0,2,1:T(8,128)}), f32[125,128,8]{0,2,1:T(8,128)S(1)}, u32[]{:S(2)}, u32[]{:S(2)}) async-start(f32[125,128,8]{0,2,1:T(8,128)} %select_bitcast_fusion.38), calls=%async_computation.3 | async-start | bytes 1048576 | tf_op jit(solution)/shard_map/while/body/eval_jaxpr/all_to_all | solution.py:55
  243.4 18.4 %all-to-all-start.4 = ((f32[125,128,8]{0,2,1:T(8,128)}), f32[125,128,8]{0,2,1:T(8,128)S(1)}, u32[]{:S(2)}, u32[]{:S(2)}) async-start(f32[125,128,8]{0,2,1:T(8,128)} %select_bitcast_fusion.40), calls=%async_computation.4 | async-start | bytes 1048576 | tf_op jit(solution)/shard_map/while/body/eval_jaxpr/all_to_all | solution.py:55
  287.7 19.1 %all-to-all-start.5 = ((f32[125,128,8]{0,2,1:T(8,128)}), f32[125,128,8]{0,2,1:T(8,128)}, u32[]{:S(2)}, u32[]{:S(2)}) async-start(f32[125,128,8]{0,2,1:T(8,128)} %select_bitcast_fusion.42), calls=%async_computation.5 | async-start | bytes 1048576 | tf_op jit(solution)/shard_map/while/body/eval_jaxpr/all_to_all | solution.py:55
  325.4 18.7 %all-to-all-start.6 = ((f32[125,128,8]{0,2,1:T(8,128)}), f32[125,128,8]{0,2,1:T(8,128)S(1)}, u32[]{:S(2)}, u32[]{:S(2)}) async-start(f32[125,128,8]{0,2,1:T(8,128)} %select_bitcast_fusion.44), calls=%async_computation.6 | async-start | bytes 1048576 | tf_op jit(solution)/shard_map/while/body/eval_jaxpr/all_to_all | solution.py:55
  369.9 19.0 %all-to-all-start.7 = ((f32[125,128,8]{0,2,1:T(8,128)}), f32[125,128,8]{0,2,1:T(8,128)}, u32[]{:S(2)}, u32[]{:S(2)}) async-start(f32[125,128,8]{0,2,1:T(8,128)} %select_bitcast_fusion.46), calls=%async_computation.7 | async-start | bytes 1048576 | tf_op jit(solution)/shard_map/while/body/eval_jaxpr/all_to_all | solution.py:55
  411.8 78.5 %all-to-all-start = ((f32[125,128,8]{0,2,1:T(8,128)}), f32[125,128,8]{0,2,1:T(8,128)S(1)}, u32[]{:S(2)}, u32[]{:S(2)}) async-start(f32[125,128,8]{0,2,1:T(8,128)} %select_bitcast_fusion.32), calls=%async_computation | async-start | bytes 1048576 | tf_op jit(solution)/shard_map/while/body/eval_jaxpr/all_to_all | solution.py:55
  510.8 18.7 %all-to-all-start.1 = ((f32[125,128,8]{0,2,1:T(8,128)}), f32[125,128,8]{0,2,1:T(8,128)S(1)}, u32[]{:S(2)}, u32[]{:S(2)}) async-start(f32[125,128,8]{0,2,1:T(8,128)} %select_bitcast_fusion.34), calls=%async_computation.1 | async-start | bytes 1048576 | tf_op jit(solution)/shard_map/while/body/eval_jaxpr/all_to_all | solution.py:55
  555.4 19.3 %all-to-all-start.2 = ((f32[125,128,8]{0,2,1:T(8,128)}), f32[125,128,8]{0,2,1:T(8,128)}, u32[]{:S(2)}, u32[]{:S(2)}) async-start(f32[125,128,8]{0,2,1:T(8,128)} %select_bitcast_fusion.36), calls=%async_computation.2 | async-start | bytes 1048576 | tf_op jit(solution)/shard_map/while/body/eval_jaxpr/all_to_all | solution.py:55
  593.3 18.4 %all-to-all-start.3 = ((f32[125,128,8]{0,2,1:T(8,128)}), f32[125,128,8]{0,2,1:T(8,128)S(1)}, u32[]{:S(2)}, u32[]{:S(2)}) async-start(f32[125,128,8]{0,2,1:T(8,128)} %select_bitcast_fusion.38), calls=%async_computation.3 | async-start | bytes 1048576 | tf_op jit(solution)/shard_map/while/body/eval_jaxpr/all_to_all | solution.py:55
  632.0 18.4 %all-to-all-start.4 = ((f32[125,128,8]{0,2,1:T(8,128)}), f32[125,128,8]{0,2,1:T(8,128)S(1)}, u32[]{:S(2)}, u32[]{:S(2)}) async-start(f32[125,128,8]{0,2,1:T(8,128)} %select_bitcast_fusion.40), calls=%async_computation.4 | async-start | bytes 1048576 | tf_op jit(solution)/shard_map/while/body/eval_jaxpr/all_to_all | solution.py:55
  676.3 19.1 %all-to-all-start.5 = ((f32[125,128,8]{0,2,1:T(8,128)}), f32[125,128,8]{0,2,1:T(8,128)}, u32[]{:S(2)}, u32[]{:S(2)}) async-start(f32[125,128,8]{0,2,1:T(8,128)} %select_bitcast_fusion.42), calls=%async_computation.5 | async-start | bytes 1048576 | tf_op jit(solution)/shard_map/while/body/eval_jaxpr/all_to_all | solution.py:55
  713.9 18.7 %all-to-all-start.6 = ((f32[125,128,8]{0,2,1:T(8,128)}), f32[125,128,8]{0,2,1:T(8,128)S(1)}, u32[]{:S(2)}, u32[]{:S(2)}) async-start(f32[125,128,8]{0,2,1:T(8,128)} %select_bitcast_fusion.44), calls=%async_computation.6 | async-start | bytes 1048576 | tf_op jit(solution)/shard_map/while/body/eval_jaxpr/all_to_all | solution.py:55
  758.5 19.0 %all-to-all-start.7 = ((f32[125,128,8]{0,2,1:T(8,128)}), f32[125,128,8]{0,2,1:T(8,128)}, u32[]{:S(2)}, u32[]{:S(2)}) async-start(f32[125,128,8]{0,2,1:T(8,128)} %select_bitcast_fusion.46), calls=%async_computation.7 | async-start | bytes 1048576 | tf_op jit(solution)/shard_map/while/body/eval_jaxpr/all_to_all | solution.py:55
  800.3 78.5 %all-to-all-start = ((f32[125,128,8]{0,2,1:T(8,128)}), f32[125,128,8]{0,2,1:T(8,128)S(1)}, u32[]{:S(2)}, u32[]{:S(2)}) async-start(f32[125,128,8]{0,2,1:T(8,128)} %select_bitcast_fusion.32), calls=%async_computation | async-start | bytes 1048576 | tf_op jit(solution)/shard_map/while/body/eval_jaxpr/all_to_all | solution.py:55
  899.4 18.7 %all-to-all-start.1 = ((f32[125,128,8]{0,2,1:T(8,128)}), f32[125,128,8]{0,2,1:T(8,128)S(1)}, u32[]{:S(2)}, u32[]{:S(2)}) async-start(f32[125,128,8]{0,2,1:T(8,128)} %select_bitcast_fusion.34), calls=%async_computation.1 | async-start | bytes 1048576 | tf_op jit(solution)/shard_map/while/body/eval_jaxpr/all_to_all | solution.py:55
  943.9 19.3 %all-to-all-start.2 = ((f32[125,128,8]{0,2,1:T(8,128)}), f32[125,128,8]{0,2,1:T(8,128)}, u32[]{:S(2)}, u32[]{:S(2)}) async-start(f32[125,128,8]{0,2,1:T(8,128)} %select_bitcast_fusion.36), calls=%async_computation.2 | async-start | bytes 1048576 | tf_op jit(solution)/shard_map/while/body/eval_jaxpr/all_to_all | solution.py:55
  981.9 18.4 %all-to-all-start.3 = ((f32[125,128,8]{0,2,1:T(8,128)}), f32[125,128,8]{0,2,1:T(8,128)S(1)}, u32[]{:S(2)}, u32[]{:S(2)}) async-start(f32[125,128,8]{0,2,1:T(8,128)} %select_bitcast_fusion.38), calls=%async_computation.3 | async-start | bytes 1048576 | tf_op jit(solution)/shard_map/while/body/eval_jaxpr/all_to_all | solution.py:55
  1020.5 18.4 %all-to-all-start.4 = ((f32[125,128,8]{0,2,1:T(8,128)}), f32[125,128,8]{0,2,1:T(8,128)S(1)}, u32[]{:S(2)}, u32[]{:S(2)}) async-start(f32[125,128,8]{0,2,1:T(8,128)} %select_bitcast_fusion.40), calls=%async_computation.4 | async-start | bytes 1048576 | tf_op jit(solution)/shard_map/while/body/eval_jaxpr/all_to_all | solution.py:55
  1064.8 19.1 %all-to-all-start.5 = ((f32[125,128,8]{0,2,1:T(8,128)}), f32[125,128,8]{0,2,1:T(8,128)}, u32[]{:S(2)}, u32[]{:S(2)}) async-start(f32[125,128,8]{0,2,1:T(8,128)} %select_bitcast_fusion.42), calls=%async_computation.5 | async-start | bytes 1048576 | tf_op jit(solution)/shard_map/while/body/eval_jaxpr/all_to_all | solution.py:55
  1102.5 18.7 %all-to-all-start.6 = ((f32[125,128,8]{0,2,1:T(8,128)}), f32[125,128,8]{0,2,1:T(8,128)S(1)}, u32[]{:S(2)}, u32[]{:S(2)}) async-start(f32[125,128,8]{0,2,1:T(8,128)} %select_bitcast_fusion.44), calls=%async_computation.6 | async-start | bytes 1048576 | tf_op jit(solution)/shard_map/while/body/eval_jaxpr/all_to_all | solution.py:55
  1147.0 19.0 %all-to-all-start.7 = ((f32[125,128,8]{0,2,1:T(8,128)}), f32[125,128,8]{0,2,1:T(8,128)}, u32[]{:S(2)}, u32[]{:S(2)}) async-start(f32[125,128,8]{0,2,1:T(8,128)} %select_bitcast_fusion.46), calls=%async_computation.7 | async-start | bytes 1048576 | tf_op jit(solution)/shard_map/while/body/eval_jaxpr/all_to_all | solution.py:55
  (131 other events, 1059.7 us)
where the time goes:
time: 1190 us; the launch traced here: 1180 us
  local copies, waits for them, and re-layouts  352 us (30%)
  waiting for transfers between devices  247 us (21%)
  blocking collectives  202 us (17%)
  matrix products  141 us (12%)
  starting transfers between devices  132 us (11%)
  other arithmetic  98.6 us (8%)
    all_to_all x24, waiting for transfers between devices, send_slots(): lax.all_to_all(outgoing, ('wall', 'span'), split_axis=1, concat_axis=1, t...  247 us
    pmax x3, blocking collectives, coarse_step(): fastest = lax.pmax(jnp.max(element_rates), ('wall', 'span'))  202 us
    all_to_all x24, starting transfers between devices, send_slots(): lax.all_to_all(outgoing, ('wall', 'span'), split_axis=1, concat_axis=1, t...  132 us
    gather x24, local copies, waits for them, and re-layouts, coarse_step(): jnp.take(trace_table, send_row, axis=1)  78.5 us
    gather x24, local copies, waits for them, and re-layouts, coarse_step(): nearby = arrange(jnp.take(lookup, pointers, axis=1), local_count)  72.1 us
    dot_general x24, matrix products, tendency(): jnp.einsum('vw,wpe->vpe', flux_mixing, combined, precision=lax.Precision....  53.4 us
    dot_general x24, matrix products, tendency(): jnp.einsum('pq,vqe->vpe', volume_block, fields, precision=lax.Precision.H...  45.4 us
    while x318, local copies, waits for them, and re-layouts  43.8 us
  transfers between devices with their start and end apart: 24, of which 21 were waited for; matrix products, arithmetic and copies ran while one was open for 5% of the time, Pallas kernels for 0%

commit v1 on v0

--- a/solution.py
+++ b/solution.py
@@ -84,15 +84,21 @@
     def coarse_step(coarse_index, carry):
         fields, cache = carry
         element_rates = metric_scale * (1.0 + jnp.sqrt(jnp.mean(fields * fields, axis=(0, 1))))
-        fastest = lax.pmax(jnp.max(element_rates), ("wall", "span"))
-        step_sizes = COURANT / fastest / divisors
+        local_fastest = jnp.max(element_rates)
+        step_sizes = None
         for substep in range(substeps):
             lowest = lowest_level(substep)
             trace_table = make_table(fields)
-            outgoing = jnp.take(trace_table, send_row, axis=1).reshape(
-                TRACE_ROWS, peers, slot_count
-            )
-            received = send_slots(outgoing).reshape(TRACE_ROWS, peers * slot_count)
+            outgoing = jnp.take(trace_table, send_row, axis=1)
+            if substep == 0:
+                rate_row = jnp.full((1, outgoing.shape[1]), local_fastest, jnp.float32)
+                outgoing = jnp.concatenate([outgoing, rate_row], axis=0)
+            outgoing = outgoing.reshape(outgoing.shape[0], peers, slot_count)
+            received = send_slots(outgoing).reshape(outgoing.shape[0], peers * slot_count)
+            if substep == 0:
+                fastest = jnp.max(received[TRACE_ROWS])
+                received = received[:TRACE_ROWS]
+                step_sizes = COURANT / fastest / divisors
             lookup = jnp.concatenate([trace_table, received], axis=1)
             nearby = arrange(jnp.take(lookup, pointers, axis=1), local_count)
             change = tendency(fields, nearby, volume_block, lift_block, flux_mixing, metric_scale)

time: 1190 us -> 1010 us (0.85)
  blocking collectives: 202 us -> 0 us
  waiting for transfers between devices: 247 us -> 276 us
    pmax x3 -> x0, blocking collectives: 202 us -> none  [coarse_step(): fastest = lax.pmax(jnp.max(element_rates), ('wall', 'span'))]
    all_to_all x24, waiting for transfers between devices: 247 us -> 276 us  [send_slots(): lax.all_to_all(outgoing, ('wall', 'span'), split_axis=1, concat_axis=1, t...]
    reshape x24 -> x21, other arithmetic: 33.5 us -> 30.6 us  [coarse_step(): outgoing = outgoing.reshape(outgoing.shape[0], peers, slot_count)]
    while x318 -> x336, local copies, waits for them, and re-layouts: 43.8 us -> 43.7 us
  transfers between devices with their start and end apart: 24 -> 24, of which waited for: 21 -> 24; matrix products, arithmetic and copies ran while one was open for 5% -> 5% of each run, Pallas kernels for 0% -> 0%
where the time goes in v1:
time: 1010 us
  local copies, waits for them, and re-layouts  356 us (35%)
  waiting for transfers between devices  276 us (27%)
  matrix products  141 us (14%)
  starting transfers between devices  131 us (13%)
  other arithmetic  93.1 us (9%)
    all_to_all x24, waiting for transfers between devices, send_slots(): lax.all_to_all(outgoing, ('wall', 'span'), split_axis=1, concat_axis=1, t...  276 us
    all_to_all x24, starting transfers between devices, send_slots(): lax.all_to_all(outgoing, ('wall', 'span'), split_axis=1, concat_axis=1, t...  131 us
    gather x24, local copies, waits for them, and re-layouts, coarse_step(): outgoing = jnp.take(trace_table, send_row, axis=1)  78.5 us
    gather x24, local copies, waits for them, and re-layouts, coarse_step(): nearby = arrange(jnp.take(lookup, pointers, axis=1), local_count)  72.1 us
    dot_general x24, matrix products, tendency(): jnp.einsum('vw,wpe->vpe', flux_mixing, combined, precision=lax.Precision....  53.4 us
    dot_general x24, matrix products, tendency(): jnp.einsum('pq,vqe->vpe', volume_block, fields, precision=lax.Precision.H...  45.4 us
    while x336, local copies, waits for them, and re-layouts  43.7 us
    dot_general x24, matrix products, tendency(): jnp.einsum('pj,vje->vpe', lift_block, face_jumps, precision=lax.Precision...  41.9 us
  transfers between devices with their start and end apart: 24, of which 24 were waited for; matrix products, arithmetic and copies ran while one was open for 5% of the time, Pallas kernels for 0%

profile of v1, /device:TPU:1, one launch (start us, length us, event | category | flops | bytes accessed | tf_op | source)
XLA Modules:
  0.0 1006.0 jit_solution(5475105695231317987)
XLA Ops:
  3.9 999.6 %while.10 = (s32[]{:T(128)}, f32[5,125,256]{2,0,1:T(8,128)}, s32[256]{0:T(256)}, s32[1024]{0:T(1024)}, f32[256]{0:T(256)S(1)}, /*index=5*/f32[256]{0:T(256)S(1)}...) while((s32[]{:T(128)}, f32[5,125,256]{2,0,1:T(8,128)}, ...), condition=%wide.region_4.7_spmd, body=%wide.region_0.6_spmd.sunk | while | flops 4314205184 | bytes 338939136 | solution.py:108
  17.2 11.5 %all-to-all-start = ((f32[126,128,8]{0,2,1:T(8,128)}), f32[126,128,8]{0,2,1:T(8,128)S(1)}, u32[]{:S(2)}, u32[]{:S(2)}) async-start(f32[126,128,8]{0,2,1:T(8,128)} %pad_bitcast_fusion.2), calls=%async_computation | async-start | bytes 1048576 | tf_op jit(solution)/shard_map/while/body/eval_jaxpr/all_to_all | solution.py:55
  70.2 11.9 %all-to-all-done.1 = f32[125,128,8]{0,2,1:T(8,128)S(1)} async-done(((f32[125,128,8]{0,2,1:T(8,128)}), f32[125,128,8]{0,2,1:T(8,128)S(1)}, u32[]{:S(2)}, u32[]{:S(2)}) %all-to-all-start.1) | async-done | bytes 512032 | tf_op jit(solution)/shard_map/while/body/eval_jaxpr/all_to_all | solution.py:55
  115.5 11.6 %all-to-all-done.2 = f32[125,128,8]{0,2,1:T(8,128)} async-done(((f32[125,128,8]{0,2,1:T(8,128)}), f32[125,128,8]{0,2,1:T(8,128)}, u32[]{:S(2)}, u32[]{:S(2)}) %all-to-all-start.2) | async-done | bytes 512032 | tf_op jit(solution)/shard_map/while/body/eval_jaxpr/all_to_all | solution.py:55
  152.7 11.9 %all-to-all-done.3 = f32[125,128,8]{0,2,1:T(8,128)S(1)} async-done(((f32[125,128,8]{0,2,1:T(8,128)}), f32[125,128,8]{0,2,1:T(8,128)S(1)}, u32[]{:S(2)}, u32[]{:S(2)}) %all-to-all-start.3) | async-done | bytes 512032 | tf_op jit(solution)/shard_map/while/body/eval_jaxpr/all_to_all | solution.py:55
  191.3 11.9 %all-to-all-done.4 = f32[125,128,8]{0,2,1:T(8,128)S(1)} async-done(((f32[125,128,8]{0,2,1:T(8,128)}), f32[125,128,8]{0,2,1:T(8,128)S(1)}, u32[]{:S(2)}, u32[]{:S(2)}) %all-to-all-start.4) | async-done | bytes 512032 | tf_op jit(solution)/shard_map/while/body/eval_jaxpr/all_to_all | solution.py:55
  236.5 11.6 %all-to-all-done.5 = f32[125,128,8]{0,2,1:T(8,128)} async-done(((f32[125,128,8]{0,2,1:T(8,128)}), f32[125,128,8]{0,2,1:T(8,128)}, u32[]{:S(2)}, u32[]{:S(2)}) %all-to-all-start.5) | async-done | bytes 512032 | tf_op jit(solution)/shard_map/while/body/eval_jaxpr/all_to_all | solution.py:55
  273.2 11.9 %all-to-all-done.6 = f32[125,128,8]{0,2,1:T(8,128)S(1)} async-done(((f32[125,128,8]{0,2,1:T(8,128)}), f32[125,128,8]{0,2,1:T(8,128)S(1)}, u32[]{:S(2)}, u32[]{:S(2)}) %all-to-all-start.6) | async-done | bytes 512032 | tf_op jit(solution)/shard_map/while/body/eval_jaxpr/all_to_all | solution.py:55
  318.7 11.6 %all-to-all-done.7 = f32[125,128,8]{0,2,1:T(8,128)} async-done(((f32[125,128,8]{0,2,1:T(8,128)}), f32[125,128,8]{0,2,1:T(8,128)}, u32[]{:S(2)}, u32[]{:S(2)}) %all-to-all-start.7) | async-done | bytes 512032 | tf_op jit(solution)/shard_map/while/body/eval_jaxpr/all_to_all | solution.py:55
  363.7 9.5 all-to-all-done
  400.8 11.9 %all-to-all-done.1 = f32[125,128,8]{0,2,1:T(8,128)S(1)} async-done(((f32[125,128,8]{0,2,1:T(8,128)}), f32[125,128,8]{0,2,1:T(8,128)S(1)}, u32[]{:S(2)}, u32[]{:S(2)}) %all-to-all-start.1) | async-done | bytes 512032 | tf_op jit(solution)/shard_map/while/body/eval_jaxpr/all_to_all | solution.py:55
  446.0 11.6 %all-to-all-done.2 = f32[125,128,8]{0,2,1:T(8,128)} async-done(((f32[125,128,8]{0,2,1:T(8,128)}), f32[125,128,8]{0,2,1:T(8,128)}, u32[]{:S(2)}, u32[]{:S(2)}) %all-to-all-start.2) | async-done | bytes 512032 | tf_op jit(solution)/shard_map/while/body/eval_jaxpr/all_to_all | solution.py:55
  483.0 11.9 %all-to-all-done.3 = f32[125,128,8]{0,2,1:T(8,128)S(1)} async-done(((f32[125,128,8]{0,2,1:T(8,128)}), f32[125,128,8]{0,2,1:T(8,128)S(1)}, u32[]{:S(2)}, u32[]{:S(2)}) %all-to-all-start.3) | async-done | bytes 512032 | tf_op jit(solution)/shard_map/while/body/eval_jaxpr/all_to_all | solution.py:55
  521.6 11.9 %all-to-all-done.4 = f32[125,128,8]{0,2,1:T(8,128)S(1)} async-done(((f32[125,128,8]{0,2,1:T(8,128)}), f32[125,128,8]{0,2,1:T(8,128)S(1)}, u32[]{:S(2)}, u32[]{:S(2)}) %all-to-all-start.4) | async-done | bytes 512032 | tf_op jit(solution)/shard_map/while/body/eval_jaxpr/all_to_all | solution.py:55
  566.8 11.6 %all-to-all-done.5 = f32[125,128,8]{0,2,1:T(8,128)} async-done(((f32[125,128,8]{0,2,1:T(8,128)}), f32[125,128,8]{0,2,1:T(8,128)}, u32[]{:S(2)}, u32[]{:S(2)}) %all-to-all-start.5) | async-done | bytes 512032 | tf_op jit(solution)/shard_map/while/body/eval_jaxpr/all_to_all | solution.py:55
  603.6 11.9 %all-to-all-done.6 = f32[125,128,8]{0,2,1:T(8,128)S(1)} async-done(((f32[125,128,8]{0,2,1:T(8,128)}), f32[125,128,8]{0,2,1:T(8,128)S(1)}, u32[]{:S(2)}, u32[]{:S(2)}) %all-to-all-start.6) | async-done | bytes 512032 | tf_op jit(solution)/shard_map/while/body/eval_jaxpr/all_to_all | solution.py:55
  649.0 11.6 %all-to-all-done.7 = f32[125,128,8]{0,2,1:T(8,128)} async-done(((f32[125,128,8]{0,2,1:T(8,128)}), f32[125,128,8]{0,2,1:T(8,128)}, u32[]{:S(2)}, u32[]{:S(2)}) %all-to-all-start.7) | async-done | bytes 512032 | tf_op jit(solution)/shard_map/while/body/eval_jaxpr/all_to_all | solution.py:55
  731.1 11.9 %all-to-all-done.1 = f32[125,128,8]{0,2,1:T(8,128)S(1)} async-done(((f32[125,128,8]{0,2,1:T(8,128)}), f32[125,128,8]{0,2,1:T(8,128)S(1)}, u32[]{:S(2)}, u32[]{:S(2)}) %all-to-all-start.1) | async-done | bytes 512032 | tf_op jit(solution)/shard_map/while/body/eval_jaxpr/all_to_all | solution.py:55
  776.4 11.6 %all-to-all-done.2 = f32[125,128,8]{0,2,1:T(8,128)} async-done(((f32[125,128,8]{0,2,1:T(8,128)}), f32[125,128,8]{0,2,1:T(8,128)}, u32[]{:S(2)}, u32[]{:S(2)}) %all-to-all-start.2) | async-done | bytes 512032 | tf_op jit(solution)/shard_map/while/body/eval_jaxpr/all_to_all | solution.py:55
  813.3 11.9 %all-to-all-done.3 = f32[125,128,8]{0,2,1:T(8,128)S(1)} async-done(((f32[125,128,8]{0,2,1:T(8,128)}), f32[125,128,8]{0,2,1:T(8,128)S(1)}, u32[]{:S(2)}, u32[]{:S(2)}) %all-to-all-start.3) | async-done | bytes 512032 | tf_op jit(solution)/shard_map/while/body/eval_jaxpr/all_to_all | solution.py:55
  851.9 11.9 %all-to-all-done.4 = f32[125,128,8]{0,2,1:T(8,128)S(1)} async-done(((f32[125,128,8]{0,2,1:T(8,128)}), f32[125,128,8]{0,2,1:T(8,128)S(1)}, u32[]{:S(2)}, u32[]{:S(2)}) %all-to-all-start.4) | async-done | bytes 512032 | tf_op jit(solution)/shard_map/while/body/eval_jaxpr/all_to_all | solution.py:55
  897.2 11.6 %all-to-all-done.5 = f32[125,128,8]{0,2,1:T(8,128)} async-done(((f32[125,128,8]{0,2,1:T(8,128)}), f32[125,128,8]{0,2,1:T(8,128)}, u32[]{:S(2)}, u32[]{:S(2)}) %all-to-all-start.5) | async-done | bytes 512032 | tf_op jit(solution)/shard_map/while/body/eval_jaxpr/all_to_all | solution.py:55
  933.9 11.9 %all-to-all-done.6 = f32[125,128,8]{0,2,1:T(8,128)S(1)} async-done(((f32[125,128,8]{0,2,1:T(8,128)}), f32[125,128,8]{0,2,1:T(8,128)S(1)}, u32[]{:S(2)}, u32[]{:S(2)}) %all-to-all-start.6) | async-done | bytes 512032 | tf_op jit(solution)/shard_map/while/body/eval_jaxpr/all_to_all | solution.py:55
  979.4 11.6 %all-to-all-done.7 = f32[125,128,8]{0,2,1:T(8,128)} async-done(((f32[125,128,8]{0,2,1:T(8,128)}), f32[125,128,8]{0,2,1:T(8,128)}, u32[]{:S(2)}, u32[]{:S(2)}) %all-to-all-start.7) | async-done | bytes 512032 | tf_op jit(solution)/shard_map/while/body/eval_jaxpr/all_to_all | solution.py:55
  (966 shorter events, 728.5 us)
Async XLA Ops:
  17.2 25.2 %all-to-all-start = ((f32[126,128,8]{0,2,1:T(8,128)}), f32[126,128,8]{0,2,1:T(8,128)S(1)}, u32[]{:S(2)}, u32[]{:S(2)}) async-start(f32[126,128,8]{0,2,1:T(8,128)} %pad_bitcast_fusion.2), calls=%async_computation | async-start | bytes 1048576 | tf_op jit(solution)/shard_map/while/body/eval_jaxpr/all_to_all | solution.py:55
  63.5 18.6 %all-to-all-start.1 = ((f32[125,128,8]{0,2,1:T(8,128)}), f32[125,128,8]{0,2,1:T(8,128)S(1)}, u32[]{:S(2)}, u32[]{:S(2)}) async-start(f32[125,128,8]{0,2,1:T(8,128)} %select_bitcast_fusion.34), calls=%async_computation.1 | async-start | bytes 1048576 | tf_op jit(solution)/shard_map/while/body/eval_jaxpr/all_to_all | solution.py:55
  107.9 19.2 %all-to-all-start.2 = ((f32[125,128,8]{0,2,1:T(8,128)}), f32[125,128,8]{0,2,1:T(8,128)}, u32[]{:S(2)}, u32[]{:S(2)}) async-start(f32[125,128,8]{0,2,1:T(8,128)} %select_bitcast_fusion.36), calls=%async_computation.2 | async-start | bytes 1048576 | tf_op jit(solution)/shard_map/while/body/eval_jaxpr/all_to_all | solution.py:55
  145.7 18.9 %all-to-all-start.3 = ((f32[125,128,8]{0,2,1:T(8,128)}), f32[125,128,8]{0,2,1:T(8,128)S(1)}, u32[]{:S(2)}, u32[]{:S(2)}) async-start(f32[125,128,8]{0,2,1:T(8,128)} %select_bitcast_fusion.38), calls=%async_computation.3 | async-start | bytes 1048576 | tf_op jit(solution)/shard_map/while/body/eval_jaxpr/all_to_all | solution.py:55
  184.8 18.4 %all-to-all-start.4 = ((f32[125,128,8]{0,2,1:T(8,128)}), f32[125,128,8]{0,2,1:T(8,128)S(1)}, u32[]{:S(2)}, u32[]{:S(2)}) async-start(f32[125,128,8]{0,2,1:T(8,128)} %select_bitcast_fusion.40), calls=%async_computation.4 | async-start | bytes 1048576 | tf_op jit(solution)/shard_map/while/body/eval_jaxpr/all_to_all | solution.py:55
  229.0 19.1 %all-to-all-start.5 = ((f32[125,128,8]{0,2,1:T(8,128)}), f32[125,128,8]{0,2,1:T(8,128)}, u32[]{:S(2)}, u32[]{:S(2)}) async-start(f32[125,128,8]{0,2,1:T(8,128)} %select_bitcast_fusion.42), calls=%async_computation.5 | async-start | bytes 1048576 | tf_op jit(solution)/shard_map/while/body/eval_jaxpr/all_to_all | solution.py:55
  266.7 18.5 %all-to-all-start.6 = ((f32[125,128,8]{0,2,1:T(8,128)}), f32[125,128,8]{0,2,1:T(8,128)S(1)}, u32[]{:S(2)}, u32[]{:S(2)}) async-start(f32[125,128,8]{0,2,1:T(8,128)} %select_bitcast_fusion.44), calls=%async_computation.6 | async-start | bytes 1048576 | tf_op jit(solution)/shard_map/while/body/eval_jaxpr/all_to_all | solution.py:55
  311.0 19.3 %all-to-all-start.7 = ((f32[125,128,8]{0,2,1:T(8,128)}), f32[125,128,8]{0,2,1:T(8,128)}, u32[]{:S(2)}, u32[]{:S(2)}) async-start(f32[125,128,8]{0,2,1:T(8,128)} %select_bitcast_fusion.46), calls=%async_computation.7 | async-start | bytes 1048576 | tf_op jit(solution)/shard_map/while/body/eval_jaxpr/all_to_all | solution.py:55
  355.0 18.2 %all-to-all-start = ((f32[126,128,8]{0,2,1:T(8,128)}), f32[126,128,8]{0,2,1:T(8,128)S(1)}, u32[]{:S(2)}, u32[]{:S(2)}) async-start(f32[126,128,8]{0,2,1:T(8,128)} %pad_bitcast_fusion.2), calls=%async_computation | async-start | bytes 1048576 | tf_op jit(solution)/shard_map/while/body/eval_jaxpr/all_to_all | solution.py:55
  394.2 18.5 %all-to-all-start.1 = ((f32[125,128,8]{0,2,1:T(8,128)}), f32[125,128,8]{0,2,1:T(8,128)S(1)}, u32[]{:S(2)}, u32[]{:S(2)}) async-start(f32[125,128,8]{0,2,1:T(8,128)} %select_bitcast_fusion.34), calls=%async_computation.1 | async-start | bytes 1048576 | tf_op jit(solution)/shard_map/while/body/eval_jaxpr/all_to_all | solution.py:55
  438.5 19.1 %all-to-all-start.2 = ((f32[125,128,8]{0,2,1:T(8,128)}), f32[125,128,8]{0,2,1:T(8,128)}, u32[]{:S(2)}, u32[]{:S(2)}) async-start(f32[125,128,8]{0,2,1:T(8,128)} %select_bitcast_fusion.36), calls=%async_computation.2 | async-start | bytes 1048576 | tf_op jit(solution)/shard_map/while/body/eval_jaxpr/all_to_all | solution.py:55
  476.2 18.7 %all-to-all-start.3 = ((f32[125,128,8]{0,2,1:T(8,128)}), f32[125,128,8]{0,2,1:T(8,128)S(1)}, u32[]{:S(2)}, u32[]{:S(2)}) async-start(f32[125,128,8]{0,2,1:T(8,128)} %select_bitcast_fusion.38), calls=%async_computation.3 | async-start | bytes 1048576 | tf_op jit(solution)/shard_map/while/body/eval_jaxpr/all_to_all | solution.py:55
  515.1 18.4 %all-to-all-start.4 = ((f32[125,128,8]{0,2,1:T(8,128)}), f32[125,128,8]{0,2,1:T(8,128)S(1)}, u32[]{:S(2)}, u32[]{:S(2)}) async-start(f32[125,128,8]{0,2,1:T(8,128)} %select_bitcast_fusion.40), calls=%async_computation.4 | async-start | bytes 1048576 | tf_op jit(solution)/shard_map/while/body/eval_jaxpr/all_to_all | solution.py:55
  559.4 19.1 %all-to-all-start.5 = ((f32[125,128,8]{0,2,1:T(8,128)}), f32[125,128,8]{0,2,1:T(8,128)}, u32[]{:S(2)}, u32[]{:S(2)}) async-start(f32[125,128,8]{0,2,1:T(8,128)} %select_bitcast_fusion.42), calls=%async_computation.5 | async-start | bytes 1048576 | tf_op jit(solution)/shard_map/while/body/eval_jaxpr/all_to_all | solution.py:55
  597.0 18.5 %all-to-all-start.6 = ((f32[125,128,8]{0,2,1:T(8,128)}), f32[125,128,8]{0,2,1:T(8,128)S(1)}, u32[]{:S(2)}, u32[]{:S(2)}) async-start(f32[125,128,8]{0,2,1:T(8,128)} %select_bitcast_fusion.44), calls=%async_computation.6 | async-start | bytes 1048576 | tf_op jit(solution)/shard_map/while/body/eval_jaxpr/all_to_all | solution.py:55
  641.3 19.3 %all-to-all-start.7 = ((f32[125,128,8]{0,2,1:T(8,128)}), f32[125,128,8]{0,2,1:T(8,128)}, u32[]{:S(2)}, u32[]{:S(2)}) async-start(f32[125,128,8]{0,2,1:T(8,128)} %select_bitcast_fusion.46), calls=%async_computation.7 | async-start | bytes 1048576 | tf_op jit(solution)/shard_map/while/body/eval_jaxpr/all_to_all | solution.py:55
  685.3 18.2 %all-to-all-start = ((f32[126,128,8]{0,2,1:T(8,128)}), f32[126,128,8]{0,2,1:T(8,128)S(1)}, u32[]{:S(2)}, u32[]{:S(2)}) async-start(f32[126,128,8]{0,2,1:T(8,128)} %pad_bitcast_fusion.2), calls=%async_computation | async-start | bytes 1048576 | tf_op jit(solution)/shard_map/while/body/eval_jaxpr/all_to_all | solution.py:55
  724.5 18.5 %all-to-all-start.1 = ((f32[125,128,8]{0,2,1:T(8,128)}), f32[125,128,8]{0,2,1:T(8,128)S(1)}, u32[]{:S(2)}, u32[]{:S(2)}) async-start(f32[125,128,8]{0,2,1:T(8,128)} %select_bitcast_fusion.34), calls=%async_computation.1 | async-start | bytes 1048576 | tf_op jit(solution)/shard_map/while/body/eval_jaxpr/all_to_all | solution.py:55
  768.9 19.1 %all-to-all-start.2 = ((f32[125,128,8]{0,2,1:T(8,128)}), f32[125,128,8]{0,2,1:T(8,128)}, u32[]{:S(2)}, u32[]{:S(2)}) async-start(f32[125,128,8]{0,2,1:T(8,128)} %select_bitcast_fusion.36), calls=%async_computation.2 | async-start | bytes 1048576 | tf_op jit(solution)/shard_map/while/body/eval_jaxpr/all_to_all | solution.py:55
  806.5 18.7 %all-to-all-start.3 = ((f32[125,128,8]{0,2,1:T(8,128)}), f32[125,128,8]{0,2,1:T(8,128)S(1)}, u32[]{:S(2)}, u32[]{:S(2)}) async-start(f32[125,128,8]{0,2,1:T(8,128)} %select_bitcast_fusion.38), calls=%async_computation.3 | async-start | bytes 1048576 | tf_op jit(solution)/shard_map/while/body/eval_jaxpr/all_to_all | solution.py:55
  845.4 18.4 %all-to-all-start.4 = ((f32[125,128,8]{0,2,1:T(8,128)}), f32[125,128,8]{0,2,1:T(8,128)S(1)}, u32[]{:S(2)}, u32[]{:S(2)}) async-start(f32[125,128,8]{0,2,1:T(8,128)} %select_bitcast_fusion.40), calls=%async_computation.4 | async-start | bytes 1048576 | tf_op jit(solution)/shard_map/while/body/eval_jaxpr/all_to_all | solution.py:55
  889.7 19.1 %all-to-all-start.5 = ((f32[125,128,8]{0,2,1:T(8,128)}), f32[125,128,8]{0,2,1:T(8,128)}, u32[]{:S(2)}, u32[]{:S(2)}) async-start(f32[125,128,8]{0,2,1:T(8,128)} %select_bitcast_fusion.42), calls=%async_computation.5 | async-start | bytes 1048576 | tf_op jit(solution)/shard_map/while/body/eval_jaxpr/all_to_all | solution.py:55
  927.3 18.5 %all-to-all-start.6 = ((f32[125,128,8]{0,2,1:T(8,128)}), f32[125,128,8]{0,2,1:T(8,128)S(1)}, u32[]{:S(2)}, u32[]{:S(2)}) async-start(f32[125,128,8]{0,2,1:T(8,128)} %select_bitcast_fusion.44), calls=%async_computation.6 | async-start | bytes 1048576 | tf_op jit(solution)/shard_map/while/body/eval_jaxpr/all_to_all | solution.py:55
  971.6 19.3 %all-to-all-start.7 = ((f32[125,128,8]{0,2,1:T(8,128)}), f32[125,128,8]{0,2,1:T(8,128)}, u32[]{:S(2)}, u32[]{:S(2)}) async-start(f32[125,128,8]{0,2,1:T(8,128)} %select_bitcast_fusion.46), calls=%async_computation.7 | async-start | bytes 1048576 | tf_op jit(solution)/shard_map/while/body/eval_jaxpr/all_to_all | solution.py:55
  (140 other events, 992.9 us)

commit v2 on v1

v2 whole, which is shorter than its diff:
```python
import numpy as np
import jax
import jax.numpy as jnp
from jax import lax
from jax.sharding import PartitionSpec as P

VARIABLES = 5
DEGREE = 4
NODES = 125
FACE_NODES = 25
TRACE_ROWS = 125
LEVELS = 4
COARSE_STEPS = 3
FACES = 6


COURANT = 0.6
HIGHEST = lax.Precision.HIGHEST


def face_node_table():
    cube = np.arange(NODES).reshape(DEGREE + 1, DEGREE + 1, DEGREE + 1)
    faces = [cube[0], cube[-1], cube[:, 0], cube[:, -1], cube[:, :, 0], cube[:, :, -1]]
    return np.stack([face.reshape(FACE_NODES) for face in faces]).astype(np.int32)


def selection_matrix():
    nodes = jnp.asarray(face_node_table())
    row_v = lax.broadcasted_iota(jnp.int32, (VARIABLES * NODES, FACES, VARIABLES, FACE_NODES), 0) // NODES
    row_n = lax.broadcasted_iota(jnp.int32, (VARIABLES * NODES, FACES, VARIABLES, FACE_NODES), 0) % NODES
    col_v = lax.broadcasted_iota(jnp.int32, (VARIABLES * NODES, FACES, VARIABLES, FACE_NODES), 2)
    hit = (row_v == col_v) & (row_n == nodes[None, :, None, :])
    return hit.astype(jnp.float32).reshape(VARIABLES * NODES, FACES * TRACE_ROWS)


def lowest_level(substep):
    for candidate in range(LEVELS):
        if substep % 2 ** (LEVELS - 1 - candidate) == 0:
            return candidate
    return LEVELS - 1


def body(
    solution,
    level_map,
    send_list,
    face_partner,
    volume_block,
    lift_block,
    flux_mixing,
    metric_scale,
):
    local_count = solution.shape[2]
    peers = lax.axis_size(("wall", "span"))
    slot_count = send_list.shape[1] // peers
    own_faces = FACES * local_count

    def table_row(column):
        return (column % local_count) * FACES + column // local_count

    send_rows = table_row(send_list[0])
    partner = face_partner.T.reshape(-1)
    partner_rows = jnp.where(partner < own_faces, table_row(partner), partner)

    select = selection_matrix()
    lift3 = lift_block.reshape(NODES, FACES, FACE_NODES)
    lift_op = (
        flux_mixing.T[None, :, None, :, None] * lift3.transpose(1, 2, 0)[:, None, :, None, :]
    ).reshape(FACES * TRACE_ROWS, VARIABLES * NODES)
    volume_op = (flux_mixing.T[:, None, :, None] * volume_block.T[None, :, None, :]).reshape(
        VARIABLES * NODES, VARIABLES * NODES
    )

    fields = solution.transpose(2, 0, 1).reshape(local_count, VARIABLES * NODES)
    metric = metric_scale[:, None]
    divisors = jnp.power(2, level_map).astype(jnp.float32)
    substeps = 2 ** (LEVELS - 1)

    def coarse_step(coarse_index, fields):
        element_rates = metric_scale * (1.0 + jnp.sqrt(jnp.mean(fields * fields, axis=1)))
        local_fastest = jnp.max(element_rates)
        step_sizes = None
        for substep in range(substeps):
            lowest = lowest_level(substep)
            traces = jnp.dot(fields, select, precision=HIGHEST)
            table = traces.reshape(own_faces, TRACE_ROWS)
            outgoing = jnp.take(table, send_rows, axis=0)
            if substep == 0:
                rate_column = jnp.full((outgoing.shape[0], 1), local_fastest, jnp.float32)
                outgoing = jnp.concatenate([outgoing, rate_column], axis=1)
            outgoing = outgoing.reshape(peers, slot_count, outgoing.shape[1])
            received = lax.all_to_all(
                outgoing, ("wall", "span"), split_axis=0, concat_axis=0, tiled=True
            ).reshape(peers * slot_count, outgoing.shape[2])
            if substep == 0:
                fastest = jnp.max(received[:, TRACE_ROWS])
                received = received[:, :TRACE_ROWS]
                step_sizes = (COURANT / fastest / divisors)[:, None]
            lookup = jnp.concatenate([table, received], axis=0)
            nearby = jnp.take(lookup, partner_rows, axis=0).reshape(
                local_count, FACES * TRACE_ROWS
            )
            change = metric * (
                jnp.dot(nearby - traces, lift_op, precision=HIGHEST)
                - jnp.dot(fields, volume_op, precision=HIGHEST)
            )
            active = (level_map >= lowest)[:, None]
            fields = fields + jnp.where(active, step_sizes * change, 0.0)
        return fields

    final_fields = lax.fori_loop(0, COARSE_STEPS, coarse_step, fields)
    return final_fields.reshape(local_count, VARIABLES, NODES).transpose(1, 2, 0)


def solution(mesh):
    return jax.shard_map(
        body,
        mesh=mesh,
        in_specs=(
            P(None, None, ("wall", "span")),
            P(("wall", "span")),
            P(("wall", "span"), None),
            P(None, ("wall", "span")),
            P(),
            P(),
            P(),
            P(("wall", "span")),
        ),
        out_specs=P(None, None, ("wall", "span")),
        check_vma=False,
    )
```

time: 1010 us -> 1410 us (1.40)
  matrix products: 141 us -> 351 us
  local copies, waits for them, and re-layouts: 356 us -> 495 us
  other arithmetic: 93.1 us -> 203 us
  waiting for transfers between devices: 276 us -> 182 us
  starting transfers between devices: 131 us -> 157 us
    dot_general x72, matrix products: 141 us -> 351 us  [the longest x24 123 us: coarse_step(): jnp.dot(nearby - traces, lift_op, precision=HIGHEST)]
    reshape x52 -> x79, local copies, waits for them, and re-layouts: 50.1 us -> 175 us  [the longest x48 107 us: coarse_step(): jnp.take(lookup, partner_rows, axis=0)]
    all_to_all x24, waiting for transfers between devices: 276 us -> 182 us  [coarse_step(): lax.all_to_all(outgoing, ('wall', 'span'), split_axis=0, concat_axis=0, t...]
    gather x48, local copies, waits for them, and re-layouts: 151 us -> 232 us  [the longest x24 116 us: coarse_step(): jnp.take(lookup, partner_rows, axis=0)]
    dot_general x0 -> x24, local copies, waits for them, and re-layouts: none -> 49.1 us  [coarse_step(): traces = jnp.dot(fields, select, precision=HIGHEST)]
    select_n x30 -> x31, other arithmetic: 17.2 us -> 57.4 us  [the longest x27 56.2 us: coarse_step(): jnp.take(lookup, partner_rows, axis=0)]
    sub x48 -> x0, local copies, waits for them, and re-layouts: 35 us -> none  [tendency(): face_jumps = nearby - own_trace]
    concatenate x24, other arithmetic: 24 us -> 56 us  [coarse_step(): lookup = jnp.concatenate([table, received], axis=0)]
  transfers between devices with their start and end apart: 24 -> 24, of which waited for: 24 -> 21; matrix products, arithmetic and copies ran while one was open for 5% -> 11% of each run, Pallas kernels for 0% -> 0%
where the time goes in v2:
time: 1410 us; the launch traced here: 1390 us
  local copies, waits for them, and re-layouts  495 us (35%)
  matrix products  351 us (25%)
  other arithmetic  203 us (14%)
  waiting for transfers between devices  182 us (13%)
  starting transfers between devices  157 us (11%)
    all_to_all x24, waiting for transfers between devices, coarse_step(): lax.all_to_all(outgoing, ('wall', 'span'), split_axis=0, concat_axis=0, t...  182 us
    all_to_all x24, starting transfers between devices, coarse_step(): lax.all_to_all(outgoing, ('wall', 'span'), split_axis=0, concat_axis=0, t...  157 us
    dot_general x24, matrix products, coarse_step(): jnp.dot(nearby - traces, lift_op, precision=HIGHEST)  123 us
    gather x24, local copies, waits for them, and re-layouts, coarse_step(): jnp.take(lookup, partner_rows, axis=0)  116 us
    gather x24, local copies, waits for them, and re-layouts, coarse_step(): outgoing = jnp.take(table, send_rows, axis=0)  116 us
    dot_general x24, matrix products, coarse_step(): jnp.dot(fields, volume_op, precision=HIGHEST)  115 us
    dot_general x24, matrix products, coarse_step(): traces = jnp.dot(fields, select, precision=HIGHEST)  114 us
    reshape x48, local copies, waits for them, and re-layouts, coarse_step(): jnp.take(lookup, partner_rows, axis=0)  107 us
  transfers between devices with their start and end apart: 24, of which 21 were waited for; matrix products, arithmetic and copies ran while one was open for 11% of the time, Pallas kernels for 0%

profile of v2, /device:TPU:1, one launch (start us, length us, event | category | flops | bytes accessed | tf_op | source)
XLA Modules:
  0.0 1393.8 jit_solution(4657120132624051815)
XLA Ops:
  14.8 1376.8 %while.12 = (s32[]{:T(128)}, f32[256,625]{0,1:T(8,128)}, s32[256]{0:T(256)}, s32[1024]{0:T(1024)}, f32[256]{0:T(256)S(1)}, /*index=5*/f32[256]{0:T(256)}, f32[25...) while((s32[]{:T(128)}, f32[256,625]{0,1:T(8,128)}, ...), condition=%wide.region_4.7_spmd.clone.clone, body=%wide.region_0.6_spmd.clone.clone.sunk | while | flops 32676757504 | bytes 241549328 | solution.py:111
  28.1 12.0 all-to-all-start
  100.0 11.0 all-to-all-start.1
  171.7 8.6 all-to-all-done.2
  227.7 8.7 all-to-all-done.3
  284.2 8.7 all-to-all-done.4
  340.3 8.7 all-to-all-done.5
  396.5 8.7 all-to-all-done.6
  452.9 8.7 all-to-all-done.7
  556.4 10.9 all-to-all-start.1
  572.1 8.4 all-to-all-done.1
  628.1 8.6 all-to-all-done.2
  684.1 8.7 all-to-all-done.3
  740.5 8.7 all-to-all-done.4
  796.7 8.7 all-to-all-done.5
  852.9 8.7 all-to-all-done.6
  909.3 8.7 all-to-all-done.7
  1012.7 11.0 all-to-all-start.1
  1084.5 8.6 all-to-all-done.2
  1140.5 8.7 all-to-all-done.3
  1196.9 8.7 all-to-all-done.4
  1253.1 8.7 all-to-all-done.5
  1309.2 8.7 all-to-all-done.6
  1365.7 8.7 all-to-all-done.7
  (487 shorter events, 1178.9 us)
Async XLA Ops:
  28.1 31.2 %all-to-all-start = ((f32[128,8,126]{2,1,0:T(8,128)}), f32[128,8,126]{2,1,0:T(8,128)}, u32[]{:S(2)}, u32[]{:S(2)}) async-start(f32[128,8,126]{2,1,0:T(8,128)} %pad_bitcast_fusion.2), calls=%async_computation | async-start | bytes 1048576 | tf_op jit(solution)/shard_map/while/body/eval_jaxpr/all_to_all | solution.py:92
  100.0 24.2 %all-to-all-start.1 = ((f32[128,8,125]{2,1,0:T(8,128)}), f32[128,8,125]{2,1,0:T(8,128)}, u32[]{:S(2)}, u32[]{:S(2)}) async-start(f32[128,8,125]{2,1,0:T(8,128)} %select_bitcast_fusion.14), calls=%async_computation.1 | async-start | bytes 1048576 | tf_op jit(solution)/shard_map/while/body/eval_jaxpr/all_to_all | solution.py:92
  161.3 19.0 %all-to-all-start.2 = ((f32[128,8,125]{2,1,0:T(8,128)}), f32[128,8,125]{2,1,0:T(8,128)}, u32[]{:S(2)}, u32[]{:S(2)}) async-start(f32[128,8,125]{2,1,0:T(8,128)} %select_bitcast_fusion.15), calls=%async_computation.2 | async-start | bytes 1048576 | tf_op jit(solution)/shard_map/while/body/eval_jaxpr/all_to_all | solution.py:92
  217.4 19.0 %all-to-all-start.3 = ((f32[128,8,125]{2,1,0:T(8,128)}), f32[128,8,125]{2,1,0:T(8,128)}, u32[]{:S(2)}, u32[]{:S(2)}) async-start(f32[128,8,125]{2,1,0:T(8,128)} %select_bitcast_fusion.16), calls=%async_computation.3 | async-start | bytes 1048576 | tf_op jit(solution)/shard_map/while/body/eval_jaxpr/all_to_all | solution.py:92
  273.6 19.3 %all-to-all-start.4 = ((f32[128,8,125]{2,1,0:T(8,128)}), f32[128,8,125]{2,1,0:T(8,128)}, u32[]{:S(2)}, u32[]{:S(2)}) async-start(f32[128,8,125]{2,1,0:T(8,128)} %select_bitcast_fusion.17), calls=%async_computation.4 | async-start | bytes 1048576 | tf_op jit(solution)/shard_map/while/body/eval_jaxpr/all_to_all | solution.py:92
  330.0 19.0 %all-to-all-start.5 = ((f32[128,8,125]{2,1,0:T(8,128)}), f32[128,8,125]{2,1,0:T(8,128)}, u32[]{:S(2)}, u32[]{:S(2)}) async-start(f32[128,8,125]{2,1,0:T(8,128)} %select_bitcast_fusion.18), calls=%async_computation.5 | async-start | bytes 1048576 | tf_op jit(solution)/shard_map/while/body/eval_jaxpr/all_to_all | solution.py:92
  386.1 19.1 %all-to-all-start.6 = ((f32[128,8,125]{2,1,0:T(8,128)}), f32[128,8,125]{2,1,0:T(8,128)}, u32[]{:S(2)}, u32[]{:S(2)}) async-start(f32[128,8,125]{2,1,0:T(8,128)} %select_bitcast_fusion.19), calls=%async_computation.6 | async-start | bytes 1048576 | tf_op jit(solution)/shard_map/while/body/eval_jaxpr/all_to_all | solution.py:92
  442.4 19.2 %all-to-all-start.7 = ((f32[128,8,125]{2,1,0:T(8,128)}), f32[128,8,125]{2,1,0:T(8,128)}, u32[]{:S(2)}, u32[]{:S(2)}) async-start(f32[128,8,125]{2,1,0:T(8,128)} %select_bitcast_fusion.20), calls=%async_computation.7 | async-start | bytes 1048576 | tf_op jit(solution)/shard_map/while/body/eval_jaxpr/all_to_all | solution.py:92
  491.3 24.6 %all-to-all-start = ((f32[128,8,126]{2,1,0:T(8,128)}), f32[128,8,126]{2,1,0:T(8,128)}, u32[]{:S(2)}, u32[]{:S(2)}) async-start(f32[128,8,126]{2,1,0:T(8,128)} %pad_bitcast_fusion.2), calls=%async_computation | async-start | bytes 1048576 | tf_op jit(solution)/shard_map/while/body/eval_jaxpr/all_to_all | solution.py:92
  556.4 24.2 %all-to-all-start.1 = ((f32[128,8,125]{2,1,0:T(8,128)}), f32[128,8,125]{2,1,0:T(8,128)}, u32[]{:S(2)}, u32[]{:S(2)}) async-start(f32[128,8,125]{2,1,0:T(8,128)} %select_bitcast_fusion.14), calls=%async_computation.1 | async-start | bytes 1048576 | tf_op jit(solution)/shard_map/while/body/eval_jaxpr/all_to_all | solution.py:92
  617.7 19.0 %all-to-all-start.2 = ((f32[128,8,125]{2,1,0:T(8,128)}), f32[128,8,125]{2,1,0:T(8,128)}, u32[]{:S(2)}, u32[]{:S(2)}) async-start(f32[128,8,125]{2,1,0:T(8,128)} %select_bitcast_fusion.15), calls=%async_computation.2 | async-start | bytes 1048576 | tf_op jit(solution)/shard_map/while/body/eval_jaxpr/all_to_all | solution.py:92
  673.8 19.0 %all-to-all-start.3 = ((f32[128,8,125]{2,1,0:T(8,128)}), f32[128,8,125]{2,1,0:T(8,128)}, u32[]{:S(2)}, u32[]{:S(2)}) async-start(f32[128,8,125]{2,1,0:T(8,128)} %select_bitcast_fusion.16), calls=%async_computation.3 | async-start | bytes 1048576 | tf_op jit(solution)/shard_map/while/body/eval_jaxpr/all_to_all | solution.py:92
  730.0 19.3 %all-to-all-start.4 = ((f32[128,8,125]{2,1,0:T(8,128)}), f32[128,8,125]{2,1,0:T(8,128)}, u32[]{:S(2)}, u32[]{:S(2)}) async-start(f32[128,8,125]{2,1,0:T(8,128)} %select_bitcast_fusion.17), calls=%async_computation.4 | async-start | bytes 1048576 | tf_op jit(solution)/shard_map/while/body/eval_jaxpr/all_to_all | solution.py:92
  786.4 19.0 %all-to-all-start.5 = ((f32[128,8,125]{2,1,0:T(8,128)}), f32[128,8,125]{2,1,0:T(8,128)}, u32[]{:S(2)}, u32[]{:S(2)}) async-start(f32[128,8,125]{2,1,0:T(8,128)} %select_bitcast_fusion.18), calls=%async_computation.5 | async-start | bytes 1048576 | tf_op jit(solution)/shard_map/while/body/eval_jaxpr/all_to_all | solution.py:92
  842.5 19.1 %all-to-all-start.6 = ((f32[128,8,125]{2,1,0:T(8,128)}), f32[128,8,125]{2,1,0:T(8,128)}, u32[]{:S(2)}, u32[]{:S(2)}) async-start(f32[128,8,125]{2,1,0:T(8,128)} %select_bitcast_fusion.19), calls=%async_computation.6 | async-start | bytes 1048576 | tf_op jit(solution)/shard_map/while/body/eval_jaxpr/all_to_all | solution.py:92
  898.8 19.3 %all-to-all-start.7 = ((f32[128,8,125]{2,1,0:T(8,128)}), f32[128,8,125]{2,1,0:T(8,128)}, u32[]{:S(2)}, u32[]{:S(2)}) async-start(f32[128,8,125]{2,1,0:T(8,128)} %select_bitcast_fusion.20), calls=%async_computation.7 | async-start | bytes 1048576 | tf_op jit(solution)/shard_map/while/body/eval_jaxpr/all_to_all | solution.py:92
  947.6 24.6 %all-to-all-start = ((f32[128,8,126]{2,1,0:T(8,128)}), f32[128,8,126]{2,1,0:T(8,128)}, u32[]{:S(2)}, u32[]{:S(2)}) async-start(f32[128,8,126]{2,1,0:T(8,128)} %pad_bitcast_fusion.2), calls=%async_computation | async-start | bytes 1048576 | tf_op jit(solution)/shard_map/while/body/eval_jaxpr/all_to_all | solution.py:92
  1012.7 24.2 %all-to-all-start.1 = ((f32[128,8,125]{2,1,0:T(8,128)}), f32[128,8,125]{2,1,0:T(8,128)}, u32[]{:S(2)}, u32[]{:S(2)}) async-start(f32[128,8,125]{2,1,0:T(8,128)} %select_bitcast_fusion.14), calls=%async_computation.1 | async-start | bytes 1048576 | tf_op jit(solution)/shard_map/while/body/eval_jaxpr/all_to_all | solution.py:92
  1074.0 19.0 %all-to-all-start.2 = ((f32[128,8,125]{2,1,0:T(8,128)}), f32[128,8,125]{2,1,0:T(8,128)}, u32[]{:S(2)}, u32[]{:S(2)}) async-start(f32[128,8,125]{2,1,0:T(8,128)} %select_bitcast_fusion.15), calls=%async_computation.2 | async-start | bytes 1048576 | tf_op jit(solution)/shard_map/while/body/eval_jaxpr/all_to_all | solution.py:92
  1130.2 19.0 %all-to-all-start.3 = ((f32[128,8,125]{2,1,0:T(8,128)}), f32[128,8,125]{2,1,0:T(8,128)}, u32[]{:S(2)}, u32[]{:S(2)}) async-start(f32[128,8,125]{2,1,0:T(8,128)} %select_bitcast_fusion.16), calls=%async_computation.3 | async-start | bytes 1048576 | tf_op jit(solution)/shard_map/while/body/eval_jaxpr/all_to_all | solution.py:92
  1186.3 19.3 %all-to-all-start.4 = ((f32[128,8,125]{2,1,0:T(8,128)}), f32[128,8,125]{2,1,0:T(8,128)}, u32[]{:S(2)}, u32[]{:S(2)}) async-start(f32[128,8,125]{2,1,0:T(8,128)} %select_bitcast_fusion.17), calls=%async_computation.4 | async-start | bytes 1048576 | tf_op jit(solution)/shard_map/while/body/eval_jaxpr/all_to_all | solution.py:92
  1242.8 19.0 %all-to-all-start.5 = ((f32[128,8,125]{2,1,0:T(8,128)}), f32[128,8,125]{2,1,0:T(8,128)}, u32[]{:S(2)}, u32[]{:S(2)}) async-start(f32[128,8,125]{2,1,0:T(8,128)} %select_bitcast_fusion.18), calls=%async_computation.5 | async-start | bytes 1048576 | tf_op jit(solution)/shard_map/while/body/eval_jaxpr/all_to_all | solution.py:92
  1298.9 19.1 %all-to-all-start.6 = ((f32[128,8,125]{2,1,0:T(8,128)}), f32[128,8,125]{2,1,0:T(8,128)}, u32[]{:S(2)}, u32[]{:S(2)}) async-start(f32[128,8,125]{2,1,0:T(8,128)} %select_bitcast_fusion.19), calls=%async_computation.6 | async-start | bytes 1048576 | tf_op jit(solution)/shard_map/while/body/eval_jaxpr/all_to_all | solution.py:92
  1355.2 19.2 %all-to-all-start.7 = ((f32[128,8,125]{2,1,0:T(8,128)}), f32[128,8,125]{2,1,0:T(8,128)}, u32[]{:S(2)}, u32[]{:S(2)}) async-start(f32[128,8,125]{2,1,0:T(8,128)} %select_bitcast_fusion.20), calls=%async_computation.7 | async-start | bytes 1048576 | tf_op jit(solution)/shard_map/while/body/eval_jaxpr/all_to_all | solution.py:92
  (57 other events, 176.6 us)

commit v3 on v1

--- a/solution.py
+++ b/solution.py
@@ -77,6 +77,11 @@
     slot_count = send_list.shape[1] // peers
     send_row = send_list[0]
     pointers = face_partner.reshape(-1)
+    own_columns = 6 * local_count
+    local_pointers = jnp.where(pointers < own_columns, pointers, own_columns)
+    remote_pointers = jnp.where(
+        pointers >= own_columns, pointers - own_columns, peers * slot_count
+    )
     divisors = jnp.power(2, level_map).astype(jnp.float32)
     substeps = 2 ** (LEVELS - 1)
     start_cache = jnp.zeros((TRACE_ROWS, peers, slot_count), jnp.float32)
@@ -99,9 +104,29 @@
                 fastest = jnp.max(received[TRACE_ROWS])
                 received = received[:TRACE_ROWS]
                 step_sizes = COURANT / fastest / divisors
-            lookup = jnp.concatenate([trace_table, received], axis=1)
-            nearby = arrange(jnp.take(lookup, pointers, axis=1), local_count)
-            change = tendency(fields, nearby, volume_block, lift_block, flux_mixing, metric_scale)
+            lift4 = lift_block.reshape(TRACE_ROWS, 6, FACE_NODES)
+            own_table = trace_table.reshape(VARIABLES, FACE_NODES, 6, local_count)
+            local_lookup = jnp.concatenate(
+                [trace_table, jnp.zeros((TRACE_ROWS, 1), jnp.float32)], axis=1
+            )
+            local_near = jnp.take(local_lookup, local_pointers, axis=1).reshape(
+                VARIABLES, FACE_NODES, 6, local_count
+            )
+            before = jnp.einsum(
+                "pfn,vnfe->vpe", lift4, local_near - own_table, precision=lax.Precision.HIGHEST
+            ) - jnp.einsum("pq,vqe->vpe", volume_block, fields, precision=lax.Precision.HIGHEST)
+            remote_lookup = jnp.concatenate(
+                [received, jnp.zeros((TRACE_ROWS, 1), jnp.float32)], axis=1
+            )
+            remote_near = jnp.take(remote_lookup, remote_pointers, axis=1).reshape(
+                VARIABLES, FACE_NODES, 6, local_count
+            )
+            combined = before + jnp.einsum(
+                "pfn,vnfe->vpe", lift4, remote_near, precision=lax.Precision.HIGHEST
+            )
+            change = metric_scale * jnp.einsum(
+                "vw,wpe->vpe", flux_mixing, combined, precision=lax.Precision.HIGHEST
+            )
             fields = fields + jnp.where(level_map >= lowest, step_sizes * change, 0.0)
         return (fields, cache)
 

time: 1010 us -> 1150 us (1.14)
  local copies, waits for them, and re-layouts: 356 us -> 470 us
  waiting for transfers between devices: 276 us -> 239 us
  starting transfers between devices: 131 us -> 160 us
  matrix products: 141 us -> 159 us
    gather x24 -> x48, local copies, waits for them, and re-layouts: 72.1 us -> 148 us  [the longest x24 82.2 us: coarse_step(): jnp.take(remote_lookup, remote_pointers, axis=1)]
    all_to_all x24, waiting for transfers between devices: 276 us -> 239 us  [send_slots(): lax.all_to_all(outgoing, ('wall', 'span'), split_axis=1, concat_axis=1, t...]
    reshape x24 -> x51, local copies, waits for them, and re-layouts: 15.6 us -> 52.1 us  [the longest x24 25.4 us: coarse_step(): jnp.take(remote_lookup, remote_pointers, axis=1)]
    sub x48 -> x0, local copies, waits for them, and re-layouts: 35 us -> none  [tendency(): face_jumps = nearby - own_trace]
    select_n x24 -> x48, local copies, waits for them, and re-layouts: 15.2 us -> 44.4 us  [the longest x24 23.8 us: coarse_step(): jnp.take(remote_lookup, remote_pointers, axis=1)]
    all_to_all x24, starting transfers between devices: 131 us -> 160 us  [send_slots(): lax.all_to_all(outgoing, ('wall', 'span'), split_axis=1, concat_axis=1, t...]
    select_n x27 -> x52, other arithmetic: 16.6 us -> 41.1 us  [the longest x27 31.2 us: coarse_step(): jnp.take(remote_lookup, remote_pointers, axis=1)]
    concatenate x0 -> x48, local copies, waits for them, and re-layouts: none -> 24.1 us  [the longest x24 22.8 us: coarse_step(): jnp.concatenate([received, jnp.zeros((TRACE_ROWS, 1), jnp.float32)], axis=1)]
  transfers between devices with their start and end apart: 24 -> 24, of which waited for: 24 -> 24; matrix products, arithmetic and copies ran while one was open for 5% -> 7% of each run, Pallas kernels for 0% -> 0%
where the time goes in v3:
time: 1150 us; the launch traced here: 1140 us
  local copies, waits for them, and re-layouts  470 us (41%)
  waiting for transfers between devices  239 us (21%)
  starting transfers between devices  160 us (14%)
  matrix products  159 us (14%)
  other arithmetic  103 us (9%)
    all_to_all x24, waiting for transfers between devices, send_slots(): lax.all_to_all(outgoing, ('wall', 'span'), split_axis=1, concat_axis=1, t...  239 us
    all_to_all x24, starting transfers between devices, send_slots(): lax.all_to_all(outgoing, ('wall', 'span'), split_axis=1, concat_axis=1, t...  160 us
    gather x24, local copies, waits for them, and re-layouts, coarse_step(): outgoing = jnp.take(trace_table, send_row, axis=1)  85.8 us
    gather x24, local copies, waits for them, and re-layouts, coarse_step(): jnp.take(remote_lookup, remote_pointers, axis=1)  82.2 us
    dot_general x24, matrix products, coarse_step(): jnp.einsum('vw,wpe->vpe', flux_mixing, combined, precision=lax.Precision....  80.2 us
    gather x24, local copies, waits for them, and re-layouts, coarse_step(): jnp.take(local_lookup, local_pointers, axis=1)  65.5 us
    while x444, local copies, waits for them, and re-layouts  41.9 us
    select_n x27, other arithmetic, coarse_step(): jnp.take(remote_lookup, remote_pointers, axis=1)  31.2 us
  transfers between devices with their start and end apart: 24, of which 24 were waited for; matrix products, arithmetic and copies ran while one was open for 7% of the time, Pallas kernels for 0%

profile of v3, /device:TPU:1, one launch (start us, length us, event | category | flops | bytes accessed | tf_op | source)
XLA Modules:
  0.0 1140.5 jit_solution(4798749355574199301)
XLA Ops:
  4.5 1133.5 %while.10 = (s32[]{:T(128)}, f32[5,125,256]{2,0,1:T(8,128)}, s32[256]{0:T(256)S(1)}, s32[1024]{0:T(1024)S(1)}, f32[256]{0:T(256)S(1)}, /*index=5*/f32[256]{0:T(2...) while((s32[]{:T(128)}, f32[5,125,256]{2,0,1:T(8,128)}, ...), condition=%wide.region_4.8_spmd, body=%wide.region_0.7_spmd.sunk | while | flops 6618477568 | bytes 389032704 | solution.py:133
  15.7 12.0 %all-to-all-start = ((f32[126,128,8]{0,2,1:T(8,128)}), f32[126,128,8]{0,2,1:T(8,128)S(1)}, u32[]{:S(2)}, u32[]{:S(2)}) async-start(f32[126,128,8]{0,2,1:T(8,128)} %pad_bitcast_fusion.2), calls=%async_computation | async-start | bytes 1048576 | tf_op jit(solution)/shard_map/while/body/eval_jaxpr/all_to_all | solution.py:55
  74.3 11.0 all-to-all-start.1
  87.2 11.3 all-to-all-done.1
  132.0 11.4 all-to-all-done.2
  180.4 11.4 all-to-all-done.3
  224.2 11.4 all-to-all-done.4
  269.1 11.4 all-to-all-done.5
  316.9 11.4 all-to-all-done.6
  360.5 11.4 all-to-all-done.7
  462.1 11.3 all-to-all-done.1
  507.2 11.4 all-to-all-done.2
  555.5 11.4 all-to-all-done.3
  599.1 11.4 all-to-all-done.4
  644.2 11.4 all-to-all-done.5
  692.0 11.4 all-to-all-done.6
  735.5 11.4 all-to-all-done.7
  837.2 11.3 all-to-all-done.1
  882.1 11.4 all-to-all-done.2
  930.7 11.4 all-to-all-done.3
  974.2 11.4 all-to-all-done.4
  1019.2 11.4 all-to-all-done.5
  1067.1 11.4 all-to-all-done.6
  1110.6 11.4 all-to-all-done.7
  (1179 shorter events, 868.3 us)
Async XLA Ops:
  15.7 25.6 %all-to-all-start = ((f32[126,128,8]{0,2,1:T(8,128)}), f32[126,128,8]{0,2,1:T(8,128)S(1)}, u32[]{:S(2)}, u32[]{:S(2)}) async-start(f32[126,128,8]{0,2,1:T(8,128)} %pad_bitcast_fusion.2), calls=%async_computation | async-start | bytes 1048576 | tf_op jit(solution)/shard_map/while/body/eval_jaxpr/all_to_all | solution.py:55
  74.3 24.2 %all-to-all-start.1 = ((f32[125,128,8]{0,2,1:T(8,128)}), f32[125,128,8]{0,2,1:T(8,128)}, u32[]{:S(2)}, u32[]{:S(2)}) async-start(f32[125,128,8]{0,2,1:T(8,128)} %select_bitcast_fusion.51), calls=%async_computation.1 | async-start | bytes 1048576 | tf_op jit(solution)/shard_map/while/body/eval_jaxpr/all_to_all | solution.py:55
  124.2 19.2 %all-to-all-start.2 = ((f32[125,128,8]{0,2,1:T(8,128)}), f32[125,128,8]{0,2,1:T(8,128)}, u32[]{:S(2)}, u32[]{:S(2)}) async-start(f32[125,128,8]{0,2,1:T(8,128)} %select_bitcast_fusion.54), calls=%async_computation.2 | async-start | bytes 1048576 | tf_op jit(solution)/shard_map/while/body/eval_jaxpr/all_to_all | solution.py:55
  172.6 19.2 %all-to-all-start.3 = ((f32[125,128,8]{0,2,1:T(8,128)}), f32[125,128,8]{0,2,1:T(8,128)}, u32[]{:S(2)}, u32[]{:S(2)}) async-start(f32[125,128,8]{0,2,1:T(8,128)} %select_bitcast_fusion.57), calls=%async_computation.3 | async-start | bytes 1048576 | tf_op jit(solution)/shard_map/while/body/eval_jaxpr/all_to_all | solution.py:55
  216.2 19.4 %all-to-all-start.4 = ((f32[125,128,8]{0,2,1:T(8,128)}), f32[125,128,8]{0,2,1:T(8,128)}, u32[]{:S(2)}, u32[]{:S(2)}) async-start(f32[125,128,8]{0,2,1:T(8,128)} %select_bitcast_fusion.60), calls=%async_computation.4 | async-start | bytes 1048576 | tf_op jit(solution)/shard_map/while/body/eval_jaxpr/all_to_all | solution.py:55
  261.3 19.2 %all-to-all-start.5 = ((f32[125,128,8]{0,2,1:T(8,128)}), f32[125,128,8]{0,2,1:T(8,128)}, u32[]{:S(2)}, u32[]{:S(2)}) async-start(f32[125,128,8]{0,2,1:T(8,128)} %select_bitcast_fusion.63), calls=%async_computation.5 | async-start | bytes 1048576 | tf_op jit(solution)/shard_map/while/body/eval_jaxpr/all_to_all | solution.py:55
  309.0 19.2 %all-to-all-start.6 = ((f32[125,128,8]{0,2,1:T(8,128)}), f32[125,128,8]{0,2,1:T(8,128)}, u32[]{:S(2)}, u32[]{:S(2)}) async-start(f32[125,128,8]{0,2,1:T(8,128)} %select_bitcast_fusion.66), calls=%async_computation.6 | async-start | bytes 1048576 | tf_op jit(solution)/shard_map/while/body/eval_jaxpr/all_to_all | solution.py:55
  352.6 19.2 %all-to-all-start.7 = ((f32[125,128,8]{0,2,1:T(8,128)}), f32[125,128,8]{0,2,1:T(8,128)}, u32[]{:S(2)}, u32[]{:S(2)}) async-start(f32[125,128,8]{0,2,1:T(8,128)} %select_bitcast_fusion.69), calls=%async_computation.7 | async-start | bytes 1048576 | tf_op jit(solution)/shard_map/while/body/eval_jaxpr/all_to_all | solution.py:55
  398.3 18.4 %all-to-all-start = ((f32[126,128,8]{0,2,1:T(8,128)}), f32[126,128,8]{0,2,1:T(8,128)S(1)}, u32[]{:S(2)}, u32[]{:S(2)}) async-start(f32[126,128,8]{0,2,1:T(8,128)} %pad_bitcast_fusion.2), calls=%async_computation | async-start | bytes 1048576 | tf_op jit(solution)/shard_map/while/body/eval_jaxpr/all_to_all | solution.py:55
  449.6 23.8 %all-to-all-start.1 = ((f32[125,128,8]{0,2,1:T(8,128)}), f32[125,128,8]{0,2,1:T(8,128)}, u32[]{:S(2)}, u32[]{:S(2)}) async-start(f32[125,128,8]{0,2,1:T(8,128)} %select_bitcast_fusion.51), calls=%async_computation.1 | async-start | bytes 1048576 | tf_op jit(solution)/shard_map/while/body/eval_jaxpr/all_to_all | solution.py:55
  499.2 19.4 %all-to-all-start.2 = ((f32[125,128,8]{0,2,1:T(8,128)}), f32[125,128,8]{0,2,1:T(8,128)}, u32[]{:S(2)}, u32[]{:S(2)}) async-start(f32[125,128,8]{0,2,1:T(8,128)} %select_bitcast_fusion.54), calls=%async_computation.2 | async-start | bytes 1048576 | tf_op jit(solution)/shard_map/while/body/eval_jaxpr/all_to_all | solution.py:55
  547.7 19.2 %all-to-all-start.3 = ((f32[125,128,8]{0,2,1:T(8,128)}), f32[125,128,8]{0,2,1:T(8,128)}, u32[]{:S(2)}, u32[]{:S(2)}) async-start(f32[125,128,8]{0,2,1:T(8,128)} %select_bitcast_fusion.57), calls=%async_computation.3 | async-start | bytes 1048576 | tf_op jit(solution)/shard_map/while/body/eval_jaxpr/all_to_all | solution.py:55
  591.3 19.2 %all-to-all-start.4 = ((f32[125,128,8]{0,2,1:T(8,128)}), f32[125,128,8]{0,2,1:T(8,128)}, u32[]{:S(2)}, u32[]{:S(2)}) async-start(f32[125,128,8]{0,2,1:T(8,128)} %select_bitcast_fusion.60), calls=%async_computation.4 | async-start | bytes 1048576 | tf_op jit(solution)/shard_map/while/body/eval_jaxpr/all_to_all | solution.py:55
  636.2 19.4 %all-to-all-start.5 = ((f32[125,128,8]{0,2,1:T(8,128)}), f32[125,128,8]{0,2,1:T(8,128)}, u32[]{:S(2)}, u32[]{:S(2)}) async-start(f32[125,128,8]{0,2,1:T(8,128)} %select_bitcast_fusion.63), calls=%async_computation.5 | async-start | bytes 1048576 | tf_op jit(solution)/shard_map/while/body/eval_jaxpr/all_to_all | solution.py:55
  684.2 19.2 %all-to-all-start.6 = ((f32[125,128,8]{0,2,1:T(8,128)}), f32[125,128,8]{0,2,1:T(8,128)}, u32[]{:S(2)}, u32[]{:S(2)}) async-start(f32[125,128,8]{0,2,1:T(8,128)} %select_bitcast_fusion.66), calls=%async_computation.6 | async-start | bytes 1048576 | tf_op jit(solution)/shard_map/while/body/eval_jaxpr/all_to_all | solution.py:55
  727.7 19.2 %all-to-all-start.7 = ((f32[125,128,8]{0,2,1:T(8,128)}), f32[125,128,8]{0,2,1:T(8,128)}, u32[]{:S(2)}, u32[]{:S(2)}) async-start(f32[125,128,8]{0,2,1:T(8,128)} %select_bitcast_fusion.69), calls=%async_computation.7 | async-start | bytes 1048576 | tf_op jit(solution)/shard_map/while/body/eval_jaxpr/all_to_all | solution.py:55
  773.1 18.7 %all-to-all-start = ((f32[126,128,8]{0,2,1:T(8,128)}), f32[126,128,8]{0,2,1:T(8,128)S(1)}, u32[]{:S(2)}, u32[]{:S(2)}) async-start(f32[126,128,8]{0,2,1:T(8,128)} %pad_bitcast_fusion.2), calls=%async_computation | async-start | bytes 1048576 | tf_op jit(solution)/shard_map/while/body/eval_jaxpr/all_to_all | solution.py:55
  824.7 23.8 %all-to-all-start.1 = ((f32[125,128,8]{0,2,1:T(8,128)}), f32[125,128,8]{0,2,1:T(8,128)}, u32[]{:S(2)}, u32[]{:S(2)}) async-start(f32[125,128,8]{0,2,1:T(8,128)} %select_bitcast_fusion.51), calls=%async_computation.1 | async-start | bytes 1048576 | tf_op jit(solution)/shard_map/while/body/eval_jaxpr/all_to_all | solution.py:55
  874.3 19.2 %all-to-all-start.2 = ((f32[125,128,8]{0,2,1:T(8,128)}), f32[125,128,8]{0,2,1:T(8,128)}, u32[]{:S(2)}, u32[]{:S(2)}) async-start(f32[125,128,8]{0,2,1:T(8,128)} %select_bitcast_fusion.54), calls=%async_computation.2 | async-start | bytes 1048576 | tf_op jit(solution)/shard_map/while/body/eval_jaxpr/all_to_all | solution.py:55
  922.6 19.4 %all-to-all-start.3 = ((f32[125,128,8]{0,2,1:T(8,128)}), f32[125,128,8]{0,2,1:T(8,128)}, u32[]{:S(2)}, u32[]{:S(2)}) async-start(f32[125,128,8]{0,2,1:T(8,128)} %select_bitcast_fusion.57), calls=%async_computation.3 | async-start | bytes 1048576 | tf_op jit(solution)/shard_map/while/body/eval_jaxpr/all_to_all | solution.py:55
  966.4 19.2 %all-to-all-start.4 = ((f32[125,128,8]{0,2,1:T(8,128)}), f32[125,128,8]{0,2,1:T(8,128)}, u32[]{:S(2)}, u32[]{:S(2)}) async-start(f32[125,128,8]{0,2,1:T(8,128)} %select_bitcast_fusion.60), calls=%async_computation.4 | async-start | bytes 1048576 | tf_op jit(solution)/shard_map/while/body/eval_jaxpr/all_to_all | solution.py:55
  1011.3 19.2 %all-to-all-start.5 = ((f32[125,128,8]{0,2,1:T(8,128)}), f32[125,128,8]{0,2,1:T(8,128)}, u32[]{:S(2)}, u32[]{:S(2)}) async-start(f32[125,128,8]{0,2,1:T(8,128)} %select_bitcast_fusion.63), calls=%async_computation.5 | async-start | bytes 1048576 | tf_op jit(solution)/shard_map/while/body/eval_jaxpr/all_to_all | solution.py:55
  1059.1 19.4 %all-to-all-start.6 = ((f32[125,128,8]{0,2,1:T(8,128)}), f32[125,128,8]{0,2,1:T(8,128)}, u32[]{:S(2)}, u32[]{:S(2)}) async-start(f32[125,128,8]{0,2,1:T(8,128)} %select_bitcast_fusion.66), calls=%async_computation.6 | async-start | bytes 1048576 | tf_op jit(solution)/shard_map/while/body/eval_jaxpr/all_to_all | solution.py:55
  1102.9 19.2 %all-to-all-start.7 = ((f32[125,128,8]{0,2,1:T(8,128)}), f32[125,128,8]{0,2,1:T(8,128)}, u32[]{:S(2)}, u32[]{:S(2)}) async-start(f32[125,128,8]{0,2,1:T(8,128)} %select_bitcast_fusion.69), calls=%async_computation.7 | async-start | bytes 1048576 | tf_op jit(solution)/shard_map/while/body/eval_jaxpr/all_to_all | solution.py:55
  (195 other events, 661.6 us)

commit v4 on v1

--- a/solution.py
+++ b/solution.py
@@ -62,6 +62,22 @@
     return LEVELS - 1
 
 
+def slot_level(slot, slot_count):
+    power = 0
+    while power < LEVELS - 1 and 2 ** (power + 1) * (slot_count - slot) <= slot_count:
+        power = power + 1
+    return max(LEVELS - 1 - power, 0)
+
+
+def changed_slots(substep, slot_count):
+    if substep == 0:
+        return slot_count
+    previous = lowest_level(substep - 1)
+    levels = [slot_level(k, slot_count) for k in range(slot_count)]
+    assert levels == sorted(levels, reverse=True)
+    return sum(1 for level in levels if level >= previous)
+
+
 def body(
     solution,
     level_map,
@@ -86,20 +102,27 @@
         element_rates = metric_scale * (1.0 + jnp.sqrt(jnp.mean(fields * fields, axis=(0, 1))))
         local_fastest = jnp.max(element_rates)
         step_sizes = None
+        received = None
         for substep in range(substeps):
             lowest = lowest_level(substep)
+            fresh = changed_slots(substep, slot_count)
             trace_table = make_table(fields)
-            outgoing = jnp.take(trace_table, send_row, axis=1)
+            send_columns = send_row.reshape(peers, slot_count)[:, :fresh].reshape(-1)
+            outgoing = jnp.take(trace_table, send_columns, axis=1)
             if substep == 0:
                 rate_row = jnp.full((1, outgoing.shape[1]), local_fastest, jnp.float32)
                 outgoing = jnp.concatenate([outgoing, rate_row], axis=0)
-            outgoing = outgoing.reshape(outgoing.shape[0], peers, slot_count)
-            received = send_slots(outgoing).reshape(outgoing.shape[0], peers * slot_count)
+            outgoing = outgoing.reshape(outgoing.shape[0], peers, fresh)
+            arrived = send_slots(outgoing)
             if substep == 0:
-                fastest = jnp.max(received[TRACE_ROWS])
-                received = received[:TRACE_ROWS]
+                fastest = jnp.max(arrived[TRACE_ROWS])
+                arrived = arrived[:TRACE_ROWS]
                 step_sizes = COURANT / fastest / divisors
-            lookup = jnp.concatenate([trace_table, received], axis=1)
+            if fresh < slot_count:
+                arrived = jnp.concatenate([arrived, received[:, :, fresh:]], axis=2)
+            received = arrived
+            received_flat = received.reshape(TRACE_ROWS, peers * slot_count)
+            lookup = jnp.concatenate([trace_table, received_flat], axis=1)
             nearby = arrange(jnp.take(lookup, pointers, axis=1), local_count)
             change = tendency(fields, nearby, volume_block, lift_block, flux_mixing, metric_scale)
             fields = fields + jnp.where(level_map >= lowest, step_sizes * change, 0.0)

time: 1010 us -> 933 us (0.924)
  waiting for transfers between devices: 276 us -> 212 us
  local copies, waits for them, and re-layouts: 356 us -> 340 us
  matrix products: 141 us -> 129 us
    all_to_all x24, waiting for transfers between devices: 276 us -> 212 us  [send_slots(): lax.all_to_all(outgoing, ('wall', 'span'), split_axis=1, concat_axis=1, t...]
    gather x24 -> x27, local copies, waits for them, and re-layouts: 78.5 us -> 45.2 us  [coarse_step(): outgoing = jnp.take(trace_table, send_columns, axis=1)]
    reshape x21, other arithmetic: 30.6 us -> 14.5 us  [the longest x18 11.5 us: coarse_step(): received_flat = received.reshape(TRACE_ROWS, peers * slot_count)]
    select_n x3 -> x30, other arithmetic: 0.6 us -> 15.3 us  [coarse_step(): outgoing = jnp.take(trace_table, send_columns, axis=1)]
    reshape x3 -> x21, local copies, waits for them, and re-layouts: 4.25 us -> 15.7 us  [the longest x9 9.42 us: coarse_step(): outgoing = outgoing.reshape(outgoing.shape[0], peers, fresh)]
    while x336 -> x384, local copies, waits for them, and re-layouts: 43.7 us -> 32.3 us
    concatenate x24 -> x33, other arithmetic: 24 us -> 16.2 us  [the longest x9 10.9 us: coarse_step(): arrived = jnp.concatenate([arrived, received[:, :, fresh:]], axis=2)]
  transfers between devices with their start and end apart: 24 -> 24, of which waited for: 24 -> 24; matrix products, arithmetic and copies ran while one was open for 5% -> 9% of each run, Pallas kernels for 0% -> 0%
where the time goes in v4:
time: 933 us; the launch traced here: 926 us
  local copies, waits for them, and re-layouts  340 us (36%)
  waiting for transfers between devices  212 us (23%)
  starting transfers between devices  136 us (15%)
  matrix products  129 us (14%)
  other arithmetic  98.7 us (11%)
  loops' own time  10.5 us (1%)
    all_to_all x24, waiting for transfers between devices, send_slots(): lax.all_to_all(outgoing, ('wall', 'span'), split_axis=1, concat_axis=1, t...  212 us
    all_to_all x24, starting transfers between devices, send_slots(): lax.all_to_all(outgoing, ('wall', 'span'), split_axis=1, concat_axis=1, t...  136 us
    gather x24, local copies, waits for them, and re-layouts, coarse_step(): nearby = arrange(jnp.take(lookup, pointers, axis=1), local_count)  75.5 us
    dot_general x24, matrix products, tendency(): jnp.einsum('vw,wpe->vpe', flux_mixing, combined, precision=lax.Precision....  45.2 us
    gather x27, local copies, waits for them, and re-layouts, coarse_step(): outgoing = jnp.take(trace_table, send_columns, axis=1)  45.2 us
    dot_general x24, matrix products, tendency(): jnp.einsum('pq,vqe->vpe', volume_block, fields, precision=lax.Precision.H...  41.8 us
    dot_general x24, matrix products, tendency(): jnp.einsum('pj,vje->vpe', lift_block, face_jumps, precision=lax.Precision...  41.7 us
    another operation x24, local copies, waits for them, and re-layouts, face_traces(): jnp.stack([face.reshape(VARIABLES, FACE_NODES, local_count) for face in f...  35.6 us
  transfers between devices with their start and end apart: 24, of which 24 were waited for; matrix products, arithmetic and copies ran while one was open for 9% of the time, Pallas kernels for 0%

profile of v4, /device:TPU:1, one launch (start us, length us, event | category | flops | bytes accessed | tf_op | source)
XLA Modules:
  0.0 925.8 jit_solution(2858921966115668529)
XLA Ops:
  4.3 920.2 %while.10 = (s32[]{:T(128)}, f32[5,125,256]{2,0,1:T(8,128)S(1)}, s32[256]{0:T(256)S(1)}, s32[1024]{0:T(1024)S(1)}, f32[256]{0:T(256)S(1)}, /*index=5*/f32[256]{0...) while((s32[]{:T(128)}, f32[5,125,256]{2,0,1:T(8,128)S(1)}, ...), condition=%wide.region_4.9_spmd, body=%wide.region_0.8_spmd.sunk | while | flops 4314883584 | bytes 332453920 | solution.py:131
  16.8 12.0 %all-to-all-start = ((f32[126,128,8]{0,2,1:T(8,128)}), f32[126,128,8]{0,2,1:T(8,128)}, u32[]{:S(2)}, u32[]{:S(2)}) async-start(f32[126,128,8]{0,2,1:T(8,128)} %pad_bitcast_fusion.2), calls=%async_computation | async-start | bytes 1048576 | tf_op jit(solution)/shard_map/while/body/eval_jaxpr/all_to_all | solution.py:55
  71.0 9.6 %all-to-all-done.1 = f32[125,128,8]{0,2,1:T(8,128)} async-done(((f32[125,128,8]{0,2,1:T(8,128)}), f32[125,128,8]{0,2,1:T(8,128)}, u32[]{:S(2)}, u32[]{:S(2)}) %all-to-all-start.1) | async-done | bytes 512032 | tf_op jit(solution)/shard_map/while/body/eval_jaxpr/all_to_all | solution.py:55
  109.6 8.0 all-to-all-done.2
  143.1 9.9 %all-to-all-done.3 = f32[125,128,6]{0,2,1:T(8,128)} async-done(((f32[125,128,6]{0,2,1:T(8,128)}), f32[125,128,6]{0,2,1:T(8,128)}, u32[]{:S(2)}, u32[]{:S(2)}) %all-to-all-start.3) | async-done | bytes 384032 | tf_op jit(solution)/shard_map/while/body/eval_jaxpr/all_to_all | solution.py:55
  185.6 7.7 all-to-all-done.4
  219.6 10.5 %all-to-all-done.5 = f32[125,128,7]{0,2,1:T(8,128)} async-done(((f32[125,128,7]{0,2,1:T(8,128)}), f32[125,128,7]{0,2,1:T(8,128)}, u32[]{:S(2)}, u32[]{:S(2)}) %all-to-all-start.5) | async-done | bytes 448032 | tf_op jit(solution)/shard_map/while/body/eval_jaxpr/all_to_all | solution.py:55
  259.1 7.9 all-to-all-done.6
  291.3 10.7 %all-to-all-done.7 = f32[125,128,6]{0,2,1:T(8,128)S(1)} async-done(((f32[125,128,6]{0,2,1:T(8,128)}), f32[125,128,6]{0,2,1:T(8,128)S(1)}, u32[]{:S(2)}, u32[]{:S(2)}) %all-to-all-start.7) | async-done | bytes 384032 | tf_op jit(solution)/shard_map/while/body/eval_jaxpr/all_to_all | solution.py:55
  340.0 6.5 all-to-all-done
  375.3 9.6 %all-to-all-done.1 = f32[125,128,8]{0,2,1:T(8,128)} async-done(((f32[125,128,8]{0,2,1:T(8,128)}), f32[125,128,8]{0,2,1:T(8,128)}, u32[]{:S(2)}, u32[]{:S(2)}) %all-to-all-start.1) | async-done | bytes 512032 | tf_op jit(solution)/shard_map/while/body/eval_jaxpr/all_to_all | solution.py:55
  413.6 8.0 all-to-all-done.2
  447.2 9.9 %all-to-all-done.3 = f32[125,128,6]{0,2,1:T(8,128)} async-done(((f32[125,128,6]{0,2,1:T(8,128)}), f32[125,128,6]{0,2,1:T(8,128)}, u32[]{:S(2)}, u32[]{:S(2)}) %all-to-all-start.3) | async-done | bytes 384032 | tf_op jit(solution)/shard_map/while/body/eval_jaxpr/all_to_all | solution.py:55
  489.7 7.7 all-to-all-done.4
  523.7 10.5 %all-to-all-done.5 = f32[125,128,7]{0,2,1:T(8,128)} async-done(((f32[125,128,7]{0,2,1:T(8,128)}), f32[125,128,7]{0,2,1:T(8,128)}, u32[]{:S(2)}, u32[]{:S(2)}) %all-to-all-start.5) | async-done | bytes 448032 | tf_op jit(solution)/shard_map/while/body/eval_jaxpr/all_to_all | solution.py:55
  563.2 7.9 all-to-all-done.6
  595.3 10.7 %all-to-all-done.7 = f32[125,128,6]{0,2,1:T(8,128)S(1)} async-done(((f32[125,128,6]{0,2,1:T(8,128)}), f32[125,128,6]{0,2,1:T(8,128)S(1)}, u32[]{:S(2)}, u32[]{:S(2)}) %all-to-all-start.7) | async-done | bytes 384032 | tf_op jit(solution)/shard_map/while/body/eval_jaxpr/all_to_all | solution.py:55
  679.3 9.6 %all-to-all-done.1 = f32[125,128,8]{0,2,1:T(8,128)} async-done(((f32[125,128,8]{0,2,1:T(8,128)}), f32[125,128,8]{0,2,1:T(8,128)}, u32[]{:S(2)}, u32[]{:S(2)}) %all-to-all-start.1) | async-done | bytes 512032 | tf_op jit(solution)/shard_map/while/body/eval_jaxpr/all_to_all | solution.py:55
  717.6 8.0 all-to-all-done.2
  751.2 9.9 %all-to-all-done.3 = f32[125,128,6]{0,2,1:T(8,128)} async-done(((f32[125,128,6]{0,2,1:T(8,128)}), f32[125,128,6]{0,2,1:T(8,128)}, u32[]{:S(2)}, u32[]{:S(2)}) %all-to-all-start.3) | async-done | bytes 384032 | tf_op jit(solution)/shard_map/while/body/eval_jaxpr/all_to_all | solution.py:55
  793.7 7.7 all-to-all-done.4
  827.7 10.5 %all-to-all-done.5 = f32[125,128,7]{0,2,1:T(8,128)} async-done(((f32[125,128,7]{0,2,1:T(8,128)}), f32[125,128,7]{0,2,1:T(8,128)}, u32[]{:S(2)}, u32[]{:S(2)}) %all-to-all-start.5) | async-done | bytes 448032 | tf_op jit(solution)/shard_map/while/body/eval_jaxpr/all_to_all | solution.py:55
  867.2 7.9 all-to-all-done.6
  899.3 10.7 %all-to-all-done.7 = f32[125,128,6]{0,2,1:T(8,128)S(1)} async-done(((f32[125,128,6]{0,2,1:T(8,128)}), f32[125,128,6]{0,2,1:T(8,128)S(1)}, u32[]{:S(2)}, u32[]{:S(2)}) %all-to-all-start.7) | async-done | bytes 384032 | tf_op jit(solution)/shard_map/while/body/eval_jaxpr/all_to_all | solution.py:55
  (1106 shorter events, 703.4 us)
Async XLA Ops:
  16.8 25.3 %all-to-all-start = ((f32[126,128,8]{0,2,1:T(8,128)}), f32[126,128,8]{0,2,1:T(8,128)}, u32[]{:S(2)}, u32[]{:S(2)}) async-start(f32[126,128,8]{0,2,1:T(8,128)} %pad_bitcast_fusion.2), calls=%async_computation | async-start | bytes 1048576 | tf_op jit(solution)/shard_map/while/body/eval_jaxpr/all_to_all | solution.py:55
  61.4 19.2 %all-to-all-start.1 = ((f32[125,128,8]{0,2,1:T(8,128)}), f32[125,128,8]{0,2,1:T(8,128)}, u32[]{:S(2)}, u32[]{:S(2)}) async-start(f32[125,128,8]{0,2,1:T(8,128)} %select_bitcast_fusion.26), calls=%async_computation.1 | async-start | bytes 1048576 | tf_op jit(solution)/shard_map/while/body/eval_jaxpr/all_to_all | solution.py:55
  101.5 16.1 %all-to-all-start.2 = ((f32[125,128,4]{0,2,1:T(4,128)}), f32[125,128,4]{0,2,1:T(4,128)S(1)}, u32[]{:S(2)}, u32[]{:S(2)}) async-start(f32[125,128,4]{0,2,1:T(4,128)} %bitcast.564), calls=%async_computation.2 | async-start | bytes 524288 | tf_op jit(solution)/shard_map/while/body/eval_jaxpr/all_to_all | solution.py:55
  134.1 19.0 %all-to-all-start.3 = ((f32[125,128,6]{0,2,1:T(8,128)}), f32[125,128,6]{0,2,1:T(8,128)}, u32[]{:S(2)}, u32[]{:S(2)}) async-start(f32[125,128,6]{0,2,1:T(8,128)} %reshape.513), calls=%async_computation.3 | async-start | bytes 1048576 | tf_op jit(solution)/shard_map/while/body/eval_jaxpr/all_to_all | solution.py:55
  177.0 16.4 %all-to-all-start.4 = ((f32[125,128,4]{0,2,1:T(4,128)}), f32[125,128,4]{0,2,1:T(4,128)}, u32[]{:S(2)}, u32[]{:S(2)}) async-start(f32[125,128,4]{0,2,1:T(4,128)} %bitcast.586), calls=%async_computation.4 | async-start | bytes 524288 | tf_op jit(solution)/shard_map/while/body/eval_jaxpr/all_to_all | solution.py:55
  211.1 19.0 %all-to-all-start.5 = ((f32[125,128,7]{0,2,1:T(8,128)}), f32[125,128,7]{0,2,1:T(8,128)}, u32[]{:S(2)}, u32[]{:S(2)}) async-start(f32[125,128,7]{0,2,1:T(8,128)} %broadcast_select_fusion.10), calls=%async_computation.5 | async-start | bytes 1048576 | tf_op jit(solution)/shard_map/while/body/eval_jaxpr/all_to_all | solution.py:55
  251.1 15.9 %all-to-all-start.6 = ((f32[125,128,4]{0,2,1:T(4,128)}), f32[125,128,4]{0,2,1:T(4,128)S(1)}, u32[]{:S(2)}, u32[]{:S(2)}) async-start(f32[125,128,4]{0,2,1:T(4,128)} %bitcast.609), calls=%async_computation.6 | async-start | bytes 524288 | tf_op jit(solution)/shard_map/while/body/eval_jaxpr/all_to_all | solution.py:55
  283.5 18.4 %all-to-all-start.7 = ((f32[125,128,6]{0,2,1:T(8,128)}), f32[125,128,6]{0,2,1:T(8,128)S(1)}, u32[]{:S(2)}, u32[]{:S(2)}) async-start(f32[125,128,6]{0,2,1:T(8,128)} %reshape.519), calls=%async_computation.7 | async-start | bytes 1048576 | tf_op jit(solution)/shard_map/while/body/eval_jaxpr/all_to_all | solution.py:55
  327.7 18.8 %all-to-all-start = ((f32[126,128,8]{0,2,1:T(8,128)}), f32[126,128,8]{0,2,1:T(8,128)}, u32[]{:S(2)}, u32[]{:S(2)}) async-start(f32[126,128,8]{0,2,1:T(8,128)} %pad_bitcast_fusion.2), calls=%async_computation | async-start | bytes 1048576 | tf_op jit(solution)/shard_map/while/body/eval_jaxpr/all_to_all | solution.py:55
  365.8 19.1 %all-to-all-start.1 = ((f32[125,128,8]{0,2,1:T(8,128)}), f32[125,128,8]{0,2,1:T(8,128)}, u32[]{:S(2)}, u32[]{:S(2)}) async-start(f32[125,128,8]{0,2,1:T(8,128)} %select_bitcast_fusion.26), calls=%async_computation.1 | async-start | bytes 1048576 | tf_op jit(solution)/shard_map/while/body/eval_jaxpr/all_to_all | solution.py:55
  405.7 15.9 %all-to-all-start.2 = ((f32[125,128,4]{0,2,1:T(4,128)}), f32[125,128,4]{0,2,1:T(4,128)S(1)}, u32[]{:S(2)}, u32[]{:S(2)}) async-start(f32[125,128,4]{0,2,1:T(4,128)} %bitcast.564), calls=%async_computation.2 | async-start | bytes 524288 | tf_op jit(solution)/shard_map/while/body/eval_jaxpr/all_to_all | solution.py:55
  438.1 19.0 %all-to-all-start.3 = ((f32[125,128,6]{0,2,1:T(8,128)}), f32[125,128,6]{0,2,1:T(8,128)}, u32[]{:S(2)}, u32[]{:S(2)}) async-start(f32[125,128,6]{0,2,1:T(8,128)} %reshape.513), calls=%async_computation.3 | async-start | bytes 1048576 | tf_op jit(solution)/shard_map/while/body/eval_jaxpr/all_to_all | solution.py:55
  481.0 16.4 %all-to-all-start.4 = ((f32[125,128,4]{0,2,1:T(4,128)}), f32[125,128,4]{0,2,1:T(4,128)}, u32[]{:S(2)}, u32[]{:S(2)}) async-start(f32[125,128,4]{0,2,1:T(4,128)} %bitcast.586), calls=%async_computation.4 | async-start | bytes 524288 | tf_op jit(solution)/shard_map/while/body/eval_jaxpr/all_to_all | solution.py:55
  515.1 19.0 %all-to-all-start.5 = ((f32[125,128,7]{0,2,1:T(8,128)}), f32[125,128,7]{0,2,1:T(8,128)}, u32[]{:S(2)}, u32[]{:S(2)}) async-start(f32[125,128,7]{0,2,1:T(8,128)} %broadcast_select_fusion.10), calls=%async_computation.5 | async-start | bytes 1048576 | tf_op jit(solution)/shard_map/while/body/eval_jaxpr/all_to_all | solution.py:55
  555.2 15.9 %all-to-all-start.6 = ((f32[125,128,4]{0,2,1:T(4,128)}), f32[125,128,4]{0,2,1:T(4,128)S(1)}, u32[]{:S(2)}, u32[]{:S(2)}) async-start(f32[125,128,4]{0,2,1:T(4,128)} %bitcast.609), calls=%async_computation.6 | async-start | bytes 524288 | tf_op jit(solution)/shard_map/while/body/eval_jaxpr/all_to_all | solution.py:55
  587.5 18.4 %all-to-all-start.7 = ((f32[125,128,6]{0,2,1:T(8,128)}), f32[125,128,6]{0,2,1:T(8,128)S(1)}, u32[]{:S(2)}, u32[]{:S(2)}) async-start(f32[125,128,6]{0,2,1:T(8,128)} %reshape.519), calls=%async_computation.7 | async-start | bytes 1048576 | tf_op jit(solution)/shard_map/while/body/eval_jaxpr/all_to_all | solution.py:55
  631.7 18.8 %all-to-all-start = ((f32[126,128,8]{0,2,1:T(8,128)}), f32[126,128,8]{0,2,1:T(8,128)}, u32[]{:S(2)}, u32[]{:S(2)}) async-start(f32[126,128,8]{0,2,1:T(8,128)} %pad_bitcast_fusion.2), calls=%async_computation | async-start | bytes 1048576 | tf_op jit(solution)/shard_map/while/body/eval_jaxpr/all_to_all | solution.py:55
  669.8 19.1 %all-to-all-start.1 = ((f32[125,128,8]{0,2,1:T(8,128)}), f32[125,128,8]{0,2,1:T(8,128)}, u32[]{:S(2)}, u32[]{:S(2)}) async-start(f32[125,128,8]{0,2,1:T(8,128)} %select_bitcast_fusion.26), calls=%async_computation.1 | async-start | bytes 1048576 | tf_op jit(solution)/shard_map/while/body/eval_jaxpr/all_to_all | solution.py:55
  709.7 15.9 %all-to-all-start.2 = ((f32[125,128,4]{0,2,1:T(4,128)}), f32[125,128,4]{0,2,1:T(4,128)S(1)}, u32[]{:S(2)}, u32[]{:S(2)}) async-start(f32[125,128,4]{0,2,1:T(4,128)} %bitcast.564), calls=%async_computation.2 | async-start | bytes 524288 | tf_op jit(solution)/shard_map/while/body/eval_jaxpr/all_to_all | solution.py:55
  742.1 19.0 %all-to-all-start.3 = ((f32[125,128,6]{0,2,1:T(8,128)}), f32[125,128,6]{0,2,1:T(8,128)}, u32[]{:S(2)}, u32[]{:S(2)}) async-start(f32[125,128,6]{0,2,1:T(8,128)} %reshape.513), calls=%async_computation.3 | async-start | bytes 1048576 | tf_op jit(solution)/shard_map/while/body/eval_jaxpr/all_to_all | solution.py:55
  785.0 16.4 %all-to-all-start.4 = ((f32[125,128,4]{0,2,1:T(4,128)}), f32[125,128,4]{0,2,1:T(4,128)}, u32[]{:S(2)}, u32[]{:S(2)}) async-start(f32[125,128,4]{0,2,1:T(4,128)} %bitcast.586), calls=%async_computation.4 | async-start | bytes 524288 | tf_op jit(solution)/shard_map/while/body/eval_jaxpr/all_to_all | solution.py:55
  819.2 19.0 %all-to-all-start.5 = ((f32[125,128,7]{0,2,1:T(8,128)}), f32[125,128,7]{0,2,1:T(8,128)}, u32[]{:S(2)}, u32[]{:S(2)}) async-start(f32[125,128,7]{0,2,1:T(8,128)} %broadcast_select_fusion.10), calls=%async_computation.5 | async-start | bytes 1048576 | tf_op jit(solution)/shard_map/while/body/eval_jaxpr/all_to_all | solution.py:55
  859.2 15.9 %all-to-all-start.6 = ((f32[125,128,4]{0,2,1:T(4,128)}), f32[125,128,4]{0,2,1:T(4,128)S(1)}, u32[]{:S(2)}, u32[]{:S(2)}) async-start(f32[125,128,4]{0,2,1:T(4,128)} %bitcast.609), calls=%async_computation.6 | async-start | bytes 524288 | tf_op jit(solution)/shard_map/while/body/eval_jaxpr/all_to_all | solution.py:55
  891.6 18.4 %all-to-all-start.7 = ((f32[125,128,6]{0,2,1:T(8,128)}), f32[125,128,6]{0,2,1:T(8,128)S(1)}, u32[]{:S(2)}, u32[]{:S(2)}) async-start(f32[125,128,6]{0,2,1:T(8,128)} %reshape.519), calls=%async_computation.7 | async-start | bytes 1048576 | tf_op jit(solution)/shard_map/while/body/eval_jaxpr/all_to_all | solution.py:55
  (165 other events, 843.4 us)

commit v5 on v4

--- a/solution.py
+++ b/solution.py
@@ -33,12 +33,12 @@
 def tendency(fields, nearby, volume_block, lift_block, flux_mixing, metric_scale):
     own_trace = face_traces(fields).reshape(VARIABLES, 6 * FACE_NODES, fields.shape[2])
     face_jumps = nearby - own_trace
-    combined = jnp.einsum("pj,vje->vpe", lift_block, face_jumps, precision=lax.Precision.HIGHEST)
+    combined = jnp.einsum("pj,vje->vpe", lift_block, face_jumps, precision=lax.Precision.HIGH)
     combined = combined - jnp.einsum(
-        "pq,vqe->vpe", volume_block, fields, precision=lax.Precision.HIGHEST
+        "pq,vqe->vpe", volume_block, fields, precision=lax.Precision.HIGH
     )
     return metric_scale * jnp.einsum(
-        "vw,wpe->vpe", flux_mixing, combined, precision=lax.Precision.HIGHEST
+        "vw,wpe->vpe", flux_mixing, combined, precision=lax.Precision.HIGH
     )
 
 

time: 933 us -> 913 us (0.979)
  matrix products: 129 us -> 102 us
    dot_general x24, matrix products: 45.2 us -> 32.3 us  [tendency(): jnp.einsum('vw,wpe->vpe', flux_mixing, combined, precision=lax.Precision....]
where the time goes in v5:
time: 913 us; the launch traced here: 905 us
  local copies, waits for them, and re-layouts  340 us (37%)
  waiting for transfers between devices  220 us (24%)
  starting transfers between devices  135 us (15%)
  matrix products  102 us (11%)
  other arithmetic  98.7 us (11%)
  loops' own time  10.4 us (1%)
    all_to_all x24, waiting for transfers between devices, send_slots(): lax.all_to_all(outgoing, ('wall', 'span'), split_axis=1, concat_axis=1, t...  220 us
    all_to_all x24, starting transfers between devices, send_slots(): lax.all_to_all(outgoing, ('wall', 'span'), split_axis=1, concat_axis=1, t...  135 us
    gather x24, local copies, waits for them, and re-layouts, coarse_step(): nearby = arrange(jnp.take(lookup, pointers, axis=1), local_count)  75.5 us
    gather x27, local copies, waits for them, and re-layouts, coarse_step(): outgoing = jnp.take(trace_table, send_columns, axis=1)  45.2 us
    another operation x24, local copies, waits for them, and re-layouts, face_traces(): jnp.stack([face.reshape(VARIABLES, FACE_NODES, local_count) for face in f...  35.6 us
    dot_general x24, matrix products, tendency(): jnp.einsum('pj,vje->vpe', lift_block, face_jumps, precision=lax.Precision...  35.2 us
    dot_general x24, matrix products, tendency(): jnp.einsum('pq,vqe->vpe', volume_block, fields, precision=lax.Precision.H...  34.6 us
    reshape x24, local copies, waits for them, and re-layouts, make_table(): face_traces(fields).transpose(0, 2, 1, 3)  33.6 us
  transfers between devices with their start and end apart: 24, of which 24 were waited for; matrix products, arithmetic and copies ran while one was open for 9% of the time, Pallas kernels for 0%

profile of v5, /device:TPU:1, one launch (start us, length us, event | category | flops | bytes accessed | tf_op | source)
XLA Modules:
  0.0 905.4 jit_solution(14386244670235178938)
XLA Ops:
  4.3 899.8 %while.10 = (s32[]{:T(128)}, f32[5,125,256]{2,0,1:T(8,128)S(1)}, s32[256]{0:T(256)S(1)}, s32[1024]{0:T(1024)S(1)}, f32[256]{0:T(256)S(1)}, /*index=5*/f32[256]{0...) while((s32[]{:T(128)}, f32[5,125,256]{2,0,1:T(8,128)S(1)}, ...), condition=%wide.region_4.9_spmd, body=%wide.region_0.8_spmd.sunk | while | flops 2164483840 | bytes 332453920 | solution.py:131
  16.8 12.0 %all-to-all-start = ((f32[126,128,8]{0,2,1:T(8,128)}), f32[126,128,8]{0,2,1:T(8,128)}, u32[]{:S(2)}, u32[]{:S(2)}) async-start(f32[126,128,8]{0,2,1:T(8,128)} %pad_bitcast_fusion.2), calls=%async_computation | async-start | bytes 1048576 | tf_op jit(solution)/shard_map/while/body/eval_jaxpr/all_to_all | solution.py:55
  69.9 9.9 %all-to-all-done.1 = f32[125,128,8]{0,2,1:T(8,128)} async-done(((f32[125,128,8]{0,2,1:T(8,128)}), f32[125,128,8]{0,2,1:T(8,128)}, u32[]{:S(2)}, u32[]{:S(2)}) %all-to-all-start.1) | async-done | bytes 512032 | tf_op jit(solution)/shard_map/while/body/eval_jaxpr/all_to_all | solution.py:55
  107.3 8.3 all-to-all-done.2
  140.5 10.2 %all-to-all-done.3 = f32[125,128,6]{0,2,1:T(8,128)} async-done(((f32[125,128,6]{0,2,1:T(8,128)}), f32[125,128,6]{0,2,1:T(8,128)}, u32[]{:S(2)}, u32[]{:S(2)}) %all-to-all-start.3) | async-done | bytes 384032 | tf_op jit(solution)/shard_map/while/body/eval_jaxpr/all_to_all | solution.py:55
  182.2 8.0 all-to-all-done.4
  215.3 10.8 %all-to-all-done.5 = f32[125,128,7]{0,2,1:T(8,128)} async-done(((f32[125,128,7]{0,2,1:T(8,128)}), f32[125,128,7]{0,2,1:T(8,128)}, u32[]{:S(2)}, u32[]{:S(2)}) %all-to-all-start.5) | async-done | bytes 448032 | tf_op jit(solution)/shard_map/while/body/eval_jaxpr/all_to_all | solution.py:55
  253.9 8.2 all-to-all-done.6
  285.0 11.1 %all-to-all-done.7 = f32[125,128,6]{0,2,1:T(8,128)S(1)} async-done(((f32[125,128,6]{0,2,1:T(8,128)}), f32[125,128,6]{0,2,1:T(8,128)S(1)}, u32[]{:S(2)}, u32[]{:S(2)}) %all-to-all-start.7) | async-done | bytes 384032 | tf_op jit(solution)/shard_map/while/body/eval_jaxpr/all_to_all | solution.py:55
  367.4 9.9 %all-to-all-done.1 = f32[125,128,8]{0,2,1:T(8,128)} async-done(((f32[125,128,8]{0,2,1:T(8,128)}), f32[125,128,8]{0,2,1:T(8,128)}, u32[]{:S(2)}, u32[]{:S(2)}) %all-to-all-start.1) | async-done | bytes 512032 | tf_op jit(solution)/shard_map/while/body/eval_jaxpr/all_to_all | solution.py:55
  404.7 8.3 all-to-all-done.2
  437.7 10.2 %all-to-all-done.3 = f32[125,128,6]{0,2,1:T(8,128)} async-done(((f32[125,128,6]{0,2,1:T(8,128)}), f32[125,128,6]{0,2,1:T(8,128)}, u32[]{:S(2)}, u32[]{:S(2)}) %all-to-all-start.3) | async-done | bytes 384032 | tf_op jit(solution)/shard_map/while/body/eval_jaxpr/all_to_all | solution.py:55
  479.4 8.0 all-to-all-done.4
  512.5 10.8 %all-to-all-done.5 = f32[125,128,7]{0,2,1:T(8,128)} async-done(((f32[125,128,7]{0,2,1:T(8,128)}), f32[125,128,7]{0,2,1:T(8,128)}, u32[]{:S(2)}, u32[]{:S(2)}) %all-to-all-start.5) | async-done | bytes 448032 | tf_op jit(solution)/shard_map/while/body/eval_jaxpr/all_to_all | solution.py:55
  551.2 8.2 all-to-all-done.6
  582.2 11.1 %all-to-all-done.7 = f32[125,128,6]{0,2,1:T(8,128)S(1)} async-done(((f32[125,128,6]{0,2,1:T(8,128)}), f32[125,128,6]{0,2,1:T(8,128)S(1)}, u32[]{:S(2)}, u32[]{:S(2)}) %all-to-all-start.7) | async-done | bytes 384032 | tf_op jit(solution)/shard_map/while/body/eval_jaxpr/all_to_all | solution.py:55
  630.3 6.8 all-to-all-done
  664.6 9.9 %all-to-all-done.1 = f32[125,128,8]{0,2,1:T(8,128)} async-done(((f32[125,128,8]{0,2,1:T(8,128)}), f32[125,128,8]{0,2,1:T(8,128)}, u32[]{:S(2)}, u32[]{:S(2)}) %all-to-all-start.1) | async-done | bytes 512032 | tf_op jit(solution)/shard_map/while/body/eval_jaxpr/all_to_all | solution.py:55
  701.9 8.3 all-to-all-done.2
  735.0 10.2 %all-to-all-done.3 = f32[125,128,6]{0,2,1:T(8,128)} async-done(((f32[125,128,6]{0,2,1:T(8,128)}), f32[125,128,6]{0,2,1:T(8,128)}, u32[]{:S(2)}, u32[]{:S(2)}) %all-to-all-start.3) | async-done | bytes 384032 | tf_op jit(solution)/shard_map/while/body/eval_jaxpr/all_to_all | solution.py:55
  776.6 8.0 all-to-all-done.4
  809.8 10.8 %all-to-all-done.5 = f32[125,128,7]{0,2,1:T(8,128)} async-done(((f32[125,128,7]{0,2,1:T(8,128)}), f32[125,128,7]{0,2,1:T(8,128)}, u32[]{:S(2)}, u32[]{:S(2)}) %all-to-all-start.5) | async-done | bytes 448032 | tf_op jit(solution)/shard_map/while/body/eval_jaxpr/all_to_all | solution.py:55
  848.4 8.2 all-to-all-done.6
  879.4 11.1 %all-to-all-done.7 = f32[125,128,6]{0,2,1:T(8,128)S(1)} async-done(((f32[125,128,6]{0,2,1:T(8,128)}), f32[125,128,6]{0,2,1:T(8,128)S(1)}, u32[]{:S(2)}, u32[]{:S(2)}) %all-to-all-start.7) | async-done | bytes 384032 | tf_op jit(solution)/shard_map/while/body/eval_jaxpr/all_to_all | solution.py:55
  (1106 shorter events, 676.4 us)
Async XLA Ops:
  16.8 25.3 %all-to-all-start = ((f32[126,128,8]{0,2,1:T(8,128)}), f32[126,128,8]{0,2,1:T(8,128)}, u32[]{:S(2)}, u32[]{:S(2)}) async-start(f32[126,128,8]{0,2,1:T(8,128)} %pad_bitcast_fusion.2), calls=%async_computation | async-start | bytes 1048576 | tf_op jit(solution)/shard_map/while/body/eval_jaxpr/all_to_all | solution.py:55
  60.6 19.2 %all-to-all-start.1 = ((f32[125,128,8]{0,2,1:T(8,128)}), f32[125,128,8]{0,2,1:T(8,128)}, u32[]{:S(2)}, u32[]{:S(2)}) async-start(f32[125,128,8]{0,2,1:T(8,128)} %select_bitcast_fusion.26), calls=%async_computation.1 | async-start | bytes 1048576 | tf_op jit(solution)/shard_map/while/body/eval_jaxpr/all_to_all | solution.py:55
  99.8 15.8 %all-to-all-start.2 = ((f32[125,128,4]{0,2,1:T(4,128)}), f32[125,128,4]{0,2,1:T(4,128)S(1)}, u32[]{:S(2)}, u32[]{:S(2)}) async-start(f32[125,128,4]{0,2,1:T(4,128)} %bitcast.564), calls=%async_computation.2 | async-start | bytes 524288 | tf_op jit(solution)/shard_map/while/body/eval_jaxpr/all_to_all | solution.py:55
  131.3 19.4 %all-to-all-start.3 = ((f32[125,128,6]{0,2,1:T(8,128)}), f32[125,128,6]{0,2,1:T(8,128)}, u32[]{:S(2)}, u32[]{:S(2)}) async-start(f32[125,128,6]{0,2,1:T(8,128)} %reshape.513), calls=%async_computation.3 | async-start | bytes 1048576 | tf_op jit(solution)/shard_map/while/body/eval_jaxpr/all_to_all | solution.py:55
  173.8 16.4 %all-to-all-start.4 = ((f32[125,128,4]{0,2,1:T(4,128)}), f32[125,128,4]{0,2,1:T(4,128)}, u32[]{:S(2)}, u32[]{:S(2)}) async-start(f32[125,128,4]{0,2,1:T(4,128)} %bitcast.586), calls=%async_computation.4 | async-start | bytes 524288 | tf_op jit(solution)/shard_map/while/body/eval_jaxpr/all_to_all | solution.py:55
  207.1 19.0 %all-to-all-start.5 = ((f32[125,128,7]{0,2,1:T(8,128)}), f32[125,128,7]{0,2,1:T(8,128)}, u32[]{:S(2)}, u32[]{:S(2)}) async-start(f32[125,128,7]{0,2,1:T(8,128)} %broadcast_select_fusion.10), calls=%async_computation.5 | async-start | bytes 1048576 | tf_op jit(solution)/shard_map/while/body/eval_jaxpr/all_to_all | solution.py:55
  246.3 15.9 %all-to-all-start.6 = ((f32[125,128,4]{0,2,1:T(4,128)}), f32[125,128,4]{0,2,1:T(4,128)S(1)}, u32[]{:S(2)}, u32[]{:S(2)}) async-start(f32[125,128,4]{0,2,1:T(4,128)} %bitcast.609), calls=%async_computation.6 | async-start | bytes 524288 | tf_op jit(solution)/shard_map/while/body/eval_jaxpr/all_to_all | solution.py:55
  277.8 18.2 %all-to-all-start.7 = ((f32[125,128,6]{0,2,1:T(8,128)}), f32[125,128,6]{0,2,1:T(8,128)S(1)}, u32[]{:S(2)}, u32[]{:S(2)}) async-start(f32[125,128,6]{0,2,1:T(8,128)} %reshape.519), calls=%async_computation.7 | async-start | bytes 1048576 | tf_op jit(solution)/shard_map/while/body/eval_jaxpr/all_to_all | solution.py:55
  321.0 18.8 %all-to-all-start = ((f32[126,128,8]{0,2,1:T(8,128)}), f32[126,128,8]{0,2,1:T(8,128)}, u32[]{:S(2)}, u32[]{:S(2)}) async-start(f32[126,128,8]{0,2,1:T(8,128)} %pad_bitcast_fusion.2), calls=%async_computation | async-start | bytes 1048576 | tf_op jit(solution)/shard_map/while/body/eval_jaxpr/all_to_all | solution.py:55
  358.2 19.1 %all-to-all-start.1 = ((f32[125,128,8]{0,2,1:T(8,128)}), f32[125,128,8]{0,2,1:T(8,128)}, u32[]{:S(2)}, u32[]{:S(2)}) async-start(f32[125,128,8]{0,2,1:T(8,128)} %select_bitcast_fusion.26), calls=%async_computation.1 | async-start | bytes 1048576 | tf_op jit(solution)/shard_map/while/body/eval_jaxpr/all_to_all | solution.py:55
  397.3 15.7 %all-to-all-start.2 = ((f32[125,128,4]{0,2,1:T(4,128)}), f32[125,128,4]{0,2,1:T(4,128)S(1)}, u32[]{:S(2)}, u32[]{:S(2)}) async-start(f32[125,128,4]{0,2,1:T(4,128)} %bitcast.564), calls=%async_computation.2 | async-start | bytes 524288 | tf_op jit(solution)/shard_map/while/body/eval_jaxpr/all_to_all | solution.py:55
  428.7 19.3 %all-to-all-start.3 = ((f32[125,128,6]{0,2,1:T(8,128)}), f32[125,128,6]{0,2,1:T(8,128)}, u32[]{:S(2)}, u32[]{:S(2)}) async-start(f32[125,128,6]{0,2,1:T(8,128)} %reshape.513), calls=%async_computation.3 | async-start | bytes 1048576 | tf_op jit(solution)/shard_map/while/body/eval_jaxpr/all_to_all | solution.py:55
  471.1 16.4 %all-to-all-start.4 = ((f32[125,128,4]{0,2,1:T(4,128)}), f32[125,128,4]{0,2,1:T(4,128)}, u32[]{:S(2)}, u32[]{:S(2)}) async-start(f32[125,128,4]{0,2,1:T(4,128)} %bitcast.586), calls=%async_computation.4 | async-start | bytes 524288 | tf_op jit(solution)/shard_map/while/body/eval_jaxpr/all_to_all | solution.py:55
  504.4 19.0 %all-to-all-start.5 = ((f32[125,128,7]{0,2,1:T(8,128)}), f32[125,128,7]{0,2,1:T(8,128)}, u32[]{:S(2)}, u32[]{:S(2)}) async-start(f32[125,128,7]{0,2,1:T(8,128)} %broadcast_select_fusion.10), calls=%async_computation.5 | async-start | bytes 1048576 | tf_op jit(solution)/shard_map/while/body/eval_jaxpr/all_to_all | solution.py:55
  543.5 15.9 %all-to-all-start.6 = ((f32[125,128,4]{0,2,1:T(4,128)}), f32[125,128,4]{0,2,1:T(4,128)S(1)}, u32[]{:S(2)}, u32[]{:S(2)}) async-start(f32[125,128,4]{0,2,1:T(4,128)} %bitcast.609), calls=%async_computation.6 | async-start | bytes 524288 | tf_op jit(solution)/shard_map/while/body/eval_jaxpr/all_to_all | solution.py:55
  575.0 18.2 %all-to-all-start.7 = ((f32[125,128,6]{0,2,1:T(8,128)}), f32[125,128,6]{0,2,1:T(8,128)S(1)}, u32[]{:S(2)}, u32[]{:S(2)}) async-start(f32[125,128,6]{0,2,1:T(8,128)} %reshape.519), calls=%async_computation.7 | async-start | bytes 1048576 | tf_op jit(solution)/shard_map/while/body/eval_jaxpr/all_to_all | solution.py:55
  618.2 18.8 %all-to-all-start = ((f32[126,128,8]{0,2,1:T(8,128)}), f32[126,128,8]{0,2,1:T(8,128)}, u32[]{:S(2)}, u32[]{:S(2)}) async-start(f32[126,128,8]{0,2,1:T(8,128)} %pad_bitcast_fusion.2), calls=%async_computation | async-start | bytes 1048576 | tf_op jit(solution)/shard_map/while/body/eval_jaxpr/all_to_all | solution.py:55
  655.5 19.1 %all-to-all-start.1 = ((f32[125,128,8]{0,2,1:T(8,128)}), f32[125,128,8]{0,2,1:T(8,128)}, u32[]{:S(2)}, u32[]{:S(2)}) async-start(f32[125,128,8]{0,2,1:T(8,128)} %select_bitcast_fusion.26), calls=%async_computation.1 | async-start | bytes 1048576 | tf_op jit(solution)/shard_map/while/body/eval_jaxpr/all_to_all | solution.py:55
  694.6 15.7 %all-to-all-start.2 = ((f32[125,128,4]{0,2,1:T(4,128)}), f32[125,128,4]{0,2,1:T(4,128)S(1)}, u32[]{:S(2)}, u32[]{:S(2)}) async-start(f32[125,128,4]{0,2,1:T(4,128)} %bitcast.564), calls=%async_computation.2 | async-start | bytes 524288 | tf_op jit(solution)/shard_map/while/body/eval_jaxpr/all_to_all | solution.py:55
  725.9 19.3 %all-to-all-start.3 = ((f32[125,128,6]{0,2,1:T(8,128)}), f32[125,128,6]{0,2,1:T(8,128)}, u32[]{:S(2)}, u32[]{:S(2)}) async-start(f32[125,128,6]{0,2,1:T(8,128)} %reshape.513), calls=%async_computation.3 | async-start | bytes 1048576 | tf_op jit(solution)/shard_map/while/body/eval_jaxpr/all_to_all | solution.py:55
  768.3 16.4 %all-to-all-start.4 = ((f32[125,128,4]{0,2,1:T(4,128)}), f32[125,128,4]{0,2,1:T(4,128)}, u32[]{:S(2)}, u32[]{:S(2)}) async-start(f32[125,128,4]{0,2,1:T(4,128)} %bitcast.586), calls=%async_computation.4 | async-start | bytes 524288 | tf_op jit(solution)/shard_map/while/body/eval_jaxpr/all_to_all | solution.py:55
  801.6 19.0 %all-to-all-start.5 = ((f32[125,128,7]{0,2,1:T(8,128)}), f32[125,128,7]{0,2,1:T(8,128)}, u32[]{:S(2)}, u32[]{:S(2)}) async-start(f32[125,128,7]{0,2,1:T(8,128)} %broadcast_select_fusion.10), calls=%async_computation.5 | async-start | bytes 1048576 | tf_op jit(solution)/shard_map/while/body/eval_jaxpr/all_to_all | solution.py:55
  840.8 15.9 %all-to-all-start.6 = ((f32[125,128,4]{0,2,1:T(4,128)}), f32[125,128,4]{0,2,1:T(4,128)S(1)}, u32[]{:S(2)}, u32[]{:S(2)}) async-start(f32[125,128,4]{0,2,1:T(4,128)} %bitcast.609), calls=%async_computation.6 | async-start | bytes 524288 | tf_op jit(solution)/shard_map/while/body/eval_jaxpr/all_to_all | solution.py:55
  872.3 18.2 %all-to-all-start.7 = ((f32[125,128,6]{0,2,1:T(8,128)}), f32[125,128,6]{0,2,1:T(8,128)S(1)}, u32[]{:S(2)}, u32[]{:S(2)}) async-start(f32[125,128,6]{0,2,1:T(8,128)} %reshape.519), calls=%async_computation.7 | async-start | bytes 1048576 | tf_op jit(solution)/shard_map/while/body/eval_jaxpr/all_to_all | solution.py:55
  (165 other events, 823.1 us)

commit v6 on v5

--- a/solution.py
+++ b/solution.py
@@ -108,7 +108,7 @@
             fresh = changed_slots(substep, slot_count)
             trace_table = make_table(fields)
             send_columns = send_row.reshape(peers, slot_count)[:, :fresh].reshape(-1)
-            outgoing = jnp.take(trace_table, send_columns, axis=1)
+            outgoing = trace_table.at[:, send_columns].get(mode="promise_in_bounds")
             if substep == 0:
                 rate_row = jnp.full((1, outgoing.shape[1]), local_fastest, jnp.float32)
                 outgoing = jnp.concatenate([outgoing, rate_row], axis=0)
@@ -123,7 +123,7 @@
             received = arrived
             received_flat = received.reshape(TRACE_ROWS, peers * slot_count)
             lookup = jnp.concatenate([trace_table, received_flat], axis=1)
-            nearby = arrange(jnp.take(lookup, pointers, axis=1), local_count)
+            nearby = arrange(lookup.at[:, pointers].get(mode="promise_in_bounds"), local_count)
             change = tendency(fields, nearby, volume_block, lift_block, flux_mixing, metric_scale)
             fields = fields + jnp.where(level_map >= lowest, step_sizes * change, 0.0)
         return (fields, cache)

time: 913 us -> 904 us (level)
  other arithmetic: 98.7 us -> 47.9 us
  local copies, waits for them, and re-layouts: 340 us -> 368 us
  waiting for transfers between devices: 220 us -> 233 us
    gather x51 -> x72, local copies, waits for them, and re-layouts: 121 us -> 161 us  [the longest x48 107 us: coarse_step(): lookup.at[:, pointers].get(mode='promise_in_bounds')]
    select_n x57 -> x15, other arithmetic: 37.4 us -> 0.21 us  [the longest x12 0.14 us: coarse_step(): outgoing = trace_table.at[:, send_columns].get(mode='promise_in_bounds')]
    select_n x24 -> x0, local copies, waits for them, and re-layouts: 17.8 us -> none  [coarse_step(): nearby = arrange(jnp.take(lookup, pointers, axis=1), local_count)]
    all_to_all x24, waiting for transfers between devices: 220 us -> 233 us  [send_slots(): lax.all_to_all(outgoing, ('wall', 'span'), split_axis=1, concat_axis=1, t...]
    while x384 -> x318, local copies, waits for them, and re-layouts: 32.3 us -> 32.6 us
  transfers between devices with their start and end apart: 24 -> 24, of which waited for: 24 -> 24; matrix products, arithmetic and copies ran while one was open for 9% -> 7% of each run, Pallas kernels for 0% -> 0%
where the time goes in v6:
time: 904 us; the launch traced here: 896 us
  local copies, waits for them, and re-layouts  368 us (41%)
  waiting for transfers between devices  233 us (26%)
  starting transfers between devices  134 us (15%)
  matrix products  104 us (12%)
  other arithmetic  47.9 us (5%)
  loops' own time  9.62 us (1%)
    all_to_all x24, waiting for transfers between devices, send_slots(): lax.all_to_all(outgoing, ('wall', 'span'), split_axis=1, concat_axis=1, t...  233 us
    all_to_all x24, starting transfers between devices, send_slots(): lax.all_to_all(outgoing, ('wall', 'span'), split_axis=1, concat_axis=1, t...  134 us
    gather x48, local copies, waits for them, and re-layouts, coarse_step(): lookup.at[:, pointers].get(mode='promise_in_bounds')  107 us
    gather x24, local copies, waits for them, and re-layouts, coarse_step(): outgoing = trace_table.at[:, send_columns].get(mode='promise_in_bounds')  54.1 us
    another operation x24, local copies, waits for them, and re-layouts, face_traces(): jnp.stack([face.reshape(VARIABLES, FACE_NODES, local_count) for face in f...  35.6 us
    dot_general x24, matrix products, tendency(): jnp.einsum('pj,vje->vpe', lift_block, face_jumps, precision=lax.Precision...  35.2 us
    dot_general x24, matrix products, tendency(): jnp.einsum('pq,vqe->vpe', volume_block, fields, precision=lax.Precision.H...  34.6 us
    dot_general x24, matrix products, tendency(): jnp.einsum('vw,wpe->vpe', flux_mixing, combined, precision=lax.Precision....  33.9 us
  transfers between devices with their start and end apart: 24, of which 24 were waited for; matrix products, arithmetic and copies ran while one was open for 7% of the time, Pallas kernels for 0%

profile of v6, /device:TPU:1, one launch (start us, length us, event | category | flops | bytes accessed | tf_op | source)
XLA Modules:
  0.0 896.5 jit_solution(9998514716574770866)
XLA Ops:
  4.2 891.0 %while.10 = (s32[]{:T(128)}, f32[5,125,256]{2,0,1:T(8,128)S(1)}, s32[256]{0:T(256)}, s32[1024]{0:T(1024)S(1)}, f32[256]{0:T(256)S(1)}, /*index=5*/f32[256]{0:T(2...) while((s32[]{:T(128)}, f32[5,125,256]{2,0,1:T(8,128)S(1)}, ...), condition=%wide.region_4.5_spmd, body=%wide.region_0.4_spmd.sunk | while | flops 2162167296 | bytes 314046688 | solution.py:131
  16.5 12.0 %all-to-all-start = ((f32[126,128,8]{0,2,1:T(8,128)}), f32[126,128,8]{0,2,1:T(8,128)}, u32[]{:S(2)}, u32[]{:S(2)}) async-start(f32[126,128,8]{0,2,1:T(8,128)} %pad_bitcast_fusion.2), calls=%async_computation | async-start | bytes 1048576 | tf_op jit(solution)/shard_map/while/body/eval_jaxpr/all_to_all | solution.py:55
  31.9 9.9 %all-to-all-done = f32[126,128,8]{0,2,1:T(8,128)} async-done(((f32[126,128,8]{0,2,1:T(8,128)}), f32[126,128,8]{0,2,1:T(8,128)}, u32[]{:S(2)}, u32[]{:S(2)}) %all-to-all-start) | async-done | bytes 516128 | tf_op jit(solution)/shard_map/while/body/eval_jaxpr/all_to_all | solution.py:55
  70.6 10.9 %all-to-all-done.1 = f32[125,128,8]{0,2,1:T(8,128)} async-done(((f32[125,128,8]{0,2,1:T(8,128)}), f32[125,128,8]{0,2,1:T(8,128)}, u32[]{:S(2)}, u32[]{:S(2)}) %all-to-all-start.1) | async-done | bytes 512032 | tf_op jit(solution)/shard_map/while/body/eval_jaxpr/all_to_all | solution.py:55
  106.3 8.3 all-to-all-done.2
  141.3 10.2 %all-to-all-done.3 = f32[125,128,6]{0,2,1:T(8,128)} async-done(((f32[125,128,6]{0,2,1:T(8,128)}), f32[125,128,6]{0,2,1:T(8,128)}, u32[]{:S(2)}, u32[]{:S(2)}) %all-to-all-start.3) | async-done | bytes 384032 | tf_op jit(solution)/shard_map/while/body/eval_jaxpr/all_to_all | solution.py:55
  215.1 10.8 %all-to-all-done.5 = f32[125,128,7]{0,2,1:T(8,128)} async-done(((f32[125,128,7]{0,2,1:T(8,128)}), f32[125,128,7]{0,2,1:T(8,128)}, u32[]{:S(2)}, u32[]{:S(2)}) %all-to-all-start.5) | async-done | bytes 448032 | tf_op jit(solution)/shard_map/while/body/eval_jaxpr/all_to_all | solution.py:55
  250.8 8.2 all-to-all-done.6
  283.6 11.1 %all-to-all-done.7 = f32[125,128,6]{0,2,1:T(8,128)S(1)} async-done(((f32[125,128,6]{0,2,1:T(8,128)}), f32[125,128,6]{0,2,1:T(8,128)S(1)}, u32[]{:S(2)}, u32[]{:S(2)}) %all-to-all-start.7) | async-done | bytes 384032 | tf_op jit(solution)/shard_map/while/body/eval_jaxpr/all_to_all | solution.py:55
  326.6 10.0 %all-to-all-done = f32[126,128,8]{0,2,1:T(8,128)} async-done(((f32[126,128,8]{0,2,1:T(8,128)}), f32[126,128,8]{0,2,1:T(8,128)}, u32[]{:S(2)}, u32[]{:S(2)}) %all-to-all-start) | async-done | bytes 516128 | tf_op jit(solution)/shard_map/while/body/eval_jaxpr/all_to_all | solution.py:55
  365.2 10.9 %all-to-all-done.1 = f32[125,128,8]{0,2,1:T(8,128)} async-done(((f32[125,128,8]{0,2,1:T(8,128)}), f32[125,128,8]{0,2,1:T(8,128)}, u32[]{:S(2)}, u32[]{:S(2)}) %all-to-all-start.1) | async-done | bytes 512032 | tf_op jit(solution)/shard_map/while/body/eval_jaxpr/all_to_all | solution.py:55
  400.8 8.3 all-to-all-done.2
  435.4 10.2 %all-to-all-done.3 = f32[125,128,6]{0,2,1:T(8,128)} async-done(((f32[125,128,6]{0,2,1:T(8,128)}), f32[125,128,6]{0,2,1:T(8,128)}, u32[]{:S(2)}, u32[]{:S(2)}) %all-to-all-start.3) | async-done | bytes 384032 | tf_op jit(solution)/shard_map/while/body/eval_jaxpr/all_to_all | solution.py:55
  474.4 8.0 all-to-all-done.4
  509.6 10.8 %all-to-all-done.5 = f32[125,128,7]{0,2,1:T(8,128)} async-done(((f32[125,128,7]{0,2,1:T(8,128)}), f32[125,128,7]{0,2,1:T(8,128)}, u32[]{:S(2)}, u32[]{:S(2)}) %all-to-all-start.5) | async-done | bytes 448032 | tf_op jit(solution)/shard_map/while/body/eval_jaxpr/all_to_all | solution.py:55
  545.3 8.2 all-to-all-done.6
  578.1 11.1 %all-to-all-done.7 = f32[125,128,6]{0,2,1:T(8,128)S(1)} async-done(((f32[125,128,6]{0,2,1:T(8,128)}), f32[125,128,6]{0,2,1:T(8,128)S(1)}, u32[]{:S(2)}, u32[]{:S(2)}) %all-to-all-start.7) | async-done | bytes 384032 | tf_op jit(solution)/shard_map/while/body/eval_jaxpr/all_to_all | solution.py:55
  620.7 10.0 %all-to-all-done = f32[126,128,8]{0,2,1:T(8,128)} async-done(((f32[126,128,8]{0,2,1:T(8,128)}), f32[126,128,8]{0,2,1:T(8,128)}, u32[]{:S(2)}, u32[]{:S(2)}) %all-to-all-start) | async-done | bytes 516128 | tf_op jit(solution)/shard_map/while/body/eval_jaxpr/all_to_all | solution.py:55
  659.4 10.9 %all-to-all-done.1 = f32[125,128,8]{0,2,1:T(8,128)} async-done(((f32[125,128,8]{0,2,1:T(8,128)}), f32[125,128,8]{0,2,1:T(8,128)}, u32[]{:S(2)}, u32[]{:S(2)}) %all-to-all-start.1) | async-done | bytes 512032 | tf_op jit(solution)/shard_map/while/body/eval_jaxpr/all_to_all | solution.py:55
  695.3 8.3 all-to-all-done.2
  729.8 10.2 %all-to-all-done.3 = f32[125,128,6]{0,2,1:T(8,128)} async-done(((f32[125,128,6]{0,2,1:T(8,128)}), f32[125,128,6]{0,2,1:T(8,128)}, u32[]{:S(2)}, u32[]{:S(2)}) %all-to-all-start.3) | async-done | bytes 384032 | tf_op jit(solution)/shard_map/while/body/eval_jaxpr/all_to_all | solution.py:55
  803.7 10.8 %all-to-all-done.5 = f32[125,128,7]{0,2,1:T(8,128)} async-done(((f32[125,128,7]{0,2,1:T(8,128)}), f32[125,128,7]{0,2,1:T(8,128)}, u32[]{:S(2)}, u32[]{:S(2)}) %all-to-all-start.5) | async-done | bytes 448032 | tf_op jit(solution)/shard_map/while/body/eval_jaxpr/all_to_all | solution.py:55
  839.6 8.2 all-to-all-done.6
  872.4 11.1 %all-to-all-done.7 = f32[125,128,6]{0,2,1:T(8,128)S(1)} async-done(((f32[125,128,6]{0,2,1:T(8,128)}), f32[125,128,6]{0,2,1:T(8,128)S(1)}, u32[]{:S(2)}, u32[]{:S(2)}) %all-to-all-start.7) | async-done | bytes 384032 | tf_op jit(solution)/shard_map/while/body/eval_jaxpr/all_to_all | solution.py:55
  (978 shorter events, 658.0 us)
Async XLA Ops:
  16.5 25.3 %all-to-all-start = ((f32[126,128,8]{0,2,1:T(8,128)}), f32[126,128,8]{0,2,1:T(8,128)}, u32[]{:S(2)}, u32[]{:S(2)}) async-start(f32[126,128,8]{0,2,1:T(8,128)} %pad_bitcast_fusion.2), calls=%async_computation | async-start | bytes 1048576 | tf_op jit(solution)/shard_map/while/body/eval_jaxpr/all_to_all | solution.py:55
  62.3 19.2 %all-to-all-start.1 = ((f32[125,128,8]{0,2,1:T(8,128)}), f32[125,128,8]{0,2,1:T(8,128)}, u32[]{:S(2)}, u32[]{:S(2)}) async-start(f32[125,128,8]{0,2,1:T(8,128)} %bitcast.538), calls=%async_computation.1 | async-start | bytes 1048576 | tf_op jit(solution)/shard_map/while/body/eval_jaxpr/all_to_all | solution.py:55
  98.8 15.8 %all-to-all-start.2 = ((f32[125,128,4]{0,2,1:T(4,128)}), f32[125,128,4]{0,2,1:T(4,128)S(1)}, u32[]{:S(2)}, u32[]{:S(2)}) async-start(f32[125,128,4]{0,2,1:T(4,128)} %bitcast.553), calls=%async_computation.2 | async-start | bytes 524288 | tf_op jit(solution)/shard_map/while/body/eval_jaxpr/all_to_all | solution.py:55
  132.0 19.4 %all-to-all-start.3 = ((f32[125,128,6]{0,2,1:T(8,128)}), f32[125,128,6]{0,2,1:T(8,128)}, u32[]{:S(2)}, u32[]{:S(2)}) async-start(f32[125,128,6]{0,2,1:T(8,128)} %reshape.531), calls=%async_computation.3 | async-start | bytes 1048576 | tf_op jit(solution)/shard_map/while/body/eval_jaxpr/all_to_all | solution.py:55
  171.9 16.3 %all-to-all-start.4 = ((f32[125,128,4]{0,2,1:T(4,128)}), f32[125,128,4]{0,2,1:T(4,128)}, u32[]{:S(2)}, u32[]{:S(2)}) async-start(f32[125,128,4]{0,2,1:T(4,128)} %bitcast.578), calls=%async_computation.4 | async-start | bytes 524288 | tf_op jit(solution)/shard_map/while/body/eval_jaxpr/all_to_all | solution.py:55
  206.9 19.0 %all-to-all-start.5 = ((f32[125,128,7]{0,2,1:T(8,128)}), f32[125,128,7]{0,2,1:T(8,128)}, u32[]{:S(2)}, u32[]{:S(2)}) async-start(f32[125,128,7]{0,2,1:T(8,128)} %reshape.535), calls=%async_computation.5 | async-start | bytes 1048576 | tf_op jit(solution)/shard_map/while/body/eval_jaxpr/all_to_all | solution.py:55
  243.3 15.7 %all-to-all-start.6 = ((f32[125,128,4]{0,2,1:T(4,128)}), f32[125,128,4]{0,2,1:T(4,128)S(1)}, u32[]{:S(2)}, u32[]{:S(2)}) async-start(f32[125,128,4]{0,2,1:T(4,128)} %bitcast.603), calls=%async_computation.6 | async-start | bytes 524288 | tf_op jit(solution)/shard_map/while/body/eval_jaxpr/all_to_all | solution.py:55
  276.5 18.2 %all-to-all-start.7 = ((f32[125,128,6]{0,2,1:T(8,128)}), f32[125,128,6]{0,2,1:T(8,128)S(1)}, u32[]{:S(2)}, u32[]{:S(2)}) async-start(f32[125,128,6]{0,2,1:T(8,128)} %reshape.538), calls=%async_computation.7 | async-start | bytes 1048576 | tf_op jit(solution)/shard_map/while/body/eval_jaxpr/all_to_all | solution.py:55
  317.8 18.8 %all-to-all-start = ((f32[126,128,8]{0,2,1:T(8,128)}), f32[126,128,8]{0,2,1:T(8,128)}, u32[]{:S(2)}, u32[]{:S(2)}) async-start(f32[126,128,8]{0,2,1:T(8,128)} %pad_bitcast_fusion.2), calls=%async_computation | async-start | bytes 1048576 | tf_op jit(solution)/shard_map/while/body/eval_jaxpr/all_to_all | solution.py:55
  357.1 19.0 %all-to-all-start.1 = ((f32[125,128,8]{0,2,1:T(8,128)}), f32[125,128,8]{0,2,1:T(8,128)}, u32[]{:S(2)}, u32[]{:S(2)}) async-start(f32[125,128,8]{0,2,1:T(8,128)} %bitcast.538), calls=%async_computation.1 | async-start | bytes 1048576 | tf_op jit(solution)/shard_map/while/body/eval_jaxpr/all_to_all | solution.py:55
  393.4 15.7 %all-to-all-start.2 = ((f32[125,128,4]{0,2,1:T(4,128)}), f32[125,128,4]{0,2,1:T(4,128)S(1)}, u32[]{:S(2)}, u32[]{:S(2)}) async-start(f32[125,128,4]{0,2,1:T(4,128)} %bitcast.553), calls=%async_computation.2 | async-start | bytes 524288 | tf_op jit(solution)/shard_map/while/body/eval_jaxpr/all_to_all | solution.py:55
  426.5 19.0 %all-to-all-start.3 = ((f32[125,128,6]{0,2,1:T(8,128)}), f32[125,128,6]{0,2,1:T(8,128)}, u32[]{:S(2)}, u32[]{:S(2)}) async-start(f32[125,128,6]{0,2,1:T(8,128)} %reshape.531), calls=%async_computation.3 | async-start | bytes 1048576 | tf_op jit(solution)/shard_map/while/body/eval_jaxpr/all_to_all | solution.py:55
  466.0 16.5 %all-to-all-start.4 = ((f32[125,128,4]{0,2,1:T(4,128)}), f32[125,128,4]{0,2,1:T(4,128)}, u32[]{:S(2)}, u32[]{:S(2)}) async-start(f32[125,128,4]{0,2,1:T(4,128)} %bitcast.578), calls=%async_computation.4 | async-start | bytes 524288 | tf_op jit(solution)/shard_map/while/body/eval_jaxpr/all_to_all | solution.py:55
  501.1 19.3 %all-to-all-start.5 = ((f32[125,128,7]{0,2,1:T(8,128)}), f32[125,128,7]{0,2,1:T(8,128)}, u32[]{:S(2)}, u32[]{:S(2)}) async-start(f32[125,128,7]{0,2,1:T(8,128)} %reshape.535), calls=%async_computation.5 | async-start | bytes 1048576 | tf_op jit(solution)/shard_map/while/body/eval_jaxpr/all_to_all | solution.py:55
  537.9 15.6 %all-to-all-start.6 = ((f32[125,128,4]{0,2,1:T(4,128)}), f32[125,128,4]{0,2,1:T(4,128)S(1)}, u32[]{:S(2)}, u32[]{:S(2)}) async-start(f32[125,128,4]{0,2,1:T(4,128)} %bitcast.603), calls=%async_computation.6 | async-start | bytes 524288 | tf_op jit(solution)/shard_map/while/body/eval_jaxpr/all_to_all | solution.py:55
  570.9 18.2 %all-to-all-start.7 = ((f32[125,128,6]{0,2,1:T(8,128)}), f32[125,128,6]{0,2,1:T(8,128)S(1)}, u32[]{:S(2)}, u32[]{:S(2)}) async-start(f32[125,128,6]{0,2,1:T(8,128)} %reshape.538), calls=%async_computation.7 | async-start | bytes 1048576 | tf_op jit(solution)/shard_map/while/body/eval_jaxpr/all_to_all | solution.py:55
  611.9 18.8 %all-to-all-start = ((f32[126,128,8]{0,2,1:T(8,128)}), f32[126,128,8]{0,2,1:T(8,128)}, u32[]{:S(2)}, u32[]{:S(2)}) async-start(f32[126,128,8]{0,2,1:T(8,128)} %pad_bitcast_fusion.2), calls=%async_computation | async-start | bytes 1048576 | tf_op jit(solution)/shard_map/while/body/eval_jaxpr/all_to_all | solution.py:55
  651.3 19.1 %all-to-all-start.1 = ((f32[125,128,8]{0,2,1:T(8,128)}), f32[125,128,8]{0,2,1:T(8,128)}, u32[]{:S(2)}, u32[]{:S(2)}) async-start(f32[125,128,8]{0,2,1:T(8,128)} %bitcast.538), calls=%async_computation.1 | async-start | bytes 1048576 | tf_op jit(solution)/shard_map/while/body/eval_jaxpr/all_to_all | solution.py:55
  687.7 15.9 %all-to-all-start.2 = ((f32[125,128,4]{0,2,1:T(4,128)}), f32[125,128,4]{0,2,1:T(4,128)S(1)}, u32[]{:S(2)}, u32[]{:S(2)}) async-start(f32[125,128,4]{0,2,1:T(4,128)} %bitcast.553), calls=%async_computation.2 | async-start | bytes 524288 | tf_op jit(solution)/shard_map/while/body/eval_jaxpr/all_to_all | solution.py:55
  721.0 19.0 %all-to-all-start.3 = ((f32[125,128,6]{0,2,1:T(8,128)}), f32[125,128,6]{0,2,1:T(8,128)}, u32[]{:S(2)}, u32[]{:S(2)}) async-start(f32[125,128,6]{0,2,1:T(8,128)} %reshape.531), calls=%async_computation.3 | async-start | bytes 1048576 | tf_op jit(solution)/shard_map/while/body/eval_jaxpr/all_to_all | solution.py:55
  760.4 16.4 %all-to-all-start.4 = ((f32[125,128,4]{0,2,1:T(4,128)}), f32[125,128,4]{0,2,1:T(4,128)}, u32[]{:S(2)}, u32[]{:S(2)}) async-start(f32[125,128,4]{0,2,1:T(4,128)} %bitcast.578), calls=%async_computation.4 | async-start | bytes 524288 | tf_op jit(solution)/shard_map/while/body/eval_jaxpr/all_to_all | solution.py:55
  795.5 19.0 %all-to-all-start.5 = ((f32[125,128,7]{0,2,1:T(8,128)}), f32[125,128,7]{0,2,1:T(8,128)}, u32[]{:S(2)}, u32[]{:S(2)}) async-start(f32[125,128,7]{0,2,1:T(8,128)} %reshape.535), calls=%async_computation.5 | async-start | bytes 1048576 | tf_op jit(solution)/shard_map/while/body/eval_jaxpr/all_to_all | solution.py:55
  831.9 15.9 %all-to-all-start.6 = ((f32[125,128,4]{0,2,1:T(4,128)}), f32[125,128,4]{0,2,1:T(4,128)S(1)}, u32[]{:S(2)}, u32[]{:S(2)}) async-start(f32[125,128,4]{0,2,1:T(4,128)} %bitcast.603), calls=%async_computation.6 | async-start | bytes 524288 | tf_op jit(solution)/shard_map/while/body/eval_jaxpr/all_to_all | solution.py:55
  865.3 18.2 %all-to-all-start.7 = ((f32[125,128,6]{0,2,1:T(8,128)}), f32[125,128,6]{0,2,1:T(8,128)S(1)}, u32[]{:S(2)}, u32[]{:S(2)}) async-start(f32[125,128,6]{0,2,1:T(8,128)} %reshape.538), calls=%async_computation.7 | async-start | bytes 1048576 | tf_op jit(solution)/shard_map/while/body/eval_jaxpr/all_to_all | solution.py:55
  (131 other events, 792.5 us)

commit v7 on v6

--- a/solution.py
+++ b/solution.py
@@ -107,23 +107,27 @@
             lowest = lowest_level(substep)
             fresh = changed_slots(substep, slot_count)
             trace_table = make_table(fields)
+            table_rows = trace_table.T
             send_columns = send_row.reshape(peers, slot_count)[:, :fresh].reshape(-1)
-            outgoing = trace_table.at[:, send_columns].get(mode="promise_in_bounds")
+            outgoing = table_rows.at[send_columns].get(mode="promise_in_bounds")
             if substep == 0:
-                rate_row = jnp.full((1, outgoing.shape[1]), local_fastest, jnp.float32)
-                outgoing = jnp.concatenate([outgoing, rate_row], axis=0)
-            outgoing = outgoing.reshape(outgoing.shape[0], peers, fresh)
-            arrived = send_slots(outgoing)
+                rate_column = jnp.full((outgoing.shape[0], 1), local_fastest, jnp.float32)
+                outgoing = jnp.concatenate([outgoing, rate_column], axis=1)
+            outgoing = outgoing.reshape(peers, fresh, outgoing.shape[1])
+            arrived = lax.all_to_all(
+                outgoing, ("wall", "span"), split_axis=0, concat_axis=0, tiled=True
+            )
             if substep == 0:
-                fastest = jnp.max(arrived[TRACE_ROWS])
-                arrived = arrived[:TRACE_ROWS]
+                fastest = jnp.max(arrived[:, :, TRACE_ROWS])
+                arrived = arrived[:, :, :TRACE_ROWS]
                 step_sizes = COURANT / fastest / divisors
             if fresh < slot_count:
-                arrived = jnp.concatenate([arrived, received[:, :, fresh:]], axis=2)
+                arrived = jnp.concatenate([arrived, received[:, fresh:]], axis=1)
             received = arrived
-            received_flat = received.reshape(TRACE_ROWS, peers * slot_count)
-            lookup = jnp.concatenate([trace_table, received_flat], axis=1)
-            nearby = arrange(lookup.at[:, pointers].get(mode="promise_in_bounds"), local_count)
+            lookup = jnp.concatenate(
+                [table_rows, received.reshape(peers * slot_count, TRACE_ROWS)], axis=0
+            )
+            nearby = arrange(lookup.at[pointers].get(mode="promise_in_bounds").T, local_count)
             change = tendency(fields, nearby, volume_block, lift_block, flux_mixing, metric_scale)
             fields = fields + jnp.where(level_map >= lowest, step_sizes * change, 0.0)
         return (fields, cache)

time: 904 us -> 904 us (level)
    transpose x0 -> x24, local copies, waits for them, and re-layouts: none -> 31.6 us  [coarse_step(): lookup.at[pointers].get(mode='promise_in_bounds')]
    gather x72 -> x48, local copies, waits for them, and re-layouts: 161 us -> 130 us  [the longest x24 75.6 us: coarse_step(): lookup.at[pointers].get(mode='promise_in_bounds')]
where the time goes in v7:
time: 904 us; the launch traced here: 896 us
  local copies, waits for them, and re-layouts  368 us (41%)
  waiting for transfers between devices  233 us (26%)
  starting transfers between devices  134 us (15%)
  matrix products  104 us (12%)
  other arithmetic  47.9 us (5%)
  loops' own time  9.62 us (1%)
    all_to_all x24, waiting for transfers between devices, coarse_step(): lax.all_to_all(outgoing, ('wall', 'span'), split_axis=0, concat_axis=0, t...  233 us
    all_to_all x24, starting transfers between devices, coarse_step(): lax.all_to_all(outgoing, ('wall', 'span'), split_axis=0, concat_axis=0, t...  134 us
    gather x24, local copies, waits for them, and re-layouts, coarse_step(): lookup.at[pointers].get(mode='promise_in_bounds')  75.6 us
    gather x24, local copies, waits for them, and re-layouts, coarse_step(): outgoing = table_rows.at[send_columns].get(mode='promise_in_bounds')  54.1 us
    another operation x24, local copies, waits for them, and re-layouts, face_traces(): jnp.stack([face.reshape(VARIABLES, FACE_NODES, local_count) for face in f...  35.6 us
    dot_general x24, matrix products, tendency(): jnp.einsum('pj,vje->vpe', lift_block, face_jumps, precision=lax.Precision...  35.2 us
    dot_general x24, matrix products, tendency(): jnp.einsum('pq,vqe->vpe', volume_block, fields, precision=lax.Precision.H...  34.6 us
    dot_general x24, matrix products, tendency(): jnp.einsum('vw,wpe->vpe', flux_mixing, combined, precision=lax.Precision....  33.9 us
  transfers between devices with their start and end apart: 24, of which 24 were waited for; matrix products, arithmetic and copies ran while one was open for 7% of the time, Pallas kernels for 0%

profile of v7, /device:TPU:1, one launch (start us, length us, event | category | flops | bytes accessed | tf_op | source)
XLA Modules:
  0.0 896.5 jit_solution(16612226739683889581)
XLA Ops:
  4.2 891.0 %while.10 = (s32[]{:T(128)}, f32[5,125,256]{2,0,1:T(8,128)S(1)}, s32[256]{0:T(256)}, s32[1024]{0:T(1024)S(1)}, f32[256]{0:T(256)S(1)}, /*index=5*/f32[256]{0:T(2...) while((s32[]{:T(128)}, f32[5,125,256]{2,0,1:T(8,128)S(1)}, ...), condition=%wide.region_4.5_spmd, body=%wide.region_0.4_spmd.sunk | while | flops 2162167296 | bytes 314046688 | solution.py:135
  16.5 12.0 %all-to-all-start = ((f32[128,8,126]{2,1,0:T(8,128)}), f32[128,8,126]{2,1,0:T(8,128)}, u32[]{:S(2)}, u32[]{:S(2)}) async-start(f32[128,8,126]{2,1,0:T(8,128)} %pad_bitcast_fusion.2), calls=%async_computation | async-start | bytes 1048576 | tf_op jit(solution)/shard_map/while/body/eval_jaxpr/all_to_all | solution.py:117
  31.9 9.9 %all-to-all-done = f32[128,8,126]{2,1,0:T(8,128)} async-done(((f32[128,8,126]{2,1,0:T(8,128)}), f32[128,8,126]{2,1,0:T(8,128)}, u32[]{:S(2)}, u32[]{:S(2)}) %all-to-all-start) | async-done | bytes 516128 | tf_op jit(solution)/shard_map/while/body/eval_jaxpr/all_to_all | solution.py:117
  70.6 10.9 %all-to-all-done.1 = f32[128,8,125]{2,1,0:T(8,128)} async-done(((f32[128,8,125]{2,1,0:T(8,128)}), f32[128,8,125]{2,1,0:T(8,128)}, u32[]{:S(2)}, u32[]{:S(2)}) %all-to-all-start.1) | async-done | bytes 512032 | tf_op jit(solution)/shard_map/while/body/eval_jaxpr/all_to_all | solution.py:117
  106.3 8.3 all-to-all-done.2
  141.3 10.2 %all-to-all-done.3 = f32[128,6,125]{2,1,0:T(8,128)} async-done(((f32[128,6,125]{2,1,0:T(8,128)}), f32[128,6,125]{2,1,0:T(8,128)}, u32[]{:S(2)}, u32[]{:S(2)}) %all-to-all-start.3) | async-done | bytes 384032 | tf_op jit(solution)/shard_map/while/body/eval_jaxpr/all_to_all | solution.py:117
  215.1 10.8 %all-to-all-done.5 = f32[128,7,125]{2,1,0:T(8,128)} async-done(((f32[128,7,125]{2,1,0:T(8,128)}), f32[128,7,125]{2,1,0:T(8,128)}, u32[]{:S(2)}, u32[]{:S(2)}) %all-to-all-start.5) | async-done | bytes 448032 | tf_op jit(solution)/shard_map/while/body/eval_jaxpr/all_to_all | solution.py:117
  250.9 8.2 all-to-all-done.6
  283.7 11.1 %all-to-all-done.7 = f32[128,6,125]{2,1,0:T(8,128)S(1)} async-done(((f32[128,6,125]{2,1,0:T(8,128)}), f32[128,6,125]{2,1,0:T(8,128)S(1)}, u32[]{:S(2)}, u32[]{:S(2)}) %all-to-all-start.7) | async-done | bytes 384032 | tf_op jit(solution)/shard_map/while/body/eval_jaxpr/all_to_all | solution.py:117
  326.6 10.0 %all-to-all-done = f32[128,8,126]{2,1,0:T(8,128)} async-done(((f32[128,8,126]{2,1,0:T(8,128)}), f32[128,8,126]{2,1,0:T(8,128)}, u32[]{:S(2)}, u32[]{:S(2)}) %all-to-all-start) | async-done | bytes 516128 | tf_op jit(solution)/shard_map/while/body/eval_jaxpr/all_to_all | solution.py:117
  365.2 10.9 %all-to-all-done.1 = f32[128,8,125]{2,1,0:T(8,128)} async-done(((f32[128,8,125]{2,1,0:T(8,128)}), f32[128,8,125]{2,1,0:T(8,128)}, u32[]{:S(2)}, u32[]{:S(2)}) %all-to-all-start.1) | async-done | bytes 512032 | tf_op jit(solution)/shard_map/while/body/eval_jaxpr/all_to_all | solution.py:117
  400.8 8.3 all-to-all-done.2
  435.4 10.2 %all-to-all-done.3 = f32[128,6,125]{2,1,0:T(8,128)} async-done(((f32[128,6,125]{2,1,0:T(8,128)}), f32[128,6,125]{2,1,0:T(8,128)}, u32[]{:S(2)}, u32[]{:S(2)}) %all-to-all-start.3) | async-done | bytes 384032 | tf_op jit(solution)/shard_map/while/body/eval_jaxpr/all_to_all | solution.py:117
  509.6 10.8 %all-to-all-done.5 = f32[128,7,125]{2,1,0:T(8,128)} async-done(((f32[128,7,125]{2,1,0:T(8,128)}), f32[128,7,125]{2,1,0:T(8,128)}, u32[]{:S(2)}, u32[]{:S(2)}) %all-to-all-start.5) | async-done | bytes 448032 | tf_op jit(solution)/shard_map/while/body/eval_jaxpr/all_to_all | solution.py:117
  545.3 8.2 all-to-all-done.6
  578.1 11.1 %all-to-all-done.7 = f32[128,6,125]{2,1,0:T(8,128)S(1)} async-done(((f32[128,6,125]{2,1,0:T(8,128)}), f32[128,6,125]{2,1,0:T(8,128)S(1)}, u32[]{:S(2)}, u32[]{:S(2)}) %all-to-all-start.7) | async-done | bytes 384032 | tf_op jit(solution)/shard_map/while/body/eval_jaxpr/all_to_all | solution.py:117
  620.8 10.0 %all-to-all-done = f32[128,8,126]{2,1,0:T(8,128)} async-done(((f32[128,8,126]{2,1,0:T(8,128)}), f32[128,8,126]{2,1,0:T(8,128)}, u32[]{:S(2)}, u32[]{:S(2)}) %all-to-all-start) | async-done | bytes 516128 | tf_op jit(solution)/shard_map/while/body/eval_jaxpr/all_to_all | solution.py:117
  659.5 10.9 %all-to-all-done.1 = f32[128,8,125]{2,1,0:T(8,128)} async-done(((f32[128,8,125]{2,1,0:T(8,128)}), f32[128,8,125]{2,1,0:T(8,128)}, u32[]{:S(2)}, u32[]{:S(2)}) %all-to-all-start.1) | async-done | bytes 512032 | tf_op jit(solution)/shard_map/while/body/eval_jaxpr/all_to_all | solution.py:117
  695.3 8.3 all-to-all-done.2
  729.8 10.2 %all-to-all-done.3 = f32[128,6,125]{2,1,0:T(8,128)} async-done(((f32[128,6,125]{2,1,0:T(8,128)}), f32[128,6,125]{2,1,0:T(8,128)}, u32[]{:S(2)}, u32[]{:S(2)}) %all-to-all-start.3) | async-done | bytes 384032 | tf_op jit(solution)/shard_map/while/body/eval_jaxpr/all_to_all | solution.py:117
  768.7 8.0 all-to-all-done.4
  803.7 10.8 %all-to-all-done.5 = f32[128,7,125]{2,1,0:T(8,128)} async-done(((f32[128,7,125]{2,1,0:T(8,128)}), f32[128,7,125]{2,1,0:T(8,128)}, u32[]{:S(2)}, u32[]{:S(2)}) %all-to-all-start.5) | async-done | bytes 448032 | tf_op jit(solution)/shard_map/while/body/eval_jaxpr/all_to_all | solution.py:117
  839.7 8.2 all-to-all-done.6
  872.4 11.1 %all-to-all-done.7 = f32[128,6,125]{2,1,0:T(8,128)S(1)} async-done(((f32[128,6,125]{2,1,0:T(8,128)}), f32[128,6,125]{2,1,0:T(8,128)S(1)}, u32[]{:S(2)}, u32[]{:S(2)}) %all-to-all-start.7) | async-done | bytes 384032 | tf_op jit(solution)/shard_map/while/body/eval_jaxpr/all_to_all | solution.py:117
  (978 shorter events, 658.0 us)
Async XLA Ops:
  16.5 25.3 %all-to-all-start = ((f32[128,8,126]{2,1,0:T(8,128)}), f32[128,8,126]{2,1,0:T(8,128)}, u32[]{:S(2)}, u32[]{:S(2)}) async-start(f32[128,8,126]{2,1,0:T(8,128)} %pad_bitcast_fusion.2), calls=%async_computation | async-start | bytes 1048576 | tf_op jit(solution)/shard_map/while/body/eval_jaxpr/all_to_all | solution.py:117
  62.3 19.2 %all-to-all-start.1 = ((f32[128,8,125]{2,1,0:T(8,128)}), f32[128,8,125]{2,1,0:T(8,128)}, u32[]{:S(2)}, u32[]{:S(2)}) async-start(f32[128,8,125]{2,1,0:T(8,128)} %bitcast.533), calls=%async_computation.1 | async-start | bytes 1048576 | tf_op jit(solution)/shard_map/while/body/eval_jaxpr/all_to_all | solution.py:117
  98.8 15.8 %all-to-all-start.2 = ((f32[128,4,125]{2,1,0:T(4,128)}), f32[128,4,125]{2,1,0:T(4,128)S(1)}, u32[]{:S(2)}, u32[]{:S(2)}) async-start(f32[128,4,125]{2,1,0:T(4,128)} %bitcast.549), calls=%async_computation.2 | async-start | bytes 524288 | tf_op jit(solution)/shard_map/while/body/eval_jaxpr/all_to_all | solution.py:117
  132.0 19.4 %all-to-all-start.3 = ((f32[128,6,125]{2,1,0:T(8,128)}), f32[128,6,125]{2,1,0:T(8,128)}, u32[]{:S(2)}, u32[]{:S(2)}) async-start(f32[128,6,125]{2,1,0:T(8,128)} %reshape.531), calls=%async_computation.3 | async-start | bytes 1048576 | tf_op jit(solution)/shard_map/while/body/eval_jaxpr/all_to_all | solution.py:117
  171.9 16.3 %all-to-all-start.4 = ((f32[128,4,125]{2,1,0:T(4,128)}), f32[128,4,125]{2,1,0:T(4,128)}, u32[]{:S(2)}, u32[]{:S(2)}) async-start(f32[128,4,125]{2,1,0:T(4,128)} %bitcast.575), calls=%async_computation.4 | async-start | bytes 524288 | tf_op jit(solution)/shard_map/while/body/eval_jaxpr/all_to_all | solution.py:117
  206.9 19.0 %all-to-all-start.5 = ((f32[128,7,125]{2,1,0:T(8,128)}), f32[128,7,125]{2,1,0:T(8,128)}, u32[]{:S(2)}, u32[]{:S(2)}) async-start(f32[128,7,125]{2,1,0:T(8,128)} %reshape.535), calls=%async_computation.5 | async-start | bytes 1048576 | tf_op jit(solution)/shard_map/while/body/eval_jaxpr/all_to_all | solution.py:117
  243.3 15.7 %all-to-all-start.6 = ((f32[128,4,125]{2,1,0:T(4,128)}), f32[128,4,125]{2,1,0:T(4,128)S(1)}, u32[]{:S(2)}, u32[]{:S(2)}) async-start(f32[128,4,125]{2,1,0:T(4,128)} %bitcast.601), calls=%async_computation.6 | async-start | bytes 524288 | tf_op jit(solution)/shard_map/while/body/eval_jaxpr/all_to_all | solution.py:117
  276.5 18.2 %all-to-all-start.7 = ((f32[128,6,125]{2,1,0:T(8,128)}), f32[128,6,125]{2,1,0:T(8,128)S(1)}, u32[]{:S(2)}, u32[]{:S(2)}) async-start(f32[128,6,125]{2,1,0:T(8,128)} %reshape.538), calls=%async_computation.7 | async-start | bytes 1048576 | tf_op jit(solution)/shard_map/while/body/eval_jaxpr/all_to_all | solution.py:117
  317.8 18.8 %all-to-all-start = ((f32[128,8,126]{2,1,0:T(8,128)}), f32[128,8,126]{2,1,0:T(8,128)}, u32[]{:S(2)}, u32[]{:S(2)}) async-start(f32[128,8,126]{2,1,0:T(8,128)} %pad_bitcast_fusion.2), calls=%async_computation | async-start | bytes 1048576 | tf_op jit(solution)/shard_map/while/body/eval_jaxpr/all_to_all | solution.py:117
  357.1 19.0 %all-to-all-start.1 = ((f32[128,8,125]{2,1,0:T(8,128)}), f32[128,8,125]{2,1,0:T(8,128)}, u32[]{:S(2)}, u32[]{:S(2)}) async-start(f32[128,8,125]{2,1,0:T(8,128)} %bitcast.533), calls=%async_computation.1 | async-start | bytes 1048576 | tf_op jit(solution)/shard_map/while/body/eval_jaxpr/all_to_all | solution.py:117
  393.4 15.7 %all-to-all-start.2 = ((f32[128,4,125]{2,1,0:T(4,128)}), f32[128,4,125]{2,1,0:T(4,128)S(1)}, u32[]{:S(2)}, u32[]{:S(2)}) async-start(f32[128,4,125]{2,1,0:T(4,128)} %bitcast.549), calls=%async_computation.2 | async-start | bytes 524288 | tf_op jit(solution)/shard_map/while/body/eval_jaxpr/all_to_all | solution.py:117
  426.5 19.0 %all-to-all-start.3 = ((f32[128,6,125]{2,1,0:T(8,128)}), f32[128,6,125]{2,1,0:T(8,128)}, u32[]{:S(2)}, u32[]{:S(2)}) async-start(f32[128,6,125]{2,1,0:T(8,128)} %reshape.531), calls=%async_computation.3 | async-start | bytes 1048576 | tf_op jit(solution)/shard_map/while/body/eval_jaxpr/all_to_all | solution.py:117
  466.0 16.5 %all-to-all-start.4 = ((f32[128,4,125]{2,1,0:T(4,128)}), f32[128,4,125]{2,1,0:T(4,128)}, u32[]{:S(2)}, u32[]{:S(2)}) async-start(f32[128,4,125]{2,1,0:T(4,128)} %bitcast.575), calls=%async_computation.4 | async-start | bytes 524288 | tf_op jit(solution)/shard_map/while/body/eval_jaxpr/all_to_all | solution.py:117
  501.1 19.3 %all-to-all-start.5 = ((f32[128,7,125]{2,1,0:T(8,128)}), f32[128,7,125]{2,1,0:T(8,128)}, u32[]{:S(2)}, u32[]{:S(2)}) async-start(f32[128,7,125]{2,1,0:T(8,128)} %reshape.535), calls=%async_computation.5 | async-start | bytes 1048576 | tf_op jit(solution)/shard_map/while/body/eval_jaxpr/all_to_all | solution.py:117
  537.9 15.6 %all-to-all-start.6 = ((f32[128,4,125]{2,1,0:T(4,128)}), f32[128,4,125]{2,1,0:T(4,128)S(1)}, u32[]{:S(2)}, u32[]{:S(2)}) async-start(f32[128,4,125]{2,1,0:T(4,128)} %bitcast.601), calls=%async_computation.6 | async-start | bytes 524288 | tf_op jit(solution)/shard_map/while/body/eval_jaxpr/all_to_all | solution.py:117
  570.9 18.2 %all-to-all-start.7 = ((f32[128,6,125]{2,1,0:T(8,128)}), f32[128,6,125]{2,1,0:T(8,128)S(1)}, u32[]{:S(2)}, u32[]{:S(2)}) async-start(f32[128,6,125]{2,1,0:T(8,128)} %reshape.538), calls=%async_computation.7 | async-start | bytes 1048576 | tf_op jit(solution)/shard_map/while/body/eval_jaxpr/all_to_all | solution.py:117
  611.9 18.8 %all-to-all-start = ((f32[128,8,126]{2,1,0:T(8,128)}), f32[128,8,126]{2,1,0:T(8,128)}, u32[]{:S(2)}, u32[]{:S(2)}) async-start(f32[128,8,126]{2,1,0:T(8,128)} %pad_bitcast_fusion.2), calls=%async_computation | async-start | bytes 1048576 | tf_op jit(solution)/shard_map/while/body/eval_jaxpr/all_to_all | solution.py:117
  651.3 19.1 %all-to-all-start.1 = ((f32[128,8,125]{2,1,0:T(8,128)}), f32[128,8,125]{2,1,0:T(8,128)}, u32[]{:S(2)}, u32[]{:S(2)}) async-start(f32[128,8,125]{2,1,0:T(8,128)} %bitcast.533), calls=%async_computation.1 | async-start | bytes 1048576 | tf_op jit(solution)/shard_map/while/body/eval_jaxpr/all_to_all | solution.py:117
  687.7 15.9 %all-to-all-start.2 = ((f32[128,4,125]{2,1,0:T(4,128)}), f32[128,4,125]{2,1,0:T(4,128)S(1)}, u32[]{:S(2)}, u32[]{:S(2)}) async-start(f32[128,4,125]{2,1,0:T(4,128)} %bitcast.549), calls=%async_computation.2 | async-start | bytes 524288 | tf_op jit(solution)/shard_map/while/body/eval_jaxpr/all_to_all | solution.py:117
  721.0 19.0 %all-to-all-start.3 = ((f32[128,6,125]{2,1,0:T(8,128)}), f32[128,6,125]{2,1,0:T(8,128)}, u32[]{:S(2)}, u32[]{:S(2)}) async-start(f32[128,6,125]{2,1,0:T(8,128)} %reshape.531), calls=%async_computation.3 | async-start | bytes 1048576 | tf_op jit(solution)/shard_map/while/body/eval_jaxpr/all_to_all | solution.py:117
  760.4 16.4 %all-to-all-start.4 = ((f32[128,4,125]{2,1,0:T(4,128)}), f32[128,4,125]{2,1,0:T(4,128)}, u32[]{:S(2)}, u32[]{:S(2)}) async-start(f32[128,4,125]{2,1,0:T(4,128)} %bitcast.575), calls=%async_computation.4 | async-start | bytes 524288 | tf_op jit(solution)/shard_map/while/body/eval_jaxpr/all_to_all | solution.py:117
  795.5 19.0 %all-to-all-start.5 = ((f32[128,7,125]{2,1,0:T(8,128)}), f32[128,7,125]{2,1,0:T(8,128)}, u32[]{:S(2)}, u32[]{:S(2)}) async-start(f32[128,7,125]{2,1,0:T(8,128)} %reshape.535), calls=%async_computation.5 | async-start | bytes 1048576 | tf_op jit(solution)/shard_map/while/body/eval_jaxpr/all_to_all | solution.py:117
  831.9 15.9 %all-to-all-start.6 = ((f32[128,4,125]{2,1,0:T(4,128)}), f32[128,4,125]{2,1,0:T(4,128)S(1)}, u32[]{:S(2)}, u32[]{:S(2)}) async-start(f32[128,4,125]{2,1,0:T(4,128)} %bitcast.601), calls=%async_computation.6 | async-start | bytes 524288 | tf_op jit(solution)/shard_map/while/body/eval_jaxpr/all_to_all | solution.py:117
  865.3 18.2 %all-to-all-start.7 = ((f32[128,6,125]{2,1,0:T(8,128)}), f32[128,6,125]{2,1,0:T(8,128)S(1)}, u32[]{:S(2)}, u32[]{:S(2)}) async-start(f32[128,6,125]{2,1,0:T(8,128)} %reshape.538), calls=%async_computation.7 | async-start | bytes 1048576 | tf_op jit(solution)/shard_map/while/body/eval_jaxpr/all_to_all | solution.py:117
  (131 other events, 792.5 us)

commit v8 on v7

--- a/solution.py
+++ b/solution.py
@@ -94,6 +94,10 @@
     send_row = send_list[0]
     pointers = face_partner.reshape(-1)
     divisors = jnp.power(2, level_map).astype(jnp.float32)
+    lift_faces = lift_block.reshape(TRACE_ROWS, 6, FACE_NODES).transpose(1, 0, 2)
+    lift_big = (
+        jnp.eye(VARIABLES, dtype=jnp.float32)[None, :, None, :, None] * lift_faces[:, None, :, None, :]
+    ).reshape(6, VARIABLES, TRACE_ROWS, TRACE_ROWS)
     substeps = 2 ** (LEVELS - 1)
     start_cache = jnp.zeros((TRACE_ROWS, peers, slot_count), jnp.float32)
 
@@ -108,12 +112,11 @@
             fresh = changed_slots(substep, slot_count)
             trace_table = make_table(fields)
             table_rows = trace_table.T
-            send_columns = send_row.reshape(peers, slot_count)[:, :fresh].reshape(-1)
+            send_columns = send_row.reshape(peers, slot_count)[:, :fresh]
             outgoing = table_rows.at[send_columns].get(mode="promise_in_bounds")
             if substep == 0:
-                rate_column = jnp.full((outgoing.shape[0], 1), local_fastest, jnp.float32)
-                outgoing = jnp.concatenate([outgoing, rate_column], axis=1)
-            outgoing = outgoing.reshape(peers, fresh, outgoing.shape[1])
+                rate_column = jnp.full((peers, fresh, 1), local_fastest, jnp.float32)
+                outgoing = jnp.concatenate([outgoing, rate_column], axis=2)
             arrived = lax.all_to_all(
                 outgoing, ("wall", "span"), split_axis=0, concat_axis=0, tiled=True
             )
@@ -127,8 +130,19 @@
             lookup = jnp.concatenate(
                 [table_rows, received.reshape(peers * slot_count, TRACE_ROWS)], axis=0
             )
-            nearby = arrange(lookup.at[pointers].get(mode="promise_in_bounds").T, local_count)
-            change = tendency(fields, nearby, volume_block, lift_block, flux_mixing, metric_scale)
+            jump_rows = lookup.at[pointers].get(mode="promise_in_bounds") - table_rows
+            lifted = jnp.einsum(
+                "fvpj,fej->vpe",
+                lift_big,
+                jump_rows.reshape(6, local_count, TRACE_ROWS),
+                precision=lax.Precision.HIGH,
+            )
+            combined = lifted - jnp.einsum(
+                "pq,vqe->vpe", volume_block, fields, precision=lax.Precision.HIGH
+            )
+            change = metric_scale * jnp.einsum(
+                "vw,wpe->vpe", flux_mixing, combined, precision=lax.Precision.HIGH
+            )
             fields = fields + jnp.where(level_map >= lowest, step_sizes * change, 0.0)
         return (fields, cache)
 

time: 904 us -> 806 us (0.89)
  local copies, waits for them, and re-layouts: 368 us -> 253 us
  other arithmetic: 47.9 us -> 62.5 us
    reshape x45 -> x1, local copies, waits for them, and re-layouts: 37 us -> 0.9 us  [body(): lift_block.reshape(TRACE_ROWS, 6, FACE_NODES).transpose(1, 0, 2)]
    transpose x24 -> x0, local copies, waits for them, and re-layouts: 31.6 us -> none  [coarse_step(): lookup.at[pointers].get(mode='promise_in_bounds')]
    sub x24, other arithmetic: 3.18 us -> 31.8 us  [coarse_step(): jump_rows = lookup.at[pointers].get(mode='promise_in_bounds') - table_rows]
    sub x48 -> x0, local copies, waits for them, and re-layouts: 28.2 us -> none  [tendency(): face_jumps = nearby - own_trace]
    reshape x24, local copies, waits for them, and re-layouts: 33.6 us -> 6.73 us  [make_table(): face_traces(fields).transpose(0, 2, 1, 3)]
    gather x24, local copies, waits for them, and re-layouts: 75.6 us -> 88.3 us  [coarse_step(): jump_rows = lookup.at[pointers].get(mode='promise_in_bounds') - table_rows]
    concatenate x9, other arithmetic: 10.9 us -> 1.54 us  [coarse_step(): arrived = jnp.concatenate([arrived, received[:, fresh:]], axis=1)]
    while x318 -> x345, local copies, waits for them, and re-layouts: 32.6 us -> 25.1 us
where the time goes in v8:
time: 806 us; the launch traced here: 800 us
  local copies, waits for them, and re-layouts  253 us (31%)
  waiting for transfers between devices  241 us (30%)
  starting transfers between devices  130 us (16%)
  matrix products  104 us (13%)
  other arithmetic  62.5 us (8%)
  loops' own time  8.92 us (1%)
    all_to_all x24, waiting for transfers between devices, coarse_step(): lax.all_to_all(outgoing, ('wall', 'span'), split_axis=0, concat_axis=0, t...  241 us
    all_to_all x24, starting transfers between devices, coarse_step(): lax.all_to_all(outgoing, ('wall', 'span'), split_axis=0, concat_axis=0, t...  130 us
    gather x24, local copies, waits for them, and re-layouts, coarse_step(): jump_rows = lookup.at[pointers].get(mode='promise_in_bounds') - table_rows  88.3 us
    gather x33, local copies, waits for them, and re-layouts, coarse_step(): outgoing = table_rows.at[send_columns].get(mode='promise_in_bounds')  58.3 us
    dot_general x24, matrix products, coarse_step(): jnp.einsum('pq,vqe->vpe', volume_block, fields, precision=lax.Precision.H...  42 us
    another operation x24, local copies, waits for them, and re-layouts, face_traces(): jnp.stack([face.reshape(VARIABLES, FACE_NODES, local_count) for face in f...  35.8 us
    dot_general x24, matrix products, coarse_step(): jnp.einsum('vw,wpe->vpe', flux_mixing, combined, precision=lax.Precision....  33.9 us
    sub x24, other arithmetic, coarse_step(): jump_rows = lookup.at[pointers].get(mode='promise_in_bounds') - table_rows  31.8 us
  transfers between devices with their start and end apart: 24, of which 24 were waited for; matrix products, arithmetic and copies ran while one was open for 7% of the time, Pallas kernels for 0%

profile of v8, /device:TPU:1, one launch (start us, length us, event | category | flops | bytes accessed | tf_op | source)
XLA Modules:
  0.0 799.5 jit_solution(3117477350855897437)
XLA Ops:
  5.5 792.7 %while.11 = (s32[]{:T(128)}, f32[5,125,256]{2,0,1:T(8,128)S(1)}, s32[256]{0:T(256)S(1)}, s32[1,1024]{1,0:T(1,128)S(1)}, f32[256]{0:T(256)S(1)}, /*index=5*/f32[2...) while((s32[]{:T(128)}, f32[5,125,256]{2,0,1:T(8,128)S(1)}, ...), condition=%wide.region_4.5_spmd.clone, body=%wide.region_0.4_spmd.clone.sunk | while | flops 6773918720 | bytes 253231376 | solution.py:149
  18.7 11.5 %all-to-all-start = ((f32[128,8,126]{2,1,0:T(8,128)}), f32[128,8,126]{2,1,0:T(8,128)S(1)}, u32[]{:S(2)}, u32[]{:S(2)}) async-start(f32[128,8,126]{2,1,0:T(8,128)} %concatenate.61), calls=%async_computation | async-start | bytes 1048576 | tf_op jit(solution)/shard_map/while/body/eval_jaxpr/all_to_all | solution.py:120
  33.1 10.9 %all-to-all-done = f32[128,8,126]{2,1,0:T(8,128)S(1)} async-done(((f32[128,8,126]{2,1,0:T(8,128)}), f32[128,8,126]{2,1,0:T(8,128)S(1)}, u32[]{:S(2)}, u32[]{:S(2)}) %all-to-all-start) | async-done | bytes 516128 | tf_op jit(solution)/shard_map/while/body/eval_jaxpr/all_to_all | solution.py:120
  69.4 11.6 %all-to-all-done.1 = f32[128,8,125]{2,1,0:T(8,128)} async-done(((f32[128,8,125]{2,1,0:T(8,128)}), f32[128,8,125]{2,1,0:T(8,128)}, u32[]{:S(2)}, u32[]{:S(2)}) %all-to-all-start.1) | async-done | bytes 512032 | tf_op jit(solution)/shard_map/while/body/eval_jaxpr/all_to_all | solution.py:120
  131.2 10.8 %all-to-all-done.3 = f32[128,6,125]{2,1,0:T(8,128)S(1)} async-done(((f32[128,6,125]{2,1,0:T(8,128)}), f32[128,6,125]{2,1,0:T(8,128)S(1)}, u32[]{:S(2)}, u32[]{:S(2)}) %all-to-all-start.3) | async-done | bytes 384032 | tf_op jit(solution)/shard_map/while/body/eval_jaxpr/all_to_all | solution.py:120
  163.1 8.2 %all-to-all-done.4 = f32[128,4,125]{2,1,0:T(4,128)} async-done(((f32[128,4,125]{2,1,0:T(4,128)}), f32[128,4,125]{2,1,0:T(4,128)}, u32[]{:S(2)}, u32[]{:S(2)}) %all-to-all-start.4) | async-done | bytes 256032 | tf_op jit(solution)/shard_map/while/body/eval_jaxpr/all_to_all | solution.py:120
  193.2 11.1 %all-to-all-done.5 = f32[128,7,125]{2,1,0:T(8,128)S(1)} async-done(((f32[128,7,125]{2,1,0:T(8,128)}), f32[128,7,125]{2,1,0:T(8,128)S(1)}, u32[]{:S(2)}, u32[]{:S(2)}) %all-to-all-start.5) | async-done | bytes 448032 | tf_op jit(solution)/shard_map/while/body/eval_jaxpr/all_to_all | solution.py:120
  224.5 8.4 %all-to-all-done.6 = f32[128,4,125]{2,1,0:T(4,128)S(1)} async-done(((f32[128,4,125]{2,1,0:T(4,128)}), f32[128,4,125]{2,1,0:T(4,128)S(1)}, u32[]{:S(2)}, u32[]{:S(2)}) %all-to-all-start.6) | async-done | bytes 256032 | tf_op jit(solution)/shard_map/while/body/eval_jaxpr/all_to_all | solution.py:120
  253.0 11.9 %all-to-all-done.7 = f32[128,6,125]{2,1,0:T(8,128)} async-done(((f32[128,6,125]{2,1,0:T(8,128)}), f32[128,6,125]{2,1,0:T(8,128)}, u32[]{:S(2)}, u32[]{:S(2)}) %all-to-all-start.7) | async-done | bytes 384032 | tf_op jit(solution)/shard_map/while/body/eval_jaxpr/all_to_all | solution.py:120
  294.9 10.9 %all-to-all-done = f32[128,8,126]{2,1,0:T(8,128)S(1)} async-done(((f32[128,8,126]{2,1,0:T(8,128)}), f32[128,8,126]{2,1,0:T(8,128)S(1)}, u32[]{:S(2)}, u32[]{:S(2)}) %all-to-all-start) | async-done | bytes 516128 | tf_op jit(solution)/shard_map/while/body/eval_jaxpr/all_to_all | solution.py:120
  331.1 11.6 %all-to-all-done.1 = f32[128,8,125]{2,1,0:T(8,128)} async-done(((f32[128,8,125]{2,1,0:T(8,128)}), f32[128,8,125]{2,1,0:T(8,128)}, u32[]{:S(2)}, u32[]{:S(2)}) %all-to-all-start.1) | async-done | bytes 512032 | tf_op jit(solution)/shard_map/while/body/eval_jaxpr/all_to_all | solution.py:120
  392.3 10.8 %all-to-all-done.3 = f32[128,6,125]{2,1,0:T(8,128)S(1)} async-done(((f32[128,6,125]{2,1,0:T(8,128)}), f32[128,6,125]{2,1,0:T(8,128)S(1)}, u32[]{:S(2)}, u32[]{:S(2)}) %all-to-all-start.3) | async-done | bytes 384032 | tf_op jit(solution)/shard_map/while/body/eval_jaxpr/all_to_all | solution.py:120
  424.3 8.2 %all-to-all-done.4 = f32[128,4,125]{2,1,0:T(4,128)} async-done(((f32[128,4,125]{2,1,0:T(4,128)}), f32[128,4,125]{2,1,0:T(4,128)}, u32[]{:S(2)}, u32[]{:S(2)}) %all-to-all-start.4) | async-done | bytes 256032 | tf_op jit(solution)/shard_map/while/body/eval_jaxpr/all_to_all | solution.py:120
  454.7 11.1 %all-to-all-done.5 = f32[128,7,125]{2,1,0:T(8,128)S(1)} async-done(((f32[128,7,125]{2,1,0:T(8,128)}), f32[128,7,125]{2,1,0:T(8,128)S(1)}, u32[]{:S(2)}, u32[]{:S(2)}) %all-to-all-start.5) | async-done | bytes 448032 | tf_op jit(solution)/shard_map/while/body/eval_jaxpr/all_to_all | solution.py:120
  486.0 8.4 %all-to-all-done.6 = f32[128,4,125]{2,1,0:T(4,128)S(1)} async-done(((f32[128,4,125]{2,1,0:T(4,128)}), f32[128,4,125]{2,1,0:T(4,128)S(1)}, u32[]{:S(2)}, u32[]{:S(2)}) %all-to-all-start.6) | async-done | bytes 256032 | tf_op jit(solution)/shard_map/while/body/eval_jaxpr/all_to_all | solution.py:120
  514.5 11.9 %all-to-all-done.7 = f32[128,6,125]{2,1,0:T(8,128)} async-done(((f32[128,6,125]{2,1,0:T(8,128)}), f32[128,6,125]{2,1,0:T(8,128)}, u32[]{:S(2)}, u32[]{:S(2)}) %all-to-all-start.7) | async-done | bytes 384032 | tf_op jit(solution)/shard_map/while/body/eval_jaxpr/all_to_all | solution.py:120
  556.2 10.9 %all-to-all-done = f32[128,8,126]{2,1,0:T(8,128)S(1)} async-done(((f32[128,8,126]{2,1,0:T(8,128)}), f32[128,8,126]{2,1,0:T(8,128)S(1)}, u32[]{:S(2)}, u32[]{:S(2)}) %all-to-all-start) | async-done | bytes 516128 | tf_op jit(solution)/shard_map/while/body/eval_jaxpr/all_to_all | solution.py:120
  592.5 11.6 %all-to-all-done.1 = f32[128,8,125]{2,1,0:T(8,128)} async-done(((f32[128,8,125]{2,1,0:T(8,128)}), f32[128,8,125]{2,1,0:T(8,128)}, u32[]{:S(2)}, u32[]{:S(2)}) %all-to-all-start.1) | async-done | bytes 512032 | tf_op jit(solution)/shard_map/while/body/eval_jaxpr/all_to_all | solution.py:120
  625.5 7.5 all-to-all-done.2
  653.8 10.8 %all-to-all-done.3 = f32[128,6,125]{2,1,0:T(8,128)S(1)} async-done(((f32[128,6,125]{2,1,0:T(8,128)}), f32[128,6,125]{2,1,0:T(8,128)S(1)}, u32[]{:S(2)}, u32[]{:S(2)}) %all-to-all-start.3) | async-done | bytes 384032 | tf_op jit(solution)/shard_map/while/body/eval_jaxpr/all_to_all | solution.py:120
  685.8 8.2 %all-to-all-done.4 = f32[128,4,125]{2,1,0:T(4,128)} async-done(((f32[128,4,125]{2,1,0:T(4,128)}), f32[128,4,125]{2,1,0:T(4,128)}, u32[]{:S(2)}, u32[]{:S(2)}) %all-to-all-start.4) | async-done | bytes 256032 | tf_op jit(solution)/shard_map/while/body/eval_jaxpr/all_to_all | solution.py:120
  715.9 11.1 %all-to-all-done.5 = f32[128,7,125]{2,1,0:T(8,128)S(1)} async-done(((f32[128,7,125]{2,1,0:T(8,128)}), f32[128,7,125]{2,1,0:T(8,128)S(1)}, u32[]{:S(2)}, u32[]{:S(2)}) %all-to-all-start.5) | async-done | bytes 448032 | tf_op jit(solution)/shard_map/while/body/eval_jaxpr/all_to_all | solution.py:120
  747.4 8.4 %all-to-all-done.6 = f32[128,4,125]{2,1,0:T(4,128)S(1)} async-done(((f32[128,4,125]{2,1,0:T(4,128)}), f32[128,4,125]{2,1,0:T(4,128)S(1)}, u32[]{:S(2)}, u32[]{:S(2)}) %all-to-all-start.6) | async-done | bytes 256032 | tf_op jit(solution)/shard_map/while/body/eval_jaxpr/all_to_all | solution.py:120
  775.9 11.9 %all-to-all-done.7 = f32[128,6,125]{2,1,0:T(8,128)} async-done(((f32[128,6,125]{2,1,0:T(8,128)}), f32[128,6,125]{2,1,0:T(8,128)}, u32[]{:S(2)}, u32[]{:S(2)}) %all-to-all-start.7) | async-done | bytes 384032 | tf_op jit(solution)/shard_map/while/body/eval_jaxpr/all_to_all | solution.py:120
  (919 shorter events, 552.6 us)
Async XLA Ops:
  18.7 25.2 %all-to-all-start = ((f32[128,8,126]{2,1,0:T(8,128)}), f32[128,8,126]{2,1,0:T(8,128)S(1)}, u32[]{:S(2)}, u32[]{:S(2)}) async-start(f32[128,8,126]{2,1,0:T(8,128)} %concatenate.61), calls=%async_computation | async-start | bytes 1048576 | tf_op jit(solution)/shard_map/while/body/eval_jaxpr/all_to_all | solution.py:120
  61.7 19.3 %all-to-all-start.1 = ((f32[128,8,125]{2,1,0:T(8,128)}), f32[128,8,125]{2,1,0:T(8,128)}, u32[]{:S(2)}, u32[]{:S(2)}) async-start(f32[128,8,125]{2,1,0:T(8,128)} %bitcast.623), calls=%async_computation.1 | async-start | bytes 1048576 | tf_op jit(solution)/shard_map/while/body/eval_jaxpr/all_to_all | solution.py:120
  94.0 15.8 %all-to-all-start.2 = ((f32[128,4,125]{2,1,0:T(4,128)}), f32[128,4,125]{2,1,0:T(4,128)S(1)}, u32[]{:S(2)}, u32[]{:S(2)}) async-start(f32[128,4,125]{2,1,0:T(4,128)} %bitcast.638), calls=%async_computation.2 | async-start | bytes 524288 | tf_op jit(solution)/shard_map/while/body/eval_jaxpr/all_to_all | solution.py:120
  123.1 18.9 %all-to-all-start.3 = ((f32[128,6,125]{2,1,0:T(8,128)}), f32[128,6,125]{2,1,0:T(8,128)S(1)}, u32[]{:S(2)}, u32[]{:S(2)}) async-start(f32[128,6,125]{2,1,0:T(8,128)} %reshape.491), calls=%async_computation.3 | async-start | bytes 1048576 | tf_op jit(solution)/shard_map/while/body/eval_jaxpr/all_to_all | solution.py:120
  154.9 16.3 %all-to-all-start.4 = ((f32[128,4,125]{2,1,0:T(4,128)}), f32[128,4,125]{2,1,0:T(4,128)}, u32[]{:S(2)}, u32[]{:S(2)}) async-start(f32[128,4,125]{2,1,0:T(4,128)} %bitcast.663), calls=%async_computation.4 | async-start | bytes 524288 | tf_op jit(solution)/shard_map/while/body/eval_jaxpr/all_to_all | solution.py:120
  185.8 18.5 %all-to-all-start.5 = ((f32[128,7,125]{2,1,0:T(8,128)}), f32[128,7,125]{2,1,0:T(8,128)S(1)}, u32[]{:S(2)}, u32[]{:S(2)}) async-start(f32[128,7,125]{2,1,0:T(8,128)} %reshape.493), calls=%async_computation.5 | async-start | bytes 1048576 | tf_op jit(solution)/shard_map/while/body/eval_jaxpr/all_to_all | solution.py:120
  217.2 15.7 %all-to-all-start.6 = ((f32[128,4,125]{2,1,0:T(4,128)}), f32[128,4,125]{2,1,0:T(4,128)S(1)}, u32[]{:S(2)}, u32[]{:S(2)}) async-start(f32[128,4,125]{2,1,0:T(4,128)} %bitcast.688), calls=%async_computation.6 | async-start | bytes 524288 | tf_op jit(solution)/shard_map/while/body/eval_jaxpr/all_to_all | solution.py:120
  246.1 18.8 %all-to-all-start.7 = ((f32[128,6,125]{2,1,0:T(8,128)}), f32[128,6,125]{2,1,0:T(8,128)}, u32[]{:S(2)}, u32[]{:S(2)}) async-start(f32[128,6,125]{2,1,0:T(8,128)} %reshape.494), calls=%async_computation.7 | async-start | bytes 1048576 | tf_op jit(solution)/shard_map/while/body/eval_jaxpr/all_to_all | solution.py:120
  287.6 18.2 %all-to-all-start = ((f32[128,8,126]{2,1,0:T(8,128)}), f32[128,8,126]{2,1,0:T(8,128)S(1)}, u32[]{:S(2)}, u32[]{:S(2)}) async-start(f32[128,8,126]{2,1,0:T(8,128)} %concatenate.61), calls=%async_computation | async-start | bytes 1048576 | tf_op jit(solution)/shard_map/while/body/eval_jaxpr/all_to_all | solution.py:120
  323.6 19.2 %all-to-all-start.1 = ((f32[128,8,125]{2,1,0:T(8,128)}), f32[128,8,125]{2,1,0:T(8,128)}, u32[]{:S(2)}, u32[]{:S(2)}) async-start(f32[128,8,125]{2,1,0:T(8,128)} %bitcast.623), calls=%async_computation.1 | async-start | bytes 1048576 | tf_op jit(solution)/shard_map/while/body/eval_jaxpr/all_to_all | solution.py:120
  355.7 15.7 %all-to-all-start.2 = ((f32[128,4,125]{2,1,0:T(4,128)}), f32[128,4,125]{2,1,0:T(4,128)S(1)}, u32[]{:S(2)}, u32[]{:S(2)}) async-start(f32[128,4,125]{2,1,0:T(4,128)} %bitcast.638), calls=%async_computation.2 | async-start | bytes 524288 | tf_op jit(solution)/shard_map/while/body/eval_jaxpr/all_to_all | solution.py:120
  384.6 18.5 %all-to-all-start.3 = ((f32[128,6,125]{2,1,0:T(8,128)}), f32[128,6,125]{2,1,0:T(8,128)S(1)}, u32[]{:S(2)}, u32[]{:S(2)}) async-start(f32[128,6,125]{2,1,0:T(8,128)} %reshape.491), calls=%async_computation.3 | async-start | bytes 1048576 | tf_op jit(solution)/shard_map/while/body/eval_jaxpr/all_to_all | solution.py:120
  416.1 16.5 %all-to-all-start.4 = ((f32[128,4,125]{2,1,0:T(4,128)}), f32[128,4,125]{2,1,0:T(4,128)}, u32[]{:S(2)}, u32[]{:S(2)}) async-start(f32[128,4,125]{2,1,0:T(4,128)} %bitcast.663), calls=%async_computation.4 | async-start | bytes 524288 | tf_op jit(solution)/shard_map/while/body/eval_jaxpr/all_to_all | solution.py:120
  447.1 18.8 %all-to-all-start.5 = ((f32[128,7,125]{2,1,0:T(8,128)}), f32[128,7,125]{2,1,0:T(8,128)S(1)}, u32[]{:S(2)}, u32[]{:S(2)}) async-start(f32[128,7,125]{2,1,0:T(8,128)} %reshape.493), calls=%async_computation.5 | async-start | bytes 1048576 | tf_op jit(solution)/shard_map/while/body/eval_jaxpr/all_to_all | solution.py:120
  478.7 15.7 %all-to-all-start.6 = ((f32[128,4,125]{2,1,0:T(4,128)}), f32[128,4,125]{2,1,0:T(4,128)S(1)}, u32[]{:S(2)}, u32[]{:S(2)}) async-start(f32[128,4,125]{2,1,0:T(4,128)} %bitcast.688), calls=%async_computation.6 | async-start | bytes 524288 | tf_op jit(solution)/shard_map/while/body/eval_jaxpr/all_to_all | solution.py:120
  507.6 18.8 %all-to-all-start.7 = ((f32[128,6,125]{2,1,0:T(8,128)}), f32[128,6,125]{2,1,0:T(8,128)}, u32[]{:S(2)}, u32[]{:S(2)}) async-start(f32[128,6,125]{2,1,0:T(8,128)} %reshape.494), calls=%async_computation.7 | async-start | bytes 1048576 | tf_op jit(solution)/shard_map/while/body/eval_jaxpr/all_to_all | solution.py:120
  548.8 18.2 %all-to-all-start = ((f32[128,8,126]{2,1,0:T(8,128)}), f32[128,8,126]{2,1,0:T(8,128)S(1)}, u32[]{:S(2)}, u32[]{:S(2)}) async-start(f32[128,8,126]{2,1,0:T(8,128)} %concatenate.61), calls=%async_computation | async-start | bytes 1048576 | tf_op jit(solution)/shard_map/while/body/eval_jaxpr/all_to_all | solution.py:120
  584.8 19.3 %all-to-all-start.1 = ((f32[128,8,125]{2,1,0:T(8,128)}), f32[128,8,125]{2,1,0:T(8,128)}, u32[]{:S(2)}, u32[]{:S(2)}) async-start(f32[128,8,125]{2,1,0:T(8,128)} %bitcast.623), calls=%async_computation.1 | async-start | bytes 1048576 | tf_op jit(solution)/shard_map/while/body/eval_jaxpr/all_to_all | solution.py:120
  617.1 15.9 %all-to-all-start.2 = ((f32[128,4,125]{2,1,0:T(4,128)}), f32[128,4,125]{2,1,0:T(4,128)S(1)}, u32[]{:S(2)}, u32[]{:S(2)}) async-start(f32[128,4,125]{2,1,0:T(4,128)} %bitcast.638), calls=%async_computation.2 | async-start | bytes 524288 | tf_op jit(solution)/shard_map/while/body/eval_jaxpr/all_to_all | solution.py:120
  646.2 18.4 %all-to-all-start.3 = ((f32[128,6,125]{2,1,0:T(8,128)}), f32[128,6,125]{2,1,0:T(8,128)S(1)}, u32[]{:S(2)}, u32[]{:S(2)}) async-start(f32[128,6,125]{2,1,0:T(8,128)} %reshape.491), calls=%async_computation.3 | async-start | bytes 1048576 | tf_op jit(solution)/shard_map/while/body/eval_jaxpr/all_to_all | solution.py:120
  677.6 16.4 %all-to-all-start.4 = ((f32[128,4,125]{2,1,0:T(4,128)}), f32[128,4,125]{2,1,0:T(4,128)}, u32[]{:S(2)}, u32[]{:S(2)}) async-start(f32[128,4,125]{2,1,0:T(4,128)} %bitcast.663), calls=%async_computation.4 | async-start | bytes 524288 | tf_op jit(solution)/shard_map/while/body/eval_jaxpr/all_to_all | solution.py:120
  708.5 18.5 %all-to-all-start.5 = ((f32[128,7,125]{2,1,0:T(8,128)}), f32[128,7,125]{2,1,0:T(8,128)S(1)}, u32[]{:S(2)}, u32[]{:S(2)}) async-start(f32[128,7,125]{2,1,0:T(8,128)} %reshape.493), calls=%async_computation.5 | async-start | bytes 1048576 | tf_op jit(solution)/shard_map/while/body/eval_jaxpr/all_to_all | solution.py:120
  739.9 16.0 %all-to-all-start.6 = ((f32[128,4,125]{2,1,0:T(4,128)}), f32[128,4,125]{2,1,0:T(4,128)S(1)}, u32[]{:S(2)}, u32[]{:S(2)}) async-start(f32[128,4,125]{2,1,0:T(4,128)} %bitcast.688), calls=%async_computation.6 | async-start | bytes 524288 | tf_op jit(solution)/shard_map/while/body/eval_jaxpr/all_to_all | solution.py:120
  769.0 18.8 %all-to-all-start.7 = ((f32[128,6,125]{2,1,0:T(8,128)}), f32[128,6,125]{2,1,0:T(8,128)}, u32[]{:S(2)}, u32[]{:S(2)}) async-start(f32[128,6,125]{2,1,0:T(8,128)} %reshape.494), calls=%async_computation.7 | async-start | bytes 1048576 | tf_op jit(solution)/shard_map/while/body/eval_jaxpr/all_to_all | solution.py:120
  (143 other events, 744.2 us)

commit v9 on v8

--- a/solution.py
+++ b/solution.py
@@ -130,16 +130,19 @@
             lookup = jnp.concatenate(
                 [table_rows, received.reshape(peers * slot_count, TRACE_ROWS)], axis=0
             )
-            jump_rows = lookup.at[pointers].get(mode="promise_in_bounds") - table_rows
-            lifted = jnp.einsum(
+            own_part = jnp.einsum(
                 "fvpj,fej->vpe",
                 lift_big,
-                jump_rows.reshape(6, local_count, TRACE_ROWS),
+                table_rows.reshape(6, local_count, TRACE_ROWS),
                 precision=lax.Precision.HIGH,
-            )
-            combined = lifted - jnp.einsum(
-                "pq,vqe->vpe", volume_block, fields, precision=lax.Precision.HIGH
-            )
+            ) + jnp.einsum("pq,vqe->vpe", volume_block, fields, precision=lax.Precision.HIGH)
+            near_rows = lookup.at[pointers].get(mode="promise_in_bounds")
+            combined = jnp.einsum(
+                "fvpj,fej->vpe",
+                lift_big,
+                near_rows.reshape(6, local_count, TRACE_ROWS),
+                precision=lax.Precision.HIGH,
+            ) - own_part
             change = metric_scale * jnp.einsum(
                 "vw,wpe->vpe", flux_mixing, combined, precision=lax.Precision.HIGH
             )

time: 806 us -> 883 us (1.096)
  matrix products: 104 us -> 202 us
  local copies, waits for them, and re-layouts: 253 us -> 326 us
  waiting for transfers between devices: 241 us -> 188 us
  other arithmetic: 62.5 us -> 26.6 us
    dot_general x24 -> x48, matrix products: 27.8 us -> 83 us  [the longest x24 45 us: coarse_step(): jnp.einsum('fvpj,fej->vpe', lift_big, table_rows.reshape(6, local_count,...]
    all_to_all x24, waiting for transfers between devices: 241 us -> 188 us  [coarse_step(): lax.all_to_all(outgoing, ('wall', 'span'), split_axis=0, concat_axis=0, t...]
    sub x24 -> x0, other arithmetic: 31.8 us -> none  [coarse_step(): jump_rows = lookup.at[pointers].get(mode='promise_in_bounds') - table_rows]
    dot_general x24, matrix products: 33.9 us -> 62.9 us  [coarse_step(): jnp.einsum('vw,wpe->vpe', flux_mixing, combined, precision=lax.Precision....]
    another operation x24, local copies, waits for them, and re-layouts: 35.8 us -> 63.6 us  [face_traces(): jnp.stack([face.reshape(VARIABLES, FACE_NODES, local_count) for face in f...]
    while x345 -> x297, local copies, waits for them, and re-layouts: 25.1 us -> 49.4 us
    reshape x24, local copies, waits for them, and re-layouts: 6.73 us -> 23.5 us  [make_table(): face_traces(fields).transpose(0, 2, 1, 3)]
    gather x24, local copies, waits for them, and re-layouts: 88.3 us -> 71.9 us  [coarse_step(): near_rows = lookup.at[pointers].get(mode='promise_in_bounds')]
  transfers between devices with their start and end apart: 24 -> 24, of which waited for: 24 -> 24; matrix products, arithmetic and copies ran while one was open for 7% -> 13% of each run, Pallas kernels for 0% -> 0%
where the time goes in v9:
time: 883 us; the launch traced here: 875 us
  local copies, waits for them, and re-layouts  326 us (37%)
  matrix products  202 us (23%)
  waiting for transfers between devices  188 us (21%)
  starting transfers between devices  124 us (14%)
  other arithmetic  26.6 us (3%)
    all_to_all x24, waiting for transfers between devices, coarse_step(): lax.all_to_all(outgoing, ('wall', 'span'), split_axis=0, concat_axis=0, t...  188 us
    all_to_all x24, starting transfers between devices, coarse_step(): lax.all_to_all(outgoing, ('wall', 'span'), split_axis=0, concat_axis=0, t...  124 us
    gather x24, local copies, waits for them, and re-layouts, coarse_step(): near_rows = lookup.at[pointers].get(mode='promise_in_bounds')  71.9 us
    another operation x24, local copies, waits for them, and re-layouts, face_traces(): jnp.stack([face.reshape(VARIABLES, FACE_NODES, local_count) for face in f...  63.6 us
    dot_general x24, matrix products, coarse_step(): jnp.einsum('vw,wpe->vpe', flux_mixing, combined, precision=lax.Precision....  62.9 us
    gather x33, local copies, waits for them, and re-layouts, coarse_step(): outgoing = table_rows.at[send_columns].get(mode='promise_in_bounds')  58.3 us
    dot_general x24, matrix products, coarse_step(): jnp.einsum('pq,vqe->vpe', volume_block, fields, precision=lax.Precision.H...  56 us
    while x297, local copies, waits for them, and re-layouts  49.4 us
  transfers between devices with their start and end apart: 24, of which 24 were waited for; matrix products, arithmetic and copies ran while one was open for 13% of the time, Pallas kernels for 0%

profile of v9, /device:TPU:1, one launch (start us, length us, event | category | flops | bytes accessed | tf_op | source)
XLA Modules:
  0.0 874.6 jit_solution(10391936768232787689)
XLA Ops:
  5.1 867.0 %while.11 = (s32[]{:T(128)}, f32[5,125,256]{2,0,1:T(8,128)}, s32[256]{0:T(256)}, s32[1,1024]{1,0:T(1,128)S(1)}, f32[256]{0:T(256)S(1)}, /*index=5*/f32[256]{0:T(...) while((s32[]{:T(128)}, f32[5,125,256]{2,0,1:T(8,128)}, ...), condition=%wide.region_4.5_spmd.clone, body=%wide.region_0.4_spmd.clone.sunk | while | flops 12537413632 | bytes 260818512 | solution.py:152
  18.2 11.5 %all-to-all-start = ((f32[128,8,126]{2,1,0:T(8,128)}), f32[128,8,126]{2,1,0:T(8,128)S(1)}, u32[]{:S(2)}, u32[]{:S(2)}) async-start(f32[128,8,126]{2,1,0:T(8,128)} %concatenate.61), calls=%async_computation | async-start | bytes 1048576 | tf_op jit(solution)/shard_map/while/body/eval_jaxpr/all_to_all | solution.py:120
  36.1 7.3 all-to-all-done
  74.4 9.5 %all-to-all-done.1 = f32[128,8,125]{2,1,0:T(8,128)S(1)} async-done(((f32[128,8,125]{2,1,0:T(8,128)}), f32[128,8,125]{2,1,0:T(8,128)S(1)}, u32[]{:S(2)}, u32[]{:S(2)}) %all-to-all-start.1) | async-done | bytes 512032 | tf_op jit(solution)/shard_map/while/body/eval_jaxpr/all_to_all | solution.py:120
  144.8 9.4 %all-to-all-done.3 = f32[128,6,125]{2,1,0:T(8,128)S(1)} async-done(((f32[128,6,125]{2,1,0:T(8,128)}), f32[128,6,125]{2,1,0:T(8,128)S(1)}, u32[]{:S(2)}, u32[]{:S(2)}) %all-to-all-start.3) | async-done | bytes 384032 | tf_op jit(solution)/shard_map/while/body/eval_jaxpr/all_to_all | solution.py:120
  181.3 6.6 all-to-all-done.4
  213.1 9.4 %all-to-all-done.5 = f32[128,7,125]{2,1,0:T(8,128)S(1)} async-done(((f32[128,7,125]{2,1,0:T(8,128)}), f32[128,7,125]{2,1,0:T(8,128)S(1)}, u32[]{:S(2)}, u32[]{:S(2)}) %all-to-all-start.5) | async-done | bytes 448032 | tf_op jit(solution)/shard_map/while/body/eval_jaxpr/all_to_all | solution.py:120
  248.8 5.7 all-to-all-done.6
  279.7 9.5 %all-to-all-done.7 = f32[128,6,125]{2,1,0:T(8,128)S(1)} async-done(((f32[128,6,125]{2,1,0:T(8,128)}), f32[128,6,125]{2,1,0:T(8,128)S(1)}, u32[]{:S(2)}, u32[]{:S(2)}) %all-to-all-start.7) | async-done | bytes 384032 | tf_op jit(solution)/shard_map/while/body/eval_jaxpr/all_to_all | solution.py:120
  322.7 7.3 all-to-all-done
  360.8 9.5 %all-to-all-done.1 = f32[128,8,125]{2,1,0:T(8,128)S(1)} async-done(((f32[128,8,125]{2,1,0:T(8,128)}), f32[128,8,125]{2,1,0:T(8,128)S(1)}, u32[]{:S(2)}, u32[]{:S(2)}) %all-to-all-start.1) | async-done | bytes 512032 | tf_op jit(solution)/shard_map/while/body/eval_jaxpr/all_to_all | solution.py:120
  400.5 5.3 all-to-all-done.2
  430.9 9.4 %all-to-all-done.3 = f32[128,6,125]{2,1,0:T(8,128)S(1)} async-done(((f32[128,6,125]{2,1,0:T(8,128)}), f32[128,6,125]{2,1,0:T(8,128)S(1)}, u32[]{:S(2)}, u32[]{:S(2)}) %all-to-all-start.3) | async-done | bytes 384032 | tf_op jit(solution)/shard_map/while/body/eval_jaxpr/all_to_all | solution.py:120
  467.5 6.6 all-to-all-done.4
  499.3 9.4 %all-to-all-done.5 = f32[128,7,125]{2,1,0:T(8,128)S(1)} async-done(((f32[128,7,125]{2,1,0:T(8,128)}), f32[128,7,125]{2,1,0:T(8,128)S(1)}, u32[]{:S(2)}, u32[]{:S(2)}) %all-to-all-start.5) | async-done | bytes 448032 | tf_op jit(solution)/shard_map/while/body/eval_jaxpr/all_to_all | solution.py:120
  534.9 5.7 all-to-all-done.6
  565.8 9.5 %all-to-all-done.7 = f32[128,6,125]{2,1,0:T(8,128)S(1)} async-done(((f32[128,6,125]{2,1,0:T(8,128)}), f32[128,6,125]{2,1,0:T(8,128)S(1)}, u32[]{:S(2)}, u32[]{:S(2)}) %all-to-all-start.7) | async-done | bytes 384032 | tf_op jit(solution)/shard_map/while/body/eval_jaxpr/all_to_all | solution.py:120
  608.8 7.3 all-to-all-done
  647.0 9.5 %all-to-all-done.1 = f32[128,8,125]{2,1,0:T(8,128)S(1)} async-done(((f32[128,8,125]{2,1,0:T(8,128)}), f32[128,8,125]{2,1,0:T(8,128)S(1)}, u32[]{:S(2)}, u32[]{:S(2)}) %all-to-all-start.1) | async-done | bytes 512032 | tf_op jit(solution)/shard_map/while/body/eval_jaxpr/all_to_all | solution.py:120
  717.1 9.4 %all-to-all-done.3 = f32[128,6,125]{2,1,0:T(8,128)S(1)} async-done(((f32[128,6,125]{2,1,0:T(8,128)}), f32[128,6,125]{2,1,0:T(8,128)S(1)}, u32[]{:S(2)}, u32[]{:S(2)}) %all-to-all-start.3) | async-done | bytes 384032 | tf_op jit(solution)/shard_map/while/body/eval_jaxpr/all_to_all | solution.py:120
  753.6 6.6 all-to-all-done.4
  785.4 9.4 %all-to-all-done.5 = f32[128,7,125]{2,1,0:T(8,128)S(1)} async-done(((f32[128,7,125]{2,1,0:T(8,128)}), f32[128,7,125]{2,1,0:T(8,128)S(1)}, u32[]{:S(2)}, u32[]{:S(2)}) %all-to-all-start.5) | async-done | bytes 448032 | tf_op jit(solution)/shard_map/while/body/eval_jaxpr/all_to_all | solution.py:120
  821.0 5.7 all-to-all-done.6
  852.0 9.5 %all-to-all-done.7 = f32[128,6,125]{2,1,0:T(8,128)S(1)} async-done(((f32[128,6,125]{2,1,0:T(8,128)}), f32[128,6,125]{2,1,0:T(8,128)S(1)}, u32[]{:S(2)}, u32[]{:S(2)}) %all-to-all-start.7) | async-done | bytes 384032 | tf_op jit(solution)/shard_map/while/body/eval_jaxpr/all_to_all | solution.py:120
  (871 shorter events, 677.4 us)
Async XLA Ops:
  18.2 25.2 %all-to-all-start = ((f32[128,8,126]{2,1,0:T(8,128)}), f32[128,8,126]{2,1,0:T(8,128)S(1)}, u32[]{:S(2)}, u32[]{:S(2)}) async-start(f32[128,8,126]{2,1,0:T(8,128)} %concatenate.61), calls=%async_computation | async-start | bytes 1048576 | tf_op jit(solution)/shard_map/while/body/eval_jaxpr/all_to_all | solution.py:120
  65.3 18.6 %all-to-all-start.1 = ((f32[128,8,125]{2,1,0:T(8,128)}), f32[128,8,125]{2,1,0:T(8,128)S(1)}, u32[]{:S(2)}, u32[]{:S(2)}) async-start(f32[128,8,125]{2,1,0:T(8,128)} %bitcast.966), calls=%async_computation.1 | async-start | bytes 1048576 | tf_op jit(solution)/shard_map/while/body/eval_jaxpr/all_to_all | solution.py:120
  103.6 15.9 %all-to-all-start.2 = ((f32[128,4,125]{2,1,0:T(4,128)}), f32[128,4,125]{2,1,0:T(4,128)S(1)}, u32[]{:S(2)}, u32[]{:S(2)}) async-start(f32[128,4,125]{2,1,0:T(4,128)} %bitcast.819), calls=%async_computation.2 | async-start | bytes 524288 | tf_op jit(solution)/shard_map/while/body/eval_jaxpr/all_to_all | solution.py:120
  135.3 18.9 %all-to-all-start.3 = ((f32[128,6,125]{2,1,0:T(8,128)}), f32[128,6,125]{2,1,0:T(8,128)S(1)}, u32[]{:S(2)}, u32[]{:S(2)}) async-start(f32[128,6,125]{2,1,0:T(8,128)} %reshape.539), calls=%async_computation.3 | async-start | bytes 1048576 | tf_op jit(solution)/shard_map/while/body/eval_jaxpr/all_to_all | solution.py:120
  172.2 15.7 %all-to-all-start.4 = ((f32[128,4,125]{2,1,0:T(4,128)}), f32[128,4,125]{2,1,0:T(4,128)S(1)}, u32[]{:S(2)}, u32[]{:S(2)}) async-start(f32[128,4,125]{2,1,0:T(4,128)} %bitcast.846), calls=%async_computation.4 | async-start | bytes 524288 | tf_op jit(solution)/shard_map/while/body/eval_jaxpr/all_to_all | solution.py:120
  204.1 18.5 %all-to-all-start.5 = ((f32[128,7,125]{2,1,0:T(8,128)}), f32[128,7,125]{2,1,0:T(8,128)S(1)}, u32[]{:S(2)}, u32[]{:S(2)}) async-start(f32[128,7,125]{2,1,0:T(8,128)} %reshape.541), calls=%async_computation.5 | async-start | bytes 1048576 | tf_op jit(solution)/shard_map/while/body/eval_jaxpr/all_to_all | solution.py:120
  238.8 15.7 %all-to-all-start.6 = ((f32[128,4,125]{2,1,0:T(4,128)}), f32[128,4,125]{2,1,0:T(4,128)S(1)}, u32[]{:S(2)}, u32[]{:S(2)}) async-start(f32[128,4,125]{2,1,0:T(4,128)} %bitcast.873), calls=%async_computation.6 | async-start | bytes 524288 | tf_op jit(solution)/shard_map/while/body/eval_jaxpr/all_to_all | solution.py:120
  270.5 18.7 %all-to-all-start.7 = ((f32[128,6,125]{2,1,0:T(8,128)}), f32[128,6,125]{2,1,0:T(8,128)S(1)}, u32[]{:S(2)}, u32[]{:S(2)}) async-start(f32[128,6,125]{2,1,0:T(8,128)} %reshape.542), calls=%async_computation.7 | async-start | bytes 1048576 | tf_op jit(solution)/shard_map/while/body/eval_jaxpr/all_to_all | solution.py:120
  311.8 18.2 %all-to-all-start = ((f32[128,8,126]{2,1,0:T(8,128)}), f32[128,8,126]{2,1,0:T(8,128)S(1)}, u32[]{:S(2)}, u32[]{:S(2)}) async-start(f32[128,8,126]{2,1,0:T(8,128)} %concatenate.61), calls=%async_computation | async-start | bytes 1048576 | tf_op jit(solution)/shard_map/while/body/eval_jaxpr/all_to_all | solution.py:120
  351.8 18.5 %all-to-all-start.1 = ((f32[128,8,125]{2,1,0:T(8,128)}), f32[128,8,125]{2,1,0:T(8,128)S(1)}, u32[]{:S(2)}, u32[]{:S(2)}) async-start(f32[128,8,125]{2,1,0:T(8,128)} %bitcast.966), calls=%async_computation.1 | async-start | bytes 1048576 | tf_op jit(solution)/shard_map/while/body/eval_jaxpr/all_to_all | solution.py:120
  390.0 15.8 %all-to-all-start.2 = ((f32[128,4,125]{2,1,0:T(4,128)}), f32[128,4,125]{2,1,0:T(4,128)S(1)}, u32[]{:S(2)}, u32[]{:S(2)}) async-start(f32[128,4,125]{2,1,0:T(4,128)} %bitcast.819), calls=%async_computation.2 | async-start | bytes 524288 | tf_op jit(solution)/shard_map/while/body/eval_jaxpr/all_to_all | solution.py:120
  421.6 18.7 %all-to-all-start.3 = ((f32[128,6,125]{2,1,0:T(8,128)}), f32[128,6,125]{2,1,0:T(8,128)S(1)}, u32[]{:S(2)}, u32[]{:S(2)}) async-start(f32[128,6,125]{2,1,0:T(8,128)} %reshape.539), calls=%async_computation.3 | async-start | bytes 1048576 | tf_op jit(solution)/shard_map/while/body/eval_jaxpr/all_to_all | solution.py:120
  458.3 15.7 %all-to-all-start.4 = ((f32[128,4,125]{2,1,0:T(4,128)}), f32[128,4,125]{2,1,0:T(4,128)S(1)}, u32[]{:S(2)}, u32[]{:S(2)}) async-start(f32[128,4,125]{2,1,0:T(4,128)} %bitcast.846), calls=%async_computation.4 | async-start | bytes 524288 | tf_op jit(solution)/shard_map/while/body/eval_jaxpr/all_to_all | solution.py:120
  490.2 18.5 %all-to-all-start.5 = ((f32[128,7,125]{2,1,0:T(8,128)}), f32[128,7,125]{2,1,0:T(8,128)S(1)}, u32[]{:S(2)}, u32[]{:S(2)}) async-start(f32[128,7,125]{2,1,0:T(8,128)} %reshape.541), calls=%async_computation.5 | async-start | bytes 1048576 | tf_op jit(solution)/shard_map/while/body/eval_jaxpr/all_to_all | solution.py:120
  524.9 15.7 %all-to-all-start.6 = ((f32[128,4,125]{2,1,0:T(4,128)}), f32[128,4,125]{2,1,0:T(4,128)S(1)}, u32[]{:S(2)}, u32[]{:S(2)}) async-start(f32[128,4,125]{2,1,0:T(4,128)} %bitcast.873), calls=%async_computation.6 | async-start | bytes 524288 | tf_op jit(solution)/shard_map/while/body/eval_jaxpr/all_to_all | solution.py:120
  556.6 18.7 %all-to-all-start.7 = ((f32[128,6,125]{2,1,0:T(8,128)}), f32[128,6,125]{2,1,0:T(8,128)S(1)}, u32[]{:S(2)}, u32[]{:S(2)}) async-start(f32[128,6,125]{2,1,0:T(8,128)} %reshape.542), calls=%async_computation.7 | async-start | bytes 1048576 | tf_op jit(solution)/shard_map/while/body/eval_jaxpr/all_to_all | solution.py:120
  597.9 18.2 %all-to-all-start = ((f32[128,8,126]{2,1,0:T(8,128)}), f32[128,8,126]{2,1,0:T(8,128)S(1)}, u32[]{:S(2)}, u32[]{:S(2)}) async-start(f32[128,8,126]{2,1,0:T(8,128)} %concatenate.61), calls=%async_computation | async-start | bytes 1048576 | tf_op jit(solution)/shard_map/while/body/eval_jaxpr/all_to_all | solution.py:120
  638.0 18.5 %all-to-all-start.1 = ((f32[128,8,125]{2,1,0:T(8,128)}), f32[128,8,125]{2,1,0:T(8,128)S(1)}, u32[]{:S(2)}, u32[]{:S(2)}) async-start(f32[128,8,125]{2,1,0:T(8,128)} %bitcast.966), calls=%async_computation.1 | async-start | bytes 1048576 | tf_op jit(solution)/shard_map/while/body/eval_jaxpr/all_to_all | solution.py:120
  676.2 15.8 %all-to-all-start.2 = ((f32[128,4,125]{2,1,0:T(4,128)}), f32[128,4,125]{2,1,0:T(4,128)S(1)}, u32[]{:S(2)}, u32[]{:S(2)}) async-start(f32[128,4,125]{2,1,0:T(4,128)} %bitcast.819), calls=%async_computation.2 | async-start | bytes 524288 | tf_op jit(solution)/shard_map/while/body/eval_jaxpr/all_to_all | solution.py:120
  707.8 18.7 %all-to-all-start.3 = ((f32[128,6,125]{2,1,0:T(8,128)}), f32[128,6,125]{2,1,0:T(8,128)S(1)}, u32[]{:S(2)}, u32[]{:S(2)}) async-start(f32[128,6,125]{2,1,0:T(8,128)} %reshape.539), calls=%async_computation.3 | async-start | bytes 1048576 | tf_op jit(solution)/shard_map/while/body/eval_jaxpr/all_to_all | solution.py:120
  744.5 15.7 %all-to-all-start.4 = ((f32[128,4,125]{2,1,0:T(4,128)}), f32[128,4,125]{2,1,0:T(4,128)S(1)}, u32[]{:S(2)}, u32[]{:S(2)}) async-start(f32[128,4,125]{2,1,0:T(4,128)} %bitcast.846), calls=%async_computation.4 | async-start | bytes 524288 | tf_op jit(solution)/shard_map/while/body/eval_jaxpr/all_to_all | solution.py:120
  776.4 18.5 %all-to-all-start.5 = ((f32[128,7,125]{2,1,0:T(8,128)}), f32[128,7,125]{2,1,0:T(8,128)S(1)}, u32[]{:S(2)}, u32[]{:S(2)}) async-start(f32[128,7,125]{2,1,0:T(8,128)} %reshape.541), calls=%async_computation.5 | async-start | bytes 1048576 | tf_op jit(solution)/shard_map/while/body/eval_jaxpr/all_to_all | solution.py:120
  811.0 15.7 %all-to-all-start.6 = ((f32[128,4,125]{2,1,0:T(4,128)}), f32[128,4,125]{2,1,0:T(4,128)S(1)}, u32[]{:S(2)}, u32[]{:S(2)}) async-start(f32[128,4,125]{2,1,0:T(4,128)} %bitcast.873), calls=%async_computation.6 | async-start | bytes 524288 | tf_op jit(solution)/shard_map/while/body/eval_jaxpr/all_to_all | solution.py:120
  842.7 18.7 %all-to-all-start.7 = ((f32[128,6,125]{2,1,0:T(8,128)}), f32[128,6,125]{2,1,0:T(8,128)S(1)}, u32[]{:S(2)}, u32[]{:S(2)}) async-start(f32[128,6,125]{2,1,0:T(8,128)} %reshape.542), calls=%async_computation.7 | async-start | bytes 1048576 | tf_op jit(solution)/shard_map/while/body/eval_jaxpr/all_to_all | solution.py:120
  (119 other events, 573.2 us)

commit v10 on v8

--- a/solution.py
+++ b/solution.py
@@ -140,9 +140,10 @@
             combined = lifted - jnp.einsum(
                 "pq,vqe->vpe", volume_block, fields, precision=lax.Precision.HIGH
             )
-            change = metric_scale * jnp.einsum(
-                "vw,wpe->vpe", flux_mixing, combined, precision=lax.Precision.HIGH
+            mixed = sum(
+                flux_mixing[:, w, None, None] * combined[None, w] for w in range(VARIABLES)
             )
+            change = metric_scale * mixed
             fields = fields + jnp.where(level_map >= lowest, step_sizes * change, 0.0)
         return (fields, cache)
 

time: 806 us -> 1130 us (1.40)
  local copies, waits for them, and re-layouts: 253 us -> 492 us
  other arithmetic: 62.5 us -> 129 us
  waiting for transfers between devices: 241 us -> 280 us
  matrix products: 104 us -> 76.4 us
    mul x0 -> x147, local copies, waits for them, and re-layouts: none -> 140 us  [coarse_step(): flux_mixing[:, w, None, None] * combined[None, w]]
    add x0 -> x24, other arithmetic: none -> 73.1 us  [coarse_step(): fields = fields + jnp.where(level_map >= lowest, step_sizes * change, 0.0)]
    all_to_all x24, waiting for transfers between devices: 241 us -> 280 us  [coarse_step(): lax.all_to_all(outgoing, ('wall', 'span'), split_axis=0, concat_axis=0, t...]
    dot_general x24 -> x0, matrix products: 33.9 us -> none  [coarse_step(): jnp.einsum('vw,wpe->vpe', flux_mixing, combined, precision=lax.Precision....]
    slice x45 -> x24, local copies, waits for them, and re-layouts: 3.49 us -> 28.7 us  [face_traces(): node_cube[:, :, :, -1]]
    reshape x0 -> x24, local copies, waits for them, and re-layouts: none -> 24.8 us  [face_traces(): fields.reshape(VARIABLES, DEGREE + 1, DEGREE + 1, DEGREE + 1, local_count)]
    squeeze x0 -> x96, local copies, waits for them, and re-layouts: none -> 23.7 us  [face_traces(): jnp.stack([face.reshape(VARIABLES, FACE_NODES, local_count) for face in f...]
    while x346 -> x1083, local copies, waits for them, and re-layouts: 26.1 us -> 38.7 us
  transfers between devices with their start and end apart: 24 -> 24, of which waited for: 24 -> 24; matrix products, arithmetic and copies ran while one was open for 7% -> 2% of each run, Pallas kernels for 0% -> 0%
where the time goes in v10:
time: 1130 us; the launch traced here: 1110 us
  local copies, waits for them, and re-layouts  492 us (44%)
  waiting for transfers between devices  280 us (25%)
  other arithmetic  129 us (11%)
  starting transfers between devices  124 us (11%)
  matrix products  76.4 us (7%)
  loops' own time  13.6 us (1%)
    all_to_all x24, waiting for transfers between devices, coarse_step(): lax.all_to_all(outgoing, ('wall', 'span'), split_axis=0, concat_axis=0, t...  280 us
    mul x147, local copies, waits for them, and re-layouts, coarse_step(): flux_mixing[:, w, None, None] * combined[None, w]  140 us
    all_to_all x24, starting transfers between devices, coarse_step(): lax.all_to_all(outgoing, ('wall', 'span'), split_axis=0, concat_axis=0, t...  124 us
    gather x24, local copies, waits for them, and re-layouts, coarse_step(): jump_rows = lookup.at[pointers].get(mode='promise_in_bounds') - table_rows  89.6 us
    add x24, other arithmetic, coarse_step(): fields = fields + jnp.where(level_map >= lowest, step_sizes * change, 0.0)  73.1 us
    gather x33, local copies, waits for them, and re-layouts, coarse_step(): outgoing = table_rows.at[send_columns].get(mode='promise_in_bounds')  58.4 us
    dot_general x24, matrix products, coarse_step(): jnp.einsum('fvpj,fej->vpe', lift_big, jump_rows.reshape(6, local_count, T...  39.6 us
    while x1083, local copies, waits for them, and re-layouts  38.7 us
  transfers between devices with their start and end apart: 24, of which 24 were waited for; matrix products, arithmetic and copies ran while one was open for 2% of the time, Pallas kernels for 0%

profile of v10, /device:TPU:1, one launch (start us, length us, event | category | flops | bytes accessed | tf_op | source)
XLA Modules:
  0.0 1114.3 jit_solution(13890864319102656230)
XLA Ops:
  3.1 1110.2 %while.11 = (s32[]{:T(128)}, f32[5,125,256]{2,1,0:T(8,128)S(1)}, s32[256]{0:T(256)}, s32[1,1024]{1,0:T(1,128)}, f32[256]{0:T(256)}, /*index=5*/f32[256]{0:T(256)...) while((s32[]{:T(128)}, f32[5,125,256]{2,1,0:T(8,128)S(1)}, ...), condition=%wide.region_4.5_spmd.clone, body=%wide.region_0.4_spmd.clone.sunk | while | flops 6805277696 | bytes 344863584 | solution.py:150
  14.3 11.5 %all-to-all-start = ((f32[128,8,126]{2,1,0:T(8,128)}), f32[128,8,126]{2,1,0:T(8,128)S(1)}, u32[]{:S(2)}, u32[]{:S(2)}) async-start(f32[128,8,126]{2,1,0:T(8,128)} %concatenate.61), calls=%async_computation | async-start | bytes 1048576 | tf_op jit(solution)/shard_map/while/body/eval_jaxpr/all_to_all | solution.py:120
  29.3 10.2 all-to-all-done
  70.1 12.7 %all-to-all-done.1 = f32[128,8,125]{2,1,0:T(8,128)S(1)} async-done(((f32[128,8,125]{2,1,0:T(8,128)}), f32[128,8,125]{2,1,0:T(8,128)S(1)}, u32[]{:S(2)}, u32[]{:S(2)}) %all-to-all-start.1) | async-done | bytes 512032 | tf_op jit(solution)/shard_map/while/body/eval_jaxpr/all_to_all | solution.py:120
  111.3 10.6 all-to-all-done.2
  156.9 12.5 %all-to-all-done.3 = f32[128,6,125]{2,1,0:T(8,128)S(1)} async-done(((f32[128,6,125]{2,1,0:T(8,128)}), f32[128,6,125]{2,1,0:T(8,128)S(1)}, u32[]{:S(2)}, u32[]{:S(2)}) %all-to-all-start.3) | async-done | bytes 384032 | tf_op jit(solution)/shard_map/while/body/eval_jaxpr/all_to_all | solution.py:120
  200.0 10.4 all-to-all-done.4
  246.3 12.5 %all-to-all-done.5 = f32[128,7,125]{2,1,0:T(8,128)S(1)} async-done(((f32[128,7,125]{2,1,0:T(8,128)}), f32[128,7,125]{2,1,0:T(8,128)S(1)}, u32[]{:S(2)}, u32[]{:S(2)}) %all-to-all-start.5) | async-done | bytes 448032 | tf_op jit(solution)/shard_map/while/body/eval_jaxpr/all_to_all | solution.py:120
  296.3 10.7 all-to-all-done.6
  342.5 13.4 %all-to-all-done.7 = f32[128,6,125]{2,1,0:T(8,128)S(1)} async-done(((f32[128,6,125]{2,1,0:T(8,128)}), f32[128,6,125]{2,1,0:T(8,128)S(1)}, u32[]{:S(2)}, u32[]{:S(2)}) %all-to-all-start.7) | async-done | bytes 384032 | tf_op jit(solution)/shard_map/while/body/eval_jaxpr/all_to_all | solution.py:120
  437.7 12.7 %all-to-all-done.1 = f32[128,8,125]{2,1,0:T(8,128)S(1)} async-done(((f32[128,8,125]{2,1,0:T(8,128)}), f32[128,8,125]{2,1,0:T(8,128)S(1)}, u32[]{:S(2)}, u32[]{:S(2)}) %all-to-all-start.1) | async-done | bytes 512032 | tf_op jit(solution)/shard_map/while/body/eval_jaxpr/all_to_all | solution.py:120
  478.7 10.6 all-to-all-done.2
  524.1 12.5 %all-to-all-done.3 = f32[128,6,125]{2,1,0:T(8,128)S(1)} async-done(((f32[128,6,125]{2,1,0:T(8,128)}), f32[128,6,125]{2,1,0:T(8,128)S(1)}, u32[]{:S(2)}, u32[]{:S(2)}) %all-to-all-start.3) | async-done | bytes 384032 | tf_op jit(solution)/shard_map/while/body/eval_jaxpr/all_to_all | solution.py:120
  567.2 10.4 all-to-all-done.4
  613.5 12.5 %all-to-all-done.5 = f32[128,7,125]{2,1,0:T(8,128)S(1)} async-done(((f32[128,7,125]{2,1,0:T(8,128)}), f32[128,7,125]{2,1,0:T(8,128)S(1)}, u32[]{:S(2)}, u32[]{:S(2)}) %all-to-all-start.5) | async-done | bytes 448032 | tf_op jit(solution)/shard_map/while/body/eval_jaxpr/all_to_all | solution.py:120
  663.5 10.7 all-to-all-done.6
  709.8 13.4 %all-to-all-done.7 = f32[128,6,125]{2,1,0:T(8,128)S(1)} async-done(((f32[128,6,125]{2,1,0:T(8,128)}), f32[128,6,125]{2,1,0:T(8,128)S(1)}, u32[]{:S(2)}, u32[]{:S(2)}) %all-to-all-start.7) | async-done | bytes 384032 | tf_op jit(solution)/shard_map/while/body/eval_jaxpr/all_to_all | solution.py:120
  804.9 12.7 %all-to-all-done.1 = f32[128,8,125]{2,1,0:T(8,128)S(1)} async-done(((f32[128,8,125]{2,1,0:T(8,128)}), f32[128,8,125]{2,1,0:T(8,128)S(1)}, u32[]{:S(2)}, u32[]{:S(2)}) %all-to-all-start.1) | async-done | bytes 512032 | tf_op jit(solution)/shard_map/while/body/eval_jaxpr/all_to_all | solution.py:120
  845.9 10.6 all-to-all-done.2
  891.3 12.5 %all-to-all-done.3 = f32[128,6,125]{2,1,0:T(8,128)S(1)} async-done(((f32[128,6,125]{2,1,0:T(8,128)}), f32[128,6,125]{2,1,0:T(8,128)S(1)}, u32[]{:S(2)}, u32[]{:S(2)}) %all-to-all-start.3) | async-done | bytes 384032 | tf_op jit(solution)/shard_map/while/body/eval_jaxpr/all_to_all | solution.py:120
  934.5 10.4 all-to-all-done.4
  980.7 12.5 %all-to-all-done.5 = f32[128,7,125]{2,1,0:T(8,128)S(1)} async-done(((f32[128,7,125]{2,1,0:T(8,128)}), f32[128,7,125]{2,1,0:T(8,128)S(1)}, u32[]{:S(2)}, u32[]{:S(2)}) %all-to-all-start.5) | async-done | bytes 448032 | tf_op jit(solution)/shard_map/while/body/eval_jaxpr/all_to_all | solution.py:120
  1030.7 10.7 all-to-all-done.6
  1077.0 13.4 %all-to-all-done.7 = f32[128,6,125]{2,1,0:T(8,128)S(1)} async-done(((f32[128,6,125]{2,1,0:T(8,128)}), f32[128,6,125]{2,1,0:T(8,128)S(1)}, u32[]{:S(2)}, u32[]{:S(2)}) %all-to-all-start.7) | async-done | bytes 384032 | tf_op jit(solution)/shard_map/while/body/eval_jaxpr/all_to_all | solution.py:120
  (1800 shorter events, 829.8 us)
Async XLA Ops:
  14.3 25.2 %all-to-all-start = ((f32[128,8,126]{2,1,0:T(8,128)}), f32[128,8,126]{2,1,0:T(8,128)S(1)}, u32[]{:S(2)}, u32[]{:S(2)}) async-start(f32[128,8,126]{2,1,0:T(8,128)} %concatenate.61), calls=%async_computation | async-start | bytes 1048576 | tf_op jit(solution)/shard_map/while/body/eval_jaxpr/all_to_all | solution.py:120
  64.3 18.6 %all-to-all-start.1 = ((f32[128,8,125]{2,1,0:T(8,128)}), f32[128,8,125]{2,1,0:T(8,128)S(1)}, u32[]{:S(2)}, u32[]{:S(2)}) async-start(f32[128,8,125]{2,1,0:T(8,128)} %bitcast.524), calls=%async_computation.1 | async-start | bytes 1048576 | tf_op jit(solution)/shard_map/while/body/eval_jaxpr/all_to_all | solution.py:120
  106.1 15.9 %all-to-all-start.2 = ((f32[128,4,125]{2,1,0:T(4,128)}), f32[128,4,125]{2,1,0:T(4,128)S(1)}, u32[]{:S(2)}, u32[]{:S(2)}) async-start(f32[128,4,125]{2,1,0:T(4,128)} %bitcast.534), calls=%async_computation.2 | async-start | bytes 524288 | tf_op jit(solution)/shard_map/while/body/eval_jaxpr/all_to_all | solution.py:120
  150.5 18.9 %all-to-all-start.3 = ((f32[128,6,125]{2,1,0:T(8,128)}), f32[128,6,125]{2,1,0:T(8,128)S(1)}, u32[]{:S(2)}, u32[]{:S(2)}) async-start(f32[128,6,125]{2,1,0:T(8,128)} %reshape.507), calls=%async_computation.3 | async-start | bytes 1048576 | tf_op jit(solution)/shard_map/while/body/eval_jaxpr/all_to_all | solution.py:120
  194.8 15.7 %all-to-all-start.4 = ((f32[128,4,125]{2,1,0:T(4,128)}), f32[128,4,125]{2,1,0:T(4,128)S(1)}, u32[]{:S(2)}, u32[]{:S(2)}) async-start(f32[128,4,125]{2,1,0:T(4,128)} %bitcast.549), calls=%async_computation.4 | async-start | bytes 524288 | tf_op jit(solution)/shard_map/while/body/eval_jaxpr/all_to_all | solution.py:120
  240.3 18.5 %all-to-all-start.5 = ((f32[128,7,125]{2,1,0:T(8,128)}), f32[128,7,125]{2,1,0:T(8,128)S(1)}, u32[]{:S(2)}, u32[]{:S(2)}) async-start(f32[128,7,125]{2,1,0:T(8,128)} %reshape.511), calls=%async_computation.5 | async-start | bytes 1048576 | tf_op jit(solution)/shard_map/while/body/eval_jaxpr/all_to_all | solution.py:120
  291.2 15.7 %all-to-all-start.6 = ((f32[128,4,125]{2,1,0:T(4,128)}), f32[128,4,125]{2,1,0:T(4,128)S(1)}, u32[]{:S(2)}, u32[]{:S(2)}) async-start(f32[128,4,125]{2,1,0:T(4,128)} %bitcast.564), calls=%async_computation.6 | async-start | bytes 524288 | tf_op jit(solution)/shard_map/while/body/eval_jaxpr/all_to_all | solution.py:120
  337.3 18.7 %all-to-all-start.7 = ((f32[128,6,125]{2,1,0:T(8,128)}), f32[128,6,125]{2,1,0:T(8,128)S(1)}, u32[]{:S(2)}, u32[]{:S(2)}) async-start(f32[128,6,125]{2,1,0:T(8,128)} %reshape.514), calls=%async_computation.7 | async-start | bytes 1048576 | tf_op jit(solution)/shard_map/while/body/eval_jaxpr/all_to_all | solution.py:120
  389.0 18.2 %all-to-all-start = ((f32[128,8,126]{2,1,0:T(8,128)}), f32[128,8,126]{2,1,0:T(8,128)S(1)}, u32[]{:S(2)}, u32[]{:S(2)}) async-start(f32[128,8,126]{2,1,0:T(8,128)} %concatenate.61), calls=%async_computation | async-start | bytes 1048576 | tf_op jit(solution)/shard_map/while/body/eval_jaxpr/all_to_all | solution.py:120
  431.9 18.5 %all-to-all-start.1 = ((f32[128,8,125]{2,1,0:T(8,128)}), f32[128,8,125]{2,1,0:T(8,128)S(1)}, u32[]{:S(2)}, u32[]{:S(2)}) async-start(f32[128,8,125]{2,1,0:T(8,128)} %bitcast.524), calls=%async_computation.1 | async-start | bytes 1048576 | tf_op jit(solution)/shard_map/while/body/eval_jaxpr/all_to_all | solution.py:120
  473.6 15.7 %all-to-all-start.2 = ((f32[128,4,125]{2,1,0:T(4,128)}), f32[128,4,125]{2,1,0:T(4,128)S(1)}, u32[]{:S(2)}, u32[]{:S(2)}) async-start(f32[128,4,125]{2,1,0:T(4,128)} %bitcast.534), calls=%async_computation.2 | async-start | bytes 524288 | tf_op jit(solution)/shard_map/while/body/eval_jaxpr/all_to_all | solution.py:120
  517.9 18.7 %all-to-all-start.3 = ((f32[128,6,125]{2,1,0:T(8,128)}), f32[128,6,125]{2,1,0:T(8,128)S(1)}, u32[]{:S(2)}, u32[]{:S(2)}) async-start(f32[128,6,125]{2,1,0:T(8,128)} %reshape.507), calls=%async_computation.3 | async-start | bytes 1048576 | tf_op jit(solution)/shard_map/while/body/eval_jaxpr/all_to_all | solution.py:120
  562.0 15.7 %all-to-all-start.4 = ((f32[128,4,125]{2,1,0:T(4,128)}), f32[128,4,125]{2,1,0:T(4,128)S(1)}, u32[]{:S(2)}, u32[]{:S(2)}) async-start(f32[128,4,125]{2,1,0:T(4,128)} %bitcast.549), calls=%async_computation.4 | async-start | bytes 524288 | tf_op jit(solution)/shard_map/while/body/eval_jaxpr/all_to_all | solution.py:120
  607.5 18.5 %all-to-all-start.5 = ((f32[128,7,125]{2,1,0:T(8,128)}), f32[128,7,125]{2,1,0:T(8,128)S(1)}, u32[]{:S(2)}, u32[]{:S(2)}) async-start(f32[128,7,125]{2,1,0:T(8,128)} %reshape.511), calls=%async_computation.5 | async-start | bytes 1048576 | tf_op jit(solution)/shard_map/while/body/eval_jaxpr/all_to_all | solution.py:120
  658.5 15.7 %all-to-all-start.6 = ((f32[128,4,125]{2,1,0:T(4,128)}), f32[128,4,125]{2,1,0:T(4,128)S(1)}, u32[]{:S(2)}, u32[]{:S(2)}) async-start(f32[128,4,125]{2,1,0:T(4,128)} %bitcast.564), calls=%async_computation.6 | async-start | bytes 524288 | tf_op jit(solution)/shard_map/while/body/eval_jaxpr/all_to_all | solution.py:120
  704.5 18.7 %all-to-all-start.7 = ((f32[128,6,125]{2,1,0:T(8,128)}), f32[128,6,125]{2,1,0:T(8,128)S(1)}, u32[]{:S(2)}, u32[]{:S(2)}) async-start(f32[128,6,125]{2,1,0:T(8,128)} %reshape.514), calls=%async_computation.7 | async-start | bytes 1048576 | tf_op jit(solution)/shard_map/while/body/eval_jaxpr/all_to_all | solution.py:120
  756.2 18.2 %all-to-all-start = ((f32[128,8,126]{2,1,0:T(8,128)}), f32[128,8,126]{2,1,0:T(8,128)S(1)}, u32[]{:S(2)}, u32[]{:S(2)}) async-start(f32[128,8,126]{2,1,0:T(8,128)} %concatenate.61), calls=%async_computation | async-start | bytes 1048576 | tf_op jit(solution)/shard_map/while/body/eval_jaxpr/all_to_all | solution.py:120
  799.1 18.5 %all-to-all-start.1 = ((f32[128,8,125]{2,1,0:T(8,128)}), f32[128,8,125]{2,1,0:T(8,128)S(1)}, u32[]{:S(2)}, u32[]{:S(2)}) async-start(f32[128,8,125]{2,1,0:T(8,128)} %bitcast.524), calls=%async_computation.1 | async-start | bytes 1048576 | tf_op jit(solution)/shard_map/while/body/eval_jaxpr/all_to_all | solution.py:120
  840.8 15.7 %all-to-all-start.2 = ((f32[128,4,125]{2,1,0:T(4,128)}), f32[128,4,125]{2,1,0:T(4,128)S(1)}, u32[]{:S(2)}, u32[]{:S(2)}) async-start(f32[128,4,125]{2,1,0:T(4,128)} %bitcast.534), calls=%async_computation.2 | async-start | bytes 524288 | tf_op jit(solution)/shard_map/while/body/eval_jaxpr/all_to_all | solution.py:120
  885.1 18.7 %all-to-all-start.3 = ((f32[128,6,125]{2,1,0:T(8,128)}), f32[128,6,125]{2,1,0:T(8,128)S(1)}, u32[]{:S(2)}, u32[]{:S(2)}) async-start(f32[128,6,125]{2,1,0:T(8,128)} %reshape.507), calls=%async_computation.3 | async-start | bytes 1048576 | tf_op jit(solution)/shard_map/while/body/eval_jaxpr/all_to_all | solution.py:120
  929.2 15.7 %all-to-all-start.4 = ((f32[128,4,125]{2,1,0:T(4,128)}), f32[128,4,125]{2,1,0:T(4,128)S(1)}, u32[]{:S(2)}, u32[]{:S(2)}) async-start(f32[128,4,125]{2,1,0:T(4,128)} %bitcast.549), calls=%async_computation.4 | async-start | bytes 524288 | tf_op jit(solution)/shard_map/while/body/eval_jaxpr/all_to_all | solution.py:120
  974.8 18.5 %all-to-all-start.5 = ((f32[128,7,125]{2,1,0:T(8,128)}), f32[128,7,125]{2,1,0:T(8,128)S(1)}, u32[]{:S(2)}, u32[]{:S(2)}) async-start(f32[128,7,125]{2,1,0:T(8,128)} %reshape.511), calls=%async_computation.5 | async-start | bytes 1048576 | tf_op jit(solution)/shard_map/while/body/eval_jaxpr/all_to_all | solution.py:120
  1025.7 15.7 %all-to-all-start.6 = ((f32[128,4,125]{2,1,0:T(4,128)}), f32[128,4,125]{2,1,0:T(4,128)S(1)}, u32[]{:S(2)}, u32[]{:S(2)}) async-start(f32[128,4,125]{2,1,0:T(4,128)} %bitcast.564), calls=%async_computation.6 | async-start | bytes 524288 | tf_op jit(solution)/shard_map/while/body/eval_jaxpr/all_to_all | solution.py:120
  1071.7 18.7 %all-to-all-start.7 = ((f32[128,6,125]{2,1,0:T(8,128)}), f32[128,6,125]{2,1,0:T(8,128)S(1)}, u32[]{:S(2)}, u32[]{:S(2)}) async-start(f32[128,6,125]{2,1,0:T(8,128)} %reshape.514), calls=%async_computation.7 | async-start | bytes 1048576 | tf_op jit(solution)/shard_map/while/body/eval_jaxpr/all_to_all | solution.py:120
  (521 other events, 3551.1 us)

commit v11 on v8

--- a/solution.py
+++ b/solution.py
@@ -113,16 +113,19 @@
             trace_table = make_table(fields)
             table_rows = trace_table.T
             send_columns = send_row.reshape(peers, slot_count)[:, :fresh]
-            outgoing = table_rows.at[send_columns].get(mode="promise_in_bounds")
+            source_rows = table_rows
             if substep == 0:
-                rate_column = jnp.full((peers, fresh, 1), local_fastest, jnp.float32)
-                outgoing = jnp.concatenate([outgoing, rate_column], axis=2)
+                rate_row = jnp.full((1, TRACE_ROWS), local_fastest, jnp.float32)
+                source_rows = jnp.concatenate([table_rows, rate_row], axis=0)
+                rate_index = jnp.full((peers, 1), table_rows.shape[0], send_columns.dtype)
+                send_columns = jnp.concatenate([send_columns, rate_index], axis=1)
+            outgoing = source_rows.at[send_columns].get(mode="promise_in_bounds")
             arrived = lax.all_to_all(
                 outgoing, ("wall", "span"), split_axis=0, concat_axis=0, tiled=True
             )
             if substep == 0:
-                fastest = jnp.max(arrived[:, :, TRACE_ROWS])
-                arrived = arrived[:, :, :TRACE_ROWS]
+                fastest = jnp.max(arrived[:, slot_count, 0])
+                arrived = arrived[:, :slot_count]
                 step_sizes = COURANT / fastest / divisors
             if fresh < slot_count:
                 arrived = jnp.concatenate([arrived, received[:, fresh:]], axis=1)

time: 806 us -> 877 us (1.088)
  local copies, waits for them, and re-layouts: 253 us -> 291 us
  waiting for transfers between devices: 241 us -> 269 us
    all_to_all x24, waiting for transfers between devices: 241 us -> 269 us  [coarse_step(): lax.all_to_all(outgoing, ('wall', 'span'), split_axis=0, concat_axis=0, t...]
    another operation x24, local copies, waits for them, and re-layouts: 35.8 us -> 50.2 us  [face_traces(): jnp.stack([face.reshape(VARIABLES, FACE_NODES, local_count) for face in f...]
    while x345 -> x465, local copies, waits for them, and re-layouts: 25.1 us -> 31 us
    gather x33 -> x36, local copies, waits for them, and re-layouts: 58.3 us -> 60.2 us  [coarse_step(): outgoing = source_rows.at[send_columns].get(mode='promise_in_bounds')]
  transfers between devices with their start and end apart: 24 -> 24, of which waited for: 24 -> 24; matrix products, arithmetic and copies ran while one was open for 7% -> 6% of each run, Pallas kernels for 0% -> 0%
where the time goes in v11:
time: 877 us; the launch traced here: 869 us
  local copies, waits for them, and re-layouts  291 us (33%)
  waiting for transfers between devices  269 us (31%)
  starting transfers between devices  127 us (14%)
  matrix products  103 us (12%)
  other arithmetic  68.3 us (8%)
  loops' own time  10.2 us (1%)
    all_to_all x24, waiting for transfers between devices, coarse_step(): lax.all_to_all(outgoing, ('wall', 'span'), split_axis=0, concat_axis=0, t...  269 us
    all_to_all x24, starting transfers between devices, coarse_step(): lax.all_to_all(outgoing, ('wall', 'span'), split_axis=0, concat_axis=0, t...  127 us
    gather x24, local copies, waits for them, and re-layouts, coarse_step(): jump_rows = lookup.at[pointers].get(mode='promise_in_bounds') - table_rows  88.2 us
    gather x36, local copies, waits for them, and re-layouts, coarse_step(): outgoing = source_rows.at[send_columns].get(mode='promise_in_bounds')  60.2 us
    another operation x24, local copies, waits for them, and re-layouts, face_traces(): jnp.stack([face.reshape(VARIABLES, FACE_NODES, local_count) for face in f...  50.2 us
    dot_general x24, matrix products, coarse_step(): jnp.einsum('vw,wpe->vpe', flux_mixing, combined, precision=lax.Precision....  39.4 us
    dot_general x24, matrix products, coarse_step(): jnp.einsum('pq,vqe->vpe', volume_block, fields, precision=lax.Precision.H...  35.7 us
    sub x24, other arithmetic, coarse_step(): jump_rows = lookup.at[pointers].get(mode='promise_in_bounds') - table_rows  32.5 us
  transfers between devices with their start and end apart: 24, of which 24 were waited for; matrix products, arithmetic and copies ran while one was open for 6% of the time, Pallas kernels for 0%

profile of v11, /device:TPU:1, one launch (start us, length us, event | category | flops | bytes accessed | tf_op | source)
XLA Modules:
  0.0 868.8 jit_solution(9920612537661814919)
XLA Ops:
  4.3 861.9 %while.11 = (s32[]{:T(128)}, f32[5,125,256]{2,0,1:T(8,128)}, s32[256]{0:T(256)S(1)}, f32[256]{0:T(256)S(1)}, s32[1,1024]{1,0:T(1,128)S(1)}, /*index=5*/f32[256]{...) while((s32[]{:T(128)}, f32[5,125,256]{2,0,1:T(8,128)}, ...), condition=%wide.region_4.5_spmd.clone, body=%wide.region_0.4_spmd.clone.sunk | while | flops 6773922816 | bytes 249638256 | solution.py:152
  16.9 11.5 %all-to-all-start = ((f32[128,9,125]{2,1,0:T(8,128)}), f32[128,9,125]{2,1,0:T(8,128)S(1)}, u32[]{:S(2)}, u32[]{:S(2)}) async-start(f32[128,9,125]{2,1,0:T(8,128)} %reshape.493), calls=%async_computation | async-start | bytes 2097152 | tf_op jit(solution)/shard_map/while/body/eval_jaxpr/all_to_all | solution.py:123
  31.7 16.0 %all-to-all-done = f32[128,9,125]{2,1,0:T(8,128)S(1)} async-done(((f32[128,9,125]{2,1,0:T(8,128)}), f32[128,9,125]{2,1,0:T(8,128)S(1)}, u32[]{:S(2)}, u32[]{:S(2)}) %all-to-all-start) | async-done | bytes 576032 | tf_op jit(solution)/shard_map/while/body/eval_jaxpr/all_to_all | solution.py:123
  75.5 12.0 %all-to-all-done.1 = f32[128,8,125]{2,1,0:T(8,128)S(1)} async-done(((f32[128,8,125]{2,1,0:T(8,128)}), f32[128,8,125]{2,1,0:T(8,128)S(1)}, u32[]{:S(2)}, u32[]{:S(2)}) %all-to-all-start.1) | async-done | bytes 512032 | tf_op jit(solution)/shard_map/while/body/eval_jaxpr/all_to_all | solution.py:123
  143.1 11.0 %all-to-all-done.3 = f32[128,6,125]{2,1,0:T(8,128)S(1)} async-done(((f32[128,6,125]{2,1,0:T(8,128)}), f32[128,6,125]{2,1,0:T(8,128)S(1)}, u32[]{:S(2)}, u32[]{:S(2)}) %all-to-all-start.3) | async-done | bytes 384032 | tf_op jit(solution)/shard_map/while/body/eval_jaxpr/all_to_all | solution.py:123
  177.4 9.9 %all-to-all-done.4 = f32[128,4,125]{2,1,0:T(4,128)} async-done(((f32[128,4,125]{2,1,0:T(4,128)}), f32[128,4,125]{2,1,0:T(4,128)}, u32[]{:S(2)}, u32[]{:S(2)}) %all-to-all-start.4) | async-done | bytes 256032 | tf_op jit(solution)/shard_map/while/body/eval_jaxpr/all_to_all | solution.py:123
  211.3 11.1 %all-to-all-done.5 = f32[128,7,125]{2,1,0:T(8,128)S(1)} async-done(((f32[128,7,125]{2,1,0:T(8,128)}), f32[128,7,125]{2,1,0:T(8,128)S(1)}, u32[]{:S(2)}, u32[]{:S(2)}) %all-to-all-start.5) | async-done | bytes 448032 | tf_op jit(solution)/shard_map/while/body/eval_jaxpr/all_to_all | solution.py:123
  241.7 9.4 %all-to-all-done.6 = f32[128,4,125]{2,1,0:T(4,128)S(1)} async-done(((f32[128,4,125]{2,1,0:T(4,128)}), f32[128,4,125]{2,1,0:T(4,128)S(1)}, u32[]{:S(2)}, u32[]{:S(2)}) %all-to-all-start.6) | async-done | bytes 256032 | tf_op jit(solution)/shard_map/while/body/eval_jaxpr/all_to_all | solution.py:123
  274.3 11.9 %all-to-all-done.7 = f32[128,6,125]{2,1,0:T(8,128)} async-done(((f32[128,6,125]{2,1,0:T(8,128)}), f32[128,6,125]{2,1,0:T(8,128)}, u32[]{:S(2)}, u32[]{:S(2)}) %all-to-all-start.7) | async-done | bytes 384032 | tf_op jit(solution)/shard_map/while/body/eval_jaxpr/all_to_all | solution.py:123
  316.6 16.0 %all-to-all-done = f32[128,9,125]{2,1,0:T(8,128)S(1)} async-done(((f32[128,9,125]{2,1,0:T(8,128)}), f32[128,9,125]{2,1,0:T(8,128)S(1)}, u32[]{:S(2)}, u32[]{:S(2)}) %all-to-all-start) | async-done | bytes 576032 | tf_op jit(solution)/shard_map/while/body/eval_jaxpr/all_to_all | solution.py:123
  360.2 12.0 %all-to-all-done.1 = f32[128,8,125]{2,1,0:T(8,128)S(1)} async-done(((f32[128,8,125]{2,1,0:T(8,128)}), f32[128,8,125]{2,1,0:T(8,128)S(1)}, u32[]{:S(2)}, u32[]{:S(2)}) %all-to-all-start.1) | async-done | bytes 512032 | tf_op jit(solution)/shard_map/while/body/eval_jaxpr/all_to_all | solution.py:123
  393.3 8.5 all-to-all-done.2
  427.3 11.0 %all-to-all-done.3 = f32[128,6,125]{2,1,0:T(8,128)S(1)} async-done(((f32[128,6,125]{2,1,0:T(8,128)}), f32[128,6,125]{2,1,0:T(8,128)S(1)}, u32[]{:S(2)}, u32[]{:S(2)}) %all-to-all-start.3) | async-done | bytes 384032 | tf_op jit(solution)/shard_map/while/body/eval_jaxpr/all_to_all | solution.py:123
  461.8 9.9 %all-to-all-done.4 = f32[128,4,125]{2,1,0:T(4,128)} async-done(((f32[128,4,125]{2,1,0:T(4,128)}), f32[128,4,125]{2,1,0:T(4,128)}, u32[]{:S(2)}, u32[]{:S(2)}) %all-to-all-start.4) | async-done | bytes 256032 | tf_op jit(solution)/shard_map/while/body/eval_jaxpr/all_to_all | solution.py:123
  496.0 11.1 %all-to-all-done.5 = f32[128,7,125]{2,1,0:T(8,128)S(1)} async-done(((f32[128,7,125]{2,1,0:T(8,128)}), f32[128,7,125]{2,1,0:T(8,128)S(1)}, u32[]{:S(2)}, u32[]{:S(2)}) %all-to-all-start.5) | async-done | bytes 448032 | tf_op jit(solution)/shard_map/while/body/eval_jaxpr/all_to_all | solution.py:123
  526.3 9.4 %all-to-all-done.6 = f32[128,4,125]{2,1,0:T(4,128)S(1)} async-done(((f32[128,4,125]{2,1,0:T(4,128)}), f32[128,4,125]{2,1,0:T(4,128)S(1)}, u32[]{:S(2)}, u32[]{:S(2)}) %all-to-all-start.6) | async-done | bytes 256032 | tf_op jit(solution)/shard_map/while/body/eval_jaxpr/all_to_all | solution.py:123
  558.9 11.9 %all-to-all-done.7 = f32[128,6,125]{2,1,0:T(8,128)} async-done(((f32[128,6,125]{2,1,0:T(8,128)}), f32[128,6,125]{2,1,0:T(8,128)}, u32[]{:S(2)}, u32[]{:S(2)}) %all-to-all-start.7) | async-done | bytes 384032 | tf_op jit(solution)/shard_map/while/body/eval_jaxpr/all_to_all | solution.py:123
  601.0 16.0 %all-to-all-done = f32[128,9,125]{2,1,0:T(8,128)S(1)} async-done(((f32[128,9,125]{2,1,0:T(8,128)}), f32[128,9,125]{2,1,0:T(8,128)S(1)}, u32[]{:S(2)}, u32[]{:S(2)}) %all-to-all-start) | async-done | bytes 576032 | tf_op jit(solution)/shard_map/while/body/eval_jaxpr/all_to_all | solution.py:123
  644.6 12.0 %all-to-all-done.1 = f32[128,8,125]{2,1,0:T(8,128)S(1)} async-done(((f32[128,8,125]{2,1,0:T(8,128)}), f32[128,8,125]{2,1,0:T(8,128)S(1)}, u32[]{:S(2)}, u32[]{:S(2)}) %all-to-all-start.1) | async-done | bytes 512032 | tf_op jit(solution)/shard_map/while/body/eval_jaxpr/all_to_all | solution.py:123
  711.9 11.0 %all-to-all-done.3 = f32[128,6,125]{2,1,0:T(8,128)S(1)} async-done(((f32[128,6,125]{2,1,0:T(8,128)}), f32[128,6,125]{2,1,0:T(8,128)S(1)}, u32[]{:S(2)}, u32[]{:S(2)}) %all-to-all-start.3) | async-done | bytes 384032 | tf_op jit(solution)/shard_map/while/body/eval_jaxpr/all_to_all | solution.py:123
  746.2 9.9 %all-to-all-done.4 = f32[128,4,125]{2,1,0:T(4,128)} async-done(((f32[128,4,125]{2,1,0:T(4,128)}), f32[128,4,125]{2,1,0:T(4,128)}, u32[]{:S(2)}, u32[]{:S(2)}) %all-to-all-start.4) | async-done | bytes 256032 | tf_op jit(solution)/shard_map/while/body/eval_jaxpr/all_to_all | solution.py:123
  780.2 11.1 %all-to-all-done.5 = f32[128,7,125]{2,1,0:T(8,128)S(1)} async-done(((f32[128,7,125]{2,1,0:T(8,128)}), f32[128,7,125]{2,1,0:T(8,128)S(1)}, u32[]{:S(2)}, u32[]{:S(2)}) %all-to-all-start.5) | async-done | bytes 448032 | tf_op jit(solution)/shard_map/while/body/eval_jaxpr/all_to_all | solution.py:123
  810.8 9.4 %all-to-all-done.6 = f32[128,4,125]{2,1,0:T(4,128)S(1)} async-done(((f32[128,4,125]{2,1,0:T(4,128)}), f32[128,4,125]{2,1,0:T(4,128)S(1)}, u32[]{:S(2)}, u32[]{:S(2)}) %all-to-all-start.6) | async-done | bytes 256032 | tf_op jit(solution)/shard_map/while/body/eval_jaxpr/all_to_all | solution.py:123
  843.4 11.9 %all-to-all-done.7 = f32[128,6,125]{2,1,0:T(8,128)} async-done(((f32[128,6,125]{2,1,0:T(8,128)}), f32[128,6,125]{2,1,0:T(8,128)}, u32[]{:S(2)}, u32[]{:S(2)}) %all-to-all-start.7) | async-done | bytes 384032 | tf_op jit(solution)/shard_map/while/body/eval_jaxpr/all_to_all | solution.py:123
  (1053 shorter events, 594.6 us)
Async XLA Ops:
  16.9 30.8 %all-to-all-start = ((f32[128,9,125]{2,1,0:T(8,128)}), f32[128,9,125]{2,1,0:T(8,128)S(1)}, u32[]{:S(2)}, u32[]{:S(2)}) async-start(f32[128,9,125]{2,1,0:T(8,128)} %reshape.493), calls=%async_computation | async-start | bytes 2097152 | tf_op jit(solution)/shard_map/while/body/eval_jaxpr/all_to_all | solution.py:123
  68.9 18.5 %all-to-all-start.1 = ((f32[128,8,125]{2,1,0:T(8,128)}), f32[128,8,125]{2,1,0:T(8,128)S(1)}, u32[]{:S(2)}, u32[]{:S(2)}) async-start(f32[128,8,125]{2,1,0:T(8,128)} %bitcast.769), calls=%async_computation.1 | async-start | bytes 1048576 | tf_op jit(solution)/shard_map/while/body/eval_jaxpr/all_to_all | solution.py:123
  101.3 15.9 %all-to-all-start.2 = ((f32[128,4,125]{2,1,0:T(4,128)}), f32[128,4,125]{2,1,0:T(4,128)S(1)}, u32[]{:S(2)}, u32[]{:S(2)}) async-start(f32[128,4,125]{2,1,0:T(4,128)} %bitcast.635), calls=%async_computation.2 | async-start | bytes 524288 | tf_op jit(solution)/shard_map/while/body/eval_jaxpr/all_to_all | solution.py:123
  135.2 18.9 %all-to-all-start.3 = ((f32[128,6,125]{2,1,0:T(8,128)}), f32[128,6,125]{2,1,0:T(8,128)S(1)}, u32[]{:S(2)}, u32[]{:S(2)}) async-start(f32[128,6,125]{2,1,0:T(8,128)} %reshape.497), calls=%async_computation.3 | async-start | bytes 1048576 | tf_op jit(solution)/shard_map/while/body/eval_jaxpr/all_to_all | solution.py:123
  170.8 16.5 %all-to-all-start.4 = ((f32[128,4,125]{2,1,0:T(4,128)}), f32[128,4,125]{2,1,0:T(4,128)}, u32[]{:S(2)}, u32[]{:S(2)}) async-start(f32[128,4,125]{2,1,0:T(4,128)} %bitcast.660), calls=%async_computation.4 | async-start | bytes 524288 | tf_op jit(solution)/shard_map/while/body/eval_jaxpr/all_to_all | solution.py:123
  204.0 18.5 %all-to-all-start.5 = ((f32[128,7,125]{2,1,0:T(8,128)}), f32[128,7,125]{2,1,0:T(8,128)S(1)}, u32[]{:S(2)}, u32[]{:S(2)}) async-start(f32[128,7,125]{2,1,0:T(8,128)} %reshape.499), calls=%async_computation.5 | async-start | bytes 1048576 | tf_op jit(solution)/shard_map/while/body/eval_jaxpr/all_to_all | solution.py:123
  235.4 15.7 %all-to-all-start.6 = ((f32[128,4,125]{2,1,0:T(4,128)}), f32[128,4,125]{2,1,0:T(4,128)S(1)}, u32[]{:S(2)}, u32[]{:S(2)}) async-start(f32[128,4,125]{2,1,0:T(4,128)} %bitcast.685), calls=%async_computation.6 | async-start | bytes 524288 | tf_op jit(solution)/shard_map/while/body/eval_jaxpr/all_to_all | solution.py:123
  267.5 18.8 %all-to-all-start.7 = ((f32[128,6,125]{2,1,0:T(8,128)}), f32[128,6,125]{2,1,0:T(8,128)}, u32[]{:S(2)}, u32[]{:S(2)}) async-start(f32[128,6,125]{2,1,0:T(8,128)} %reshape.500), calls=%async_computation.7 | async-start | bytes 1048576 | tf_op jit(solution)/shard_map/while/body/eval_jaxpr/all_to_all | solution.py:123
  308.8 23.9 %all-to-all-start = ((f32[128,9,125]{2,1,0:T(8,128)}), f32[128,9,125]{2,1,0:T(8,128)S(1)}, u32[]{:S(2)}, u32[]{:S(2)}) async-start(f32[128,9,125]{2,1,0:T(8,128)} %reshape.493), calls=%async_computation | async-start | bytes 2097152 | tf_op jit(solution)/shard_map/while/body/eval_jaxpr/all_to_all | solution.py:123
  353.9 18.3 %all-to-all-start.1 = ((f32[128,8,125]{2,1,0:T(8,128)}), f32[128,8,125]{2,1,0:T(8,128)S(1)}, u32[]{:S(2)}, u32[]{:S(2)}) async-start(f32[128,8,125]{2,1,0:T(8,128)} %bitcast.769), calls=%async_computation.1 | async-start | bytes 1048576 | tf_op jit(solution)/shard_map/while/body/eval_jaxpr/all_to_all | solution.py:123
  386.1 15.7 %all-to-all-start.2 = ((f32[128,4,125]{2,1,0:T(4,128)}), f32[128,4,125]{2,1,0:T(4,128)S(1)}, u32[]{:S(2)}, u32[]{:S(2)}) async-start(f32[128,4,125]{2,1,0:T(4,128)} %bitcast.635), calls=%async_computation.2 | async-start | bytes 524288 | tf_op jit(solution)/shard_map/while/body/eval_jaxpr/all_to_all | solution.py:123
  419.8 18.5 %all-to-all-start.3 = ((f32[128,6,125]{2,1,0:T(8,128)}), f32[128,6,125]{2,1,0:T(8,128)S(1)}, u32[]{:S(2)}, u32[]{:S(2)}) async-start(f32[128,6,125]{2,1,0:T(8,128)} %reshape.497), calls=%async_computation.3 | async-start | bytes 1048576 | tf_op jit(solution)/shard_map/while/body/eval_jaxpr/all_to_all | solution.py:123
  455.0 16.6 %all-to-all-start.4 = ((f32[128,4,125]{2,1,0:T(4,128)}), f32[128,4,125]{2,1,0:T(4,128)}, u32[]{:S(2)}, u32[]{:S(2)}) async-start(f32[128,4,125]{2,1,0:T(4,128)} %bitcast.660), calls=%async_computation.4 | async-start | bytes 524288 | tf_op jit(solution)/shard_map/while/body/eval_jaxpr/all_to_all | solution.py:123
  488.3 18.8 %all-to-all-start.5 = ((f32[128,7,125]{2,1,0:T(8,128)}), f32[128,7,125]{2,1,0:T(8,128)S(1)}, u32[]{:S(2)}, u32[]{:S(2)}) async-start(f32[128,7,125]{2,1,0:T(8,128)} %reshape.499), calls=%async_computation.5 | async-start | bytes 1048576 | tf_op jit(solution)/shard_map/while/body/eval_jaxpr/all_to_all | solution.py:123
  520.0 15.7 %all-to-all-start.6 = ((f32[128,4,125]{2,1,0:T(4,128)}), f32[128,4,125]{2,1,0:T(4,128)S(1)}, u32[]{:S(2)}, u32[]{:S(2)}) async-start(f32[128,4,125]{2,1,0:T(4,128)} %bitcast.685), calls=%async_computation.6 | async-start | bytes 524288 | tf_op jit(solution)/shard_map/while/body/eval_jaxpr/all_to_all | solution.py:123
  552.1 18.8 %all-to-all-start.7 = ((f32[128,6,125]{2,1,0:T(8,128)}), f32[128,6,125]{2,1,0:T(8,128)}, u32[]{:S(2)}, u32[]{:S(2)}) async-start(f32[128,6,125]{2,1,0:T(8,128)} %reshape.500), calls=%async_computation.7 | async-start | bytes 1048576 | tf_op jit(solution)/shard_map/while/body/eval_jaxpr/all_to_all | solution.py:123
  593.1 23.9 %all-to-all-start = ((f32[128,9,125]{2,1,0:T(8,128)}), f32[128,9,125]{2,1,0:T(8,128)S(1)}, u32[]{:S(2)}, u32[]{:S(2)}) async-start(f32[128,9,125]{2,1,0:T(8,128)} %reshape.493), calls=%async_computation | async-start | bytes 2097152 | tf_op jit(solution)/shard_map/while/body/eval_jaxpr/all_to_all | solution.py:123
  638.2 18.4 %all-to-all-start.1 = ((f32[128,8,125]{2,1,0:T(8,128)}), f32[128,8,125]{2,1,0:T(8,128)S(1)}, u32[]{:S(2)}, u32[]{:S(2)}) async-start(f32[128,8,125]{2,1,0:T(8,128)} %bitcast.769), calls=%async_computation.1 | async-start | bytes 1048576 | tf_op jit(solution)/shard_map/while/body/eval_jaxpr/all_to_all | solution.py:123
  670.5 15.9 %all-to-all-start.2 = ((f32[128,4,125]{2,1,0:T(4,128)}), f32[128,4,125]{2,1,0:T(4,128)S(1)}, u32[]{:S(2)}, u32[]{:S(2)}) async-start(f32[128,4,125]{2,1,0:T(4,128)} %bitcast.635), calls=%async_computation.2 | async-start | bytes 524288 | tf_op jit(solution)/shard_map/while/body/eval_jaxpr/all_to_all | solution.py:123
  704.4 18.4 %all-to-all-start.3 = ((f32[128,6,125]{2,1,0:T(8,128)}), f32[128,6,125]{2,1,0:T(8,128)S(1)}, u32[]{:S(2)}, u32[]{:S(2)}) async-start(f32[128,6,125]{2,1,0:T(8,128)} %reshape.497), calls=%async_computation.3 | async-start | bytes 1048576 | tf_op jit(solution)/shard_map/while/body/eval_jaxpr/all_to_all | solution.py:123
  739.6 16.5 %all-to-all-start.4 = ((f32[128,4,125]{2,1,0:T(4,128)}), f32[128,4,125]{2,1,0:T(4,128)}, u32[]{:S(2)}, u32[]{:S(2)}) async-start(f32[128,4,125]{2,1,0:T(4,128)} %bitcast.660), calls=%async_computation.4 | async-start | bytes 524288 | tf_op jit(solution)/shard_map/while/body/eval_jaxpr/all_to_all | solution.py:123
  772.8 18.5 %all-to-all-start.5 = ((f32[128,7,125]{2,1,0:T(8,128)}), f32[128,7,125]{2,1,0:T(8,128)S(1)}, u32[]{:S(2)}, u32[]{:S(2)}) async-start(f32[128,7,125]{2,1,0:T(8,128)} %reshape.499), calls=%async_computation.5 | async-start | bytes 1048576 | tf_op jit(solution)/shard_map/while/body/eval_jaxpr/all_to_all | solution.py:123
  804.3 16.0 %all-to-all-start.6 = ((f32[128,4,125]{2,1,0:T(4,128)}), f32[128,4,125]{2,1,0:T(4,128)S(1)}, u32[]{:S(2)}, u32[]{:S(2)}) async-start(f32[128,4,125]{2,1,0:T(4,128)} %bitcast.685), calls=%async_computation.6 | async-start | bytes 524288 | tf_op jit(solution)/shard_map/while/body/eval_jaxpr/all_to_all | solution.py:123
  836.6 18.8 %all-to-all-start.7 = ((f32[128,6,125]{2,1,0:T(8,128)}), f32[128,6,125]{2,1,0:T(8,128)}, u32[]{:S(2)}, u32[]{:S(2)}) async-start(f32[128,6,125]{2,1,0:T(8,128)} %reshape.500), calls=%async_computation.7 | async-start | bytes 1048576 | tf_op jit(solution)/shard_map/while/body/eval_jaxpr/all_to_all | solution.py:123
  (204 other events, 1119.6 us)
